TPU v7x, 512 devices: a whole 4x8x8 slice. The times are simulated.
512 devices in a mesh: ctx: 64 (over z_lo, y, core), ch: 8 (over z_hi, x).
Axes of the slice: x: 4, y: 8, z: 8 (z_hi: 2, z_lo: 4; z = z_hi * 4 + z_lo), core: 2. Of those that a mesh axis runs over, the one named last changes fastest.
Arguments:
- query_in: bfloat16 [16384, 4096], P('ctx', 'ch'), may hold values from -6 to 6
- key_in: bfloat16 [16384, 4096], P('ctx', 'ch'), may hold values from -6 to 6
- value_in: bfloat16 [16384, 4096], P('ctx', 'ch'), may hold values from -6 to 6
- short_weight: float32 [3, 3, 4096], P(None, None, 'ch'), may hold values from -3 to 3
- long_filter: bfloat16 [32, 768], P('ch'), may hold values from -1.1 to 1.1
- skip_weight: float32 [4096], P('ch'), may hold values from -1 to 1
- out_weight: bfloat16 [4096, 4096], P('ctx', 'ch'), may hold values from -0.09375 to 0.09375
- doc_ids: int32 [16384], P('ctx'), may hold values from 0 to 41, as said below
- out_grad: bfloat16 [16384, 4096], P('ctx', 'ch'), may hold values from -6 to 6
Outputs:
- layer_out: bfloat16 [16384, 4096], P('ctx', 'ch')
- grad_query: bfloat16 [16384, 4096], P('ctx', 'ch')
- grad_key: bfloat16 [16384, 4096], P('ctx', 'ch')
- grad_value: bfloat16 [16384, 4096], P('ctx', 'ch')
Inputs may be any that keep to these rules, and one draw needn't show every extreme that they name: doc_ids never falls along the tokens; every number from 0 to 41 occurs; every document has at most 768 tokens and one has exactly 768.
All inputs are finite; a program needn't handle non-finite values.
Results may differ from a plain program's by a relative error of at most 0.0058.
Values may be sent and summed in bfloat16 or wider, within the bound.
No kernel may reach another device: no remote copies, remote signals or barrier semaphores. Data moves between devices by JAX's collectives and lax.ppermute only.
A program may use at most 64 MiB of HBM per device.

v0:
```python
import jax
import jax.numpy as jnp
from jax import lax
from jax.sharding import PartitionSpec as P

HOPS = 3


def shifted(array, axis, by):
    size = lax.axis_size(axis)
    pairs = [(i, i + by) for i in range(size) if 0 <= i + by < size]
    return lax.ppermute(array, axis, pairs)


def toeplitz_tiles(long_filter, row_count, hop_count):
    group_count, span_len = long_filter.shape
    padded = jnp.concatenate(
        [
            jnp.zeros((group_count, row_count), long_filter.dtype),
            long_filter,
            jnp.zeros((group_count, (hop_count + 3) * row_count - span_len), long_filter.dtype),
        ],
        axis=1,
    )
    tiles_list = []
    for distance in range(hop_count + 1):
        window = padded[:, distance * row_count + 1 : distance * row_count + 1 + 2 * row_count]
        cyclic = jnp.concatenate(
            [
                window[:, row_count - 1 : 2 * row_count - 1],
                jnp.zeros((group_count, 1), window.dtype),
                window[:, : row_count - 1],
            ],
            axis=1,
        )
        repeated = jnp.tile(cyclic, (1, row_count))[:, : row_count * (2 * row_count - 1)]
        tiles_list.append(
            repeated.reshape(group_count, row_count, 2 * row_count - 1)[:, :, :row_count]
        )
    return tiles_list


def apply_forward(band_tile, source):
    row_count, channels = source.shape
    grouped = source.reshape(row_count, band_tile.shape[0], -1)
    return jnp.einsum(
        "gst,sgc->tgc", band_tile, grouped, preferred_element_type=jnp.float32
    ).reshape(row_count, channels)


def apply_adjoint(band_tile, source):
    row_count, channels = source.shape
    grouped = source.reshape(row_count, band_tile.shape[0], -1)
    return jnp.einsum(
        "gst,tgc->sgc", band_tile, grouped, preferred_element_type=jnp.float32
    ).reshape(row_count, channels)


def causal_taps(extended, weights, ext_ids, doc_ids):
    row_count = doc_ids.shape[0]
    summed = jnp.zeros((row_count, extended.shape[1]), jnp.float32)
    for offset in range(3):
        first_row = 2 - offset
        same_doc = ext_ids[first_row : first_row + row_count] == doc_ids
        summed = summed + jnp.where(
            same_doc[:, None],
            weights[offset][None, :]
            * extended[first_row : first_row + row_count].astype(jnp.float32),
            0.0,
        )
    return summed


def anti_taps(extended, weights, ext_ids, doc_ids):
    row_count = doc_ids.shape[0]
    summed = jnp.zeros((row_count, extended.shape[1]), jnp.float32)
    for offset in range(3):
        same_doc = ext_ids[offset : offset + row_count] == doc_ids
        summed = summed + jnp.where(
            same_doc[:, None],
            weights[offset][None, :] * extended[offset : offset + row_count].astype(jnp.float32),
            0.0,
        )
    return summed


def local(
    query_in,
    key_in,
    value_in,
    short_weight,
    long_filter,
    skip_weight,
    out_weight,
    doc_ids,
    out_grad,
):
    row_count, channels = query_in.shape
    before_ids = shifted(doc_ids[-2:] + 1, "ctx", 1) - 1
    after_ids = shifted(doc_ids[:2] + 1, "ctx", -1) - 1
    first_id = doc_ids[0]
    last_id = doc_ids[-1]
    prev_last = before_ids[1]
    next_first = after_ids[0]
    single_doc = first_id == last_id
    joins_next = next_first == last_id
    joins_prev = prev_last == first_id
    prev_rows = shifted((query_in[-2:], key_in[-2:], value_in[-2:]), "ctx", 1)
    back_ids = jnp.concatenate([before_ids, doc_ids])
    query_short = causal_taps(
        jnp.concatenate([prev_rows[0], query_in]), short_weight[0], back_ids, doc_ids
    )
    key_short = causal_taps(
        jnp.concatenate([prev_rows[1], key_in]), short_weight[1], back_ids, doc_ids
    )
    value_short = causal_taps(
        jnp.concatenate([prev_rows[2], value_in]), short_weight[2], back_ids, doc_ids
    )
    gated = (key_short * value_short).astype(jnp.bfloat16)
    tiles_list = toeplitz_tiles(long_filter, row_count, HOPS)
    same_doc = doc_ids[:, None] == doc_ids[None, :]
    diagonal = jnp.where(same_doc[None], tiles_list[0], jnp.zeros((), tiles_list[0].dtype))
    head_rows = (doc_ids == first_id)[:, None]
    tail_rows = (doc_ids == last_id)[:, None]
    zero_half = jnp.zeros((), gated.dtype)

    def cross_term(is_live, product, band_tile, source):
        summand = jnp.where(is_live, product(band_tile, source), 0.0)
        return summand

    mixed = apply_forward(diagonal, gated) + skip_weight[None, :] * gated.astype(jnp.float32)
    own_tail = jnp.where(tail_rows, gated, zero_half)
    moving = jnp.where(joins_next, own_tail, zero_half)
    for distance in range(1, HOPS + 1):
        moving = shifted(moving, "ctx", 1)
        is_live = jnp.any(moving != 0)
        mixed = mixed + jnp.where(
            head_rows, cross_term(is_live, apply_forward, tiles_list[distance], moving), 0.0
        )
        moving = jnp.where(single_doc & joins_next, moving, zero_half)
    pre_gate = (query_short * mixed).astype(jnp.bfloat16)
    weight_rows = lax.all_gather(out_weight, "ctx", axis=0, tiled=True)
    matched = weight_rows
    out_sum = jnp.dot(
        lax.all_gather(pre_gate, "ch", axis=1, tiled=True),
        matched,
        preferred_element_type=jnp.float32,
    )
    matched = weight_rows
    grad_cols = lax.psum_scatter(
        lax.dot_general(
            matched, out_grad, (((1,), (1,)), ((), ())), preferred_element_type=jnp.float32
        ),
        "ch",
        scatter_dimension=0,
        tiled=True,
    )
    layer_out = out_sum.astype(jnp.bfloat16)
    grad_pre = jnp.transpose(grad_cols)
    grad_query_short = (grad_pre * mixed).astype(jnp.bfloat16)
    grad_mixed = (grad_pre * query_short).astype(jnp.bfloat16)
    own_head = jnp.where(head_rows, grad_mixed, zero_half)
    grad_gated = apply_adjoint(diagonal, grad_mixed) + skip_weight[None, :] * grad_mixed.astype(
        jnp.float32
    )
    moving_back = jnp.where(joins_prev, own_head, zero_half)
    for distance in range(1, HOPS + 1):
        moving_back = shifted(moving_back, "ctx", -1)
        is_live = jnp.any(moving_back != 0)
        grad_gated = grad_gated + jnp.where(
            tail_rows, cross_term(is_live, apply_adjoint, tiles_list[distance], moving_back), 0.0
        )
        moving_back = jnp.where(single_doc & joins_prev, moving_back, zero_half)
    grad_key_short = (grad_gated * value_short).astype(jnp.bfloat16)
    grad_value_short = (grad_gated * key_short).astype(jnp.bfloat16)
    next_rows = shifted((grad_query_short[:2], grad_key_short[:2], grad_value_short[:2]), "ctx", -1)
    ahead_ids = jnp.concatenate([doc_ids, after_ids])
    grad_query = anti_taps(
        jnp.concatenate([grad_query_short, next_rows[0]]), short_weight[0], ahead_ids, doc_ids
    ).astype(jnp.bfloat16)
    grad_key = anti_taps(
        jnp.concatenate([grad_key_short, next_rows[1]]), short_weight[1], ahead_ids, doc_ids
    ).astype(jnp.bfloat16)
    grad_value = anti_taps(
        jnp.concatenate([grad_value_short, next_rows[2]]), short_weight[2], ahead_ids, doc_ids
    ).astype(jnp.bfloat16)
    return (layer_out, grad_query, grad_key, grad_value)


def solution(mesh):
    return jax.shard_map(
        local,
        mesh=mesh,
        in_specs=(
            P("ctx", "ch"),
            P("ctx", "ch"),
            P("ctx", "ch"),
            P(None, None, "ch"),
            P("ch", None),
            P("ch"),
            P("ctx", "ch"),
            P("ctx"),
            P("ctx", "ch"),
        ),
        out_specs=(P("ctx", "ch"), P("ctx", "ch"), P("ctx", "ch"), P("ctx", "ch")),
        check_vma=False,
    )
```

profile of v0, /device:TPU:1, one launch (start us, length us, event | category | flops | bytes accessed | tf_op | source)
XLA Modules:
  0.0 379.4 jit_solution(4327605552182288887)
XLA Ops:
  8.0 128.3 %all-gather.5.cloned.1.call-done = bf16[4096,512]{1,0:T(8,128)(2,1)} async-done(((bf16[64,512]{1,0:T(8,128)(2,1)}), bf16[4096,512]{1,0:T(8,128)(2,1)}) %all-gather.5.cloned.1.call-update) | async-done | bytes 4194320 | tf_op jit(solution)/shard_map/all_gather | solution.py:142
  136.3 5.5 %fusion.39 = f32[4096,256]{1,0:T(8,128)} fusion(bf16[4096,512]{1,0:T(8,128)(2,1)} %all-gather.5.cloned.1.call-done, bf16[256,512]{1,0:T(8,128)(2,1)S(1)} %copy-done), kind=kOutput, calls=%fused_computation.116 | convolution fusion | flops 1073741824 | bytes 8650752 | tf_op jit(solution)/shard_map/dot_general | solution.py:151
  145.3 3.4 collective-permute-start
  166.8 3.3 select_select_fusion.1
  170.1 2.9 collective-permute-start.5
  177.2 3.1 reshape.150
  182.4 3.1 reshape.148
  187.6 3.0 reshape.146
  194.1 4.1 %reshape.143 = bf16[4,256,511]{2,1,0:T(8,128)(2,1)} reshape(bf16[4,130816]{1,0:T(4,128)(2,1)} %slice.278) | data formatting | bytes 2093056 | tf_op jit(solution)/shard_map/reshape | solution.py:38
  204.9 2.6 broadcast_select_fusion.5
  207.5 3.8 collective-permute-start.7
  216.8 58.6 %reduce-scatter.2.cloned.1.call-done = f32[512,256]{1,0:T(8,128)} async-done(((f32[4096,256]{1,0:T(8,128)}), f32[512,256]{1,0:T(8,128)}) %reduce-scatter.2.cloned.1.call-update) | async-done | bytes 524304 | tf_op jit(solution)/shard_map/reduce_scatter | solution.py:150
  275.4 2.9 fusion.6
  279.6 4.0 %collective-permute-start.8 = (bf16[2,512]{0,1:T(8,128)(2,1)}, bf16[2,512]{0,1:T(8,128)(2,1)}, u32[]{:S(2)}, u32[]{:S(2)}) collective-permute-start(bf16[2,512]{0,1:T(8,128)(2,1)} %slice.286), channel_id=1, source_target_pairs={{8,0},{16,8},{24,16},{32,24},{40,32},{48,40},{56,48},{64,56},{72,6... | collective-permute-start | bytes 6152 | tf_op jit(solution)/shard_map/ppermute | solution.py:12
  285.3 2.2 collective-permute-done.8
  287.6 3.4 add_convert_fusion.2
  293.5 2.8 select_select_fusion
  299.7 4.9 %collective-permute-done.9 = bf16[256,512]{0,1:T(8,128)(2,1)} collective-permute-done((bf16[256,512]{0,1:T(8,128)(2,1)}, bf16[256,512]{0,1:T(8,128)(2,1)}, u32[]{:S(2)}, u32[]{:S(2)}) %collective-permute-start.9) | collective-permute-done | bytes 262176 | tf_op jit(solution)/shard_map/ppermute | solution.py:12
  311.1 2.5 collective-permute-done.10
  317.3 4.1 %collective-permute-done.11 = bf16[256,512]{0,1:T(8,128)(2,1)S(1)} collective-permute-done((bf16[256,512]{0,1:T(8,128)(2,1)S(1)}, bf16[256,512]{0,1:T(8,128)(2,1)S(1)}, u32[]{:S(2)}, u32[]{:S(2)}) %collective-permute-start.11) | collective-permute-done | bytes 262176 | tf_op jit(solution)/shard_map/ppermute | solution.py:12
  326.8 4.4 %collective-permute-done.13 = bf16[2,512]{0,1:T(8,128)(2,1)S(1)} collective-permute-done((bf16[2,512]{0,1:T(8,128)(2,1)S(1)}, bf16[2,512]{0,1:T(8,128)(2,1)S(1)}, u32[]{:S(2)}, u32[]{:S(2)}) %collective-permute-start.13) | collective-permute-done | bytes 2080 | tf_op jit(solution)/shard_map/ppermute | solution.py:12
  335.7 3.1 collective-permute-done.12
  340.1 27.9 %all-gather.3.cloned.1.call-done = bf16[256,4096]{0,1:T(8,128)(2,1)} async-done(((bf16[256,512]{0,1:T(8,128)(2,1)}), bf16[256,4096]{0,1:T(8,128)(2,1)}) %all-gather.3.cloned.1.call-update) | async-done | bytes 2097168 | tf_op jit(solution)/shard_map/all_gather | solution.py:145
  368.1 4.8 %convolution_convert_fusion = bf16[256,512]{1,0:T(8,128)(2,1)} fusion(bf16[256,4096]{0,1:T(8,128)(2,1)} %all-gather.3.cloned.1.call-done, bf16[4096,512]{1,0:T(8,128)(2,1)} %all-gather.5.cloned.1.call-done), kind=kOutput, calls=%fused_computation | convolution fusion | flops 1073872896 | bytes 6553600 | tf_op jit(solution)/shard_map/dot_general | solution.py:144
  (132 shorter events, 73.1 us)
Async XLA Ops:
  7.2 129.1 %copy-start = (bf16[256,512]{1,0:T(8,128)(2,1)S(1)}, bf16[256,512]{1,0:T(8,128)(2,1)}, u32[]{:S(2)}) copy-start(bf16[256,512]{1,0:T(8,128)(2,1)} %param.17) | copy-start | bytes 786436
  7.2 129.1 %all-gather.5.cloned.1.call-start = ((), (), s32[]{:S(2)}) async-start(), calls=%async_computation.2 | async-start | bytes 4259840 | tf_op jit(solution)/shard_map/all_gather | solution.py:142
  7.9 267.4 %reduce-scatter.2.cloned.1.call-start = ((), (), s32[]{:S(2)}) async-start(), calls=%async_computation.3 | async-start | bytes 4718592 | tf_op jit(solution)/shard_map/reduce_scatter | solution.py:150
  141.8 226.3 %all-gather.3.cloned.1.call-start = ((), (), s32[]{:S(2)}) async-start(), calls=%async_computation.1 | async-start | bytes 2359296 | tf_op jit(solution)/shard_map/all_gather | solution.py:145
  143.1 19.3 %collective-permute-start.4 = (s32[2]{0:T(128)}, s32[2]{0:T(128)}, u32[]{:S(2)}, u32[]{:S(2)}) collective-permute-start(s32[2]{0:T(128)} %get-tuple-element.55), channel_id=1, source_target_pairs={{8,0},{16,8},{24,16},{32,24},{40,32},{48,40},{56,48},{64,56},{72,6... | collective-permute-start | bytes 32 | tf_op jit(solution)/shard_map/ppermute | solution.py:12
  145.3 17.7 %collective-permute-start = (s32[2]{0:T(128)}, s32[2]{0:T(128)}, u32[]{:S(2)}, u32[]{:S(2)}) collective-permute-start(s32[2]{0:T(128)} %get-tuple-element.54), channel_id=1, source_target_pairs={{0,8},{8,16},{16,24},{24,32},{32,40},{40,48},{48,56},{56,64},{64,7... | collective-permute-start | bytes 32 | tf_op jit(solution)/shard_map/ppermute | solution.py:12
  150.2 135.2 %collective-permute-start.1 = (bf16[2,512]{0,1:T(8,128)(2,1)}, bf16[2,512]{0,1:T(8,128)(2,1)}, u32[]{:S(2)}, u32[]{:S(2)}) collective-permute-start(bf16[2,512]{0,1:T(8,128)(2,1)} %copy.26), channel_id=1, source_target_pairs={{0,8},{8,16},{16,24},{24,32},{32,40},{40,48},{48,56},{56,64},{64,7... | collective-permute-start | bytes 6152 | tf_op jit(solution)/shard_map/ppermute | solution.py:12
  152.9 13.9 %collective-permute-start.2 = (bf16[2,512]{0,1:T(8,128)(2,1)}, bf16[2,512]{0,1:T(8,128)(2,1)}, u32[]{:S(2)}, u32[]{:S(2)}) collective-permute-start(bf16[2,512]{0,1:T(8,128)(2,1)} %copy.29), channel_id=1, source_target_pairs={{0,8},{8,16},{16,24},{24,32},{32,40},{40,48},{48,56},{56,64},{64,7... | collective-permute-start | bytes 6152 | tf_op jit(solution)/shard_map/ppermute | solution.py:12
  155.9 10.9 %collective-permute-start.3 = (bf16[2,512]{0,1:T(8,128)(2,1)}, bf16[2,512]{0,1:T(8,128)(2,1)S(1)}, u32[]{:S(2)}, u32[]{:S(2)}) collective-permute-start(bf16[2,512]{0,1:T(8,128)(2,1)} %copy.32), channel_id=1, source_target_pairs={{0,8},{8,16},{16,24},{24,32},{32,40},{40,48},{48,56},{56,64},{64,7... | collective-permute-start | bytes 6152 | tf_op jit(solution)/shard_map/ppermute | solution.py:12
  170.1 30.2 %collective-permute-start.5 = (bf16[256,512]{0,1:T(8,128)(2,1)}, bf16[256,512]{0,1:T(8,128)(2,1)}, u32[]{:S(2)}, u32[]{:S(2)}) collective-permute-start(bf16[256,512]{0,1:T(8,128)(2,1)} %get-tuple-element.18), channel_id=1, source_target_pairs={{0,8},{8,16},{16,24},{24,32},{32,40},{40,48},{48,56},{56,64},{64,7... | collective-permute-start | bytes 786440 | tf_op jit(solution)/shard_map/ppermute | solution.py:12
  201.3 6.2 %collective-permute-start.6 = (bf16[256,512]{0,1:T(8,128)(2,1)S(1)}, bf16[256,512]{0,1:T(8,128)(2,1)S(1)}, u32[]{:S(2)}, u32[]{:S(2)}) collective-permute-start(bf16[256,512]{0,1:T(8,128)(2,1)S(1)} %broadcast_select_fusion.9), channel_id=1, source_target_pairs={{0,8},{8,16},{16,24},{24,32},{32,40},{40,48},{48,56},{56,64},{64,7... | collective-permute-start | bytes 786440 | tf_op jit(solution)/shard_map/ppermute | solution.py:12
  207.5 80.1 %copy-start.10 = (pred[256]{0:T(512)(128)(4,1)S(1)}, pred[256]{0:T(512)(128)(4,1)}, u32[]{:S(2)}) copy-start(pred[256]{0:T(512)(128)(4,1)} %get-tuple-element.45) | copy-start | bytes 772
  207.5 6.9 %collective-permute-start.7 = (bf16[256,512]{0,1:T(8,128)(2,1)S(1)}, bf16[256,512]{0,1:T(8,128)(2,1)S(1)}, u32[]{:S(2)}, u32[]{:S(2)}) collective-permute-start(bf16[256,512]{0,1:T(8,128)(2,1)S(1)} %broadcast_select_fusion.8), channel_id=1, source_target_pairs={{0,8},{8,16},{16,24},{24,32},{32,40},{40,48},{48,56},{56,64},{64,7... | collective-permute-start | bytes 786440 | tf_op jit(solution)/shard_map/ppermute | solution.py:12
  279.6 8.0 %collective-permute-start.8 = (bf16[2,512]{0,1:T(8,128)(2,1)}, bf16[2,512]{0,1:T(8,128)(2,1)}, u32[]{:S(2)}, u32[]{:S(2)}) collective-permute-start(bf16[2,512]{0,1:T(8,128)(2,1)} %slice.286), channel_id=1, source_target_pairs={{8,0},{16,8},{24,16},{32,24},{40,32},{48,40},{56,48},{64,56},{72,6... | collective-permute-start | bytes 6152 | tf_op jit(solution)/shard_map/ppermute | solution.py:12
  296.3 8.3 %collective-permute-start.9 = (bf16[256,512]{0,1:T(8,128)(2,1)}, bf16[256,512]{0,1:T(8,128)(2,1)}, u32[]{:S(2)}, u32[]{:S(2)}) collective-permute-start(bf16[256,512]{0,1:T(8,128)(2,1)} %get-tuple-element.14), channel_id=1, source_target_pairs={{8,0},{16,8},{24,16},{32,24},{40,32},{48,40},{56,48},{64,56},{72,6... | collective-permute-start | bytes 786440 | tf_op jit(solution)/shard_map/ppermute | solution.py:12
  298.2 24.8 %copy-start.2 = (bf16[256,512]{0,1:T(8,128)(2,1)S(1)}, bf16[256,512]{0,1:T(8,128)(2,1)}, u32[]{:S(2)}) copy-start(bf16[256,512]{0,1:T(8,128)(2,1)} %copy.28) | copy-start | bytes 786436
  298.2 24.8 %copy-start.5 = (bf16[256,512]{0,1:T(8,128)(2,1)S(1)}, bf16[256,512]{0,1:T(8,128)(2,1)}, u32[]{:S(2)}) copy-start(bf16[256,512]{0,1:T(8,128)(2,1)} %get-tuple-element.15) | copy-start | bytes 786436
  305.5 8.1 %collective-permute-start.10 = (bf16[256,512]{0,1:T(8,128)(2,1)S(1)}, bf16[256,512]{0,1:T(8,128)(2,1)S(1)}, u32[]{:S(2)}, u32[]{:S(2)}) collective-permute-start(bf16[256,512]{0,1:T(8,128)(2,1)S(1)} %broadcast_select_fusion.7), channel_id=1, source_target_pairs={{8,0},{16,8},{24,16},{32,24},{40,32},{48,40},{56,48},{64,56},{72,6... | collective-permute-start | bytes 786440 | tf_op jit(solution)/shard_map/ppermute | solution.py:12
  309.1 22.0 %copy-start.14 = (f32[1,1,512]{2,1,0:T(1,128)S(1)}, f32[1,1,512]{2,1,0:T(1,128)}, u32[]{:S(2)}) copy-start(f32[1,1,512]{2,1,0:T(1,128)} %get-tuple-element.28) | copy-start | bytes 6148
  309.1 22.0 %copy-start.16 = (pred[256]{0:T(512)(128)(4,1)S(1)}, pred[256]{0:T(512)(128)(4,1)}, u32[]{:S(2)}) copy-start(pred[256]{0:T(512)(128)(4,1)} %get-tuple-element.39) | copy-start | bytes 772
  309.2 22.0 %copy-start.18 = (pred[256]{0:T(512)(128)(4,1)S(1)}, pred[256]{0:T(512)(128)(4,1)}, u32[]{:S(2)}) copy-start(pred[256]{0:T(512)(128)(4,1)} %get-tuple-element.40) | copy-start | bytes 772
  313.7 7.7 %collective-permute-start.11 = (bf16[256,512]{0,1:T(8,128)(2,1)S(1)}, bf16[256,512]{0,1:T(8,128)(2,1)S(1)}, u32[]{:S(2)}, u32[]{:S(2)}) collective-permute-start(bf16[256,512]{0,1:T(8,128)(2,1)S(1)} %broadcast_select_fusion.6), channel_id=1, source_target_pairs={{8,0},{16,8},{24,16},{32,24},{40,32},{48,40},{56,48},{64,56},{72,6... | collective-permute-start | bytes 786440 | tf_op jit(solution)/shard_map/ppermute | solution.py:12
  324.8 6.3 %collective-permute-start.13 = (bf16[2,512]{0,1:T(8,128)(2,1)S(1)}, bf16[2,512]{0,1:T(8,128)(2,1)S(1)}, u32[]{:S(2)}, u32[]{:S(2)}) collective-permute-start(bf16[2,512]{0,1:T(8,128)(2,1)S(1)} %slice.292), channel_id=1, source_target_pairs={{8,0},{16,8},{24,16},{32,24},{40,32},{48,40},{56,48},{64,56},{72,6... | collective-permute-start | bytes 6152 | tf_op jit(solution)/shard_map/ppermute | solution.py:12
  332.1 6.7 %collective-permute-start.12 = (bf16[2,512]{0,1:T(8,128)(2,1)S(1)}, bf16[2,512]{0,1:T(8,128)(2,1)S(1)}, u32[]{:S(2)}, u32[]{:S(2)}) collective-permute-start(bf16[2,512]{0,1:T(8,128)(2,1)S(1)} %slice.289), channel_id=1, source_target_pairs={{8,0},{16,8},{24,16},{32,24},{40,32},{48,40},{56,48},{64,56},{72,6... | collective-permute-start | bytes 6152 | tf_op jit(solution)/shard_map/ppermute | solution.py:12
  (15 other events, 205.9 us)
Sparse Core Ops, SparseCore 0:
  10.1 126.0 all-gather.4
  141.9 133.4 reduce-scatter.1
  291.1 76.9 all-gather.2
where the time goes:
time: 381 us; the launch traced here: 379 us
  waiting for transfers between devices  237 us (62%)
  local copies, waits for them, and re-layouts  38.3 us (10%)
  starting transfers between devices  33.8 us (9%)
  other arithmetic  28.2 us (7%)
  matrix products  23.8 us (6%)
  between operations  18 us (5%)
    all_gather x1, waiting for transfers between devices, local(): weight_rows = lax.all_gather(out_weight, 'ctx', axis=0, tiled=True)  128 us
    reduce_scatter x1, waiting for transfers between devices, local(): lax.psum_scatter(lax.dot_general(matched, out_grad, (((1,), (1,)), ((), (...  58.6 us
    ppermute x14, starting transfers between devices, shifted(): return lax.ppermute(array, axis, pairs)  33.7 us
    all_gather x1, waiting for transfers between devices, local(): lax.all_gather(pre_gate, 'ch', axis=1, tiled=True)  27.9 us
    ppermute x14, waiting for transfers between devices, shifted(): return lax.ppermute(array, axis, pairs)  21.8 us
    reshape x4, local copies, waits for them, and re-layouts, toeplitz_tiles(): repeated.reshape(group_count, row_count, 2 * row_count - 1)  13.3 us
    unnamed x58, local copies, waits for them, and re-layouts  13.2 us
    dot_general x4, matrix products, apply_forward(): jnp.einsum('gst,sgc->tgc', band_tile, grouped, preferred_element_type=jnp...  8.18 us
  transfers between devices with their start and end apart: 17, of which 10 were waited for; matrix products, arithmetic and copies ran while one was open for 20% of the time, Pallas kernels for 0%

commit v1 on v0

--- a/solution.py
+++ b/solution.py
@@ -1,9 +1,19 @@
 import jax
 import jax.numpy as jnp
 from jax import lax
-from jax.sharding import PartitionSpec as P
+from jax.sharding import Mesh, PartitionSpec as P
 
 HOPS = 3
+CHIPS = ("zl", "y")
+CTX = ("zl", "y", "core")
+CH = ("zh", "x")
+
+
+def gather_weight(out_weight, chip_count):
+    spread = jnp.broadcast_to(out_weight[None], (chip_count,) + out_weight.shape)
+    mine = lax.all_to_all(spread, CHIPS, 0, 0, tiled=True).reshape(-1, out_weight.shape[1])
+    other = lax.ppermute(mine, "core", [(0, 1), (1, 0)])
+    return mine, other, lax.axis_index("core")
 
 
 def shifted(array, axis, by):
@@ -96,8 +106,8 @@
     out_grad,
 ):
     row_count, channels = query_in.shape
-    before_ids = shifted(doc_ids[-2:] + 1, "ctx", 1) - 1
-    after_ids = shifted(doc_ids[:2] + 1, "ctx", -1) - 1
+    before_ids = shifted(doc_ids[-2:] + 1, CTX, 1) - 1
+    after_ids = shifted(doc_ids[:2] + 1, CTX, -1) - 1
     first_id = doc_ids[0]
     last_id = doc_ids[-1]
     prev_last = before_ids[1]
@@ -105,7 +115,7 @@
     single_doc = first_id == last_id
     joins_next = next_first == last_id
     joins_prev = prev_last == first_id
-    prev_rows = shifted((query_in[-2:], key_in[-2:], value_in[-2:]), "ctx", 1)
+    prev_rows = shifted((query_in[-2:], key_in[-2:], value_in[-2:]), CTX, 1)
     back_ids = jnp.concatenate([before_ids, doc_ids])
     query_short = causal_taps(
         jnp.concatenate([prev_rows[0], query_in]), short_weight[0], back_ids, doc_ids
@@ -132,29 +142,45 @@
     own_tail = jnp.where(tail_rows, gated, zero_half)
     moving = jnp.where(joins_next, own_tail, zero_half)
     for distance in range(1, HOPS + 1):
-        moving = shifted(moving, "ctx", 1)
+        moving = shifted(moving, CTX, 1)
         is_live = jnp.any(moving != 0)
         mixed = mixed + jnp.where(
             head_rows, cross_term(is_live, apply_forward, tiles_list[distance], moving), 0.0
         )
         moving = jnp.where(single_doc & joins_next, moving, zero_half)
     pre_gate = (query_short * mixed).astype(jnp.bfloat16)
-    weight_rows = lax.all_gather(out_weight, "ctx", axis=0, tiled=True)
-    matched = weight_rows
-    out_sum = jnp.dot(
-        lax.all_gather(pre_gate, "ch", axis=1, tiled=True),
-        matched,
-        preferred_element_type=jnp.float32,
-    )
-    matched = weight_rows
-    grad_cols = lax.psum_scatter(
-        lax.dot_general(
-            matched, out_grad, (((1,), (1,)), ((), ())), preferred_element_type=jnp.float32
-        ),
-        "ch",
-        scatter_dimension=0,
-        tiled=True,
-    )
+    pair_size = lax.axis_size("core")
+    chip_count = lax.axis_size(CHIPS)
+    weight_rows, weight_rows_other, core_index = gather_weight(out_weight, chip_count)
+    ch_count = lax.axis_size(CH)
+    spread = jnp.broadcast_to(pre_gate[None], (ch_count,) + pre_gate.shape)
+    gathered = lax.all_to_all(spread, CH, 0, 0, tiled=True).reshape(
+        ch_count, row_count, channels
+    )
+    full_pre = jnp.transpose(gathered, (1, 0, 2)).reshape(
+        row_count, chip_count, pair_size, out_weight.shape[0]
+    )
+    pre_first = full_pre[:, :, 0].reshape(row_count, -1)
+    pre_second = full_pre[:, :, 1].reshape(row_count, -1)
+    on_first = core_index == 0
+    pre_mine = jnp.where(on_first, pre_first, pre_second)
+    pre_other = jnp.where(on_first, pre_second, pre_first)
+    out_sum = jnp.dot(pre_mine, weight_rows, preferred_element_type=jnp.float32) + jnp.dot(
+        pre_other, weight_rows_other, preferred_element_type=jnp.float32
+    )
+    dims = (((1,), (1,)), ((), ()))
+    part_mine = lax.dot_general(
+        weight_rows, out_grad, dims, preferred_element_type=jnp.float32
+    ).reshape(chip_count, 1, -1, row_count)
+    part_other = lax.dot_general(
+        weight_rows_other, out_grad, dims, preferred_element_type=jnp.float32
+    ).reshape(chip_count, 1, -1, row_count)
+    partial = jnp.where(
+        on_first,
+        jnp.concatenate([part_mine, part_other], axis=1),
+        jnp.concatenate([part_other, part_mine], axis=1),
+    ).reshape(-1, row_count)
+    grad_cols = lax.psum_scatter(partial, CH, scatter_dimension=0, tiled=True)
     layer_out = out_sum.astype(jnp.bfloat16)
     grad_pre = jnp.transpose(grad_cols)
     grad_query_short = (grad_pre * mixed).astype(jnp.bfloat16)
@@ -165,7 +191,7 @@
     )
     moving_back = jnp.where(joins_prev, own_head, zero_half)
     for distance in range(1, HOPS + 1):
-        moving_back = shifted(moving_back, "ctx", -1)
+        moving_back = shifted(moving_back, CTX, -1)
         is_live = jnp.any(moving_back != 0)
         grad_gated = grad_gated + jnp.where(
             tail_rows, cross_term(is_live, apply_adjoint, tiles_list[distance], moving_back), 0.0
@@ -173,7 +199,7 @@
         moving_back = jnp.where(single_doc & joins_prev, moving_back, zero_half)
     grad_key_short = (grad_gated * value_short).astype(jnp.bfloat16)
     grad_value_short = (grad_gated * key_short).astype(jnp.bfloat16)
-    next_rows = shifted((grad_query_short[:2], grad_key_short[:2], grad_value_short[:2]), "ctx", -1)
+    next_rows = shifted((grad_query_short[:2], grad_key_short[:2], grad_value_short[:2]), CTX, -1)
     ahead_ids = jnp.concatenate([doc_ids, after_ids])
     grad_query = anti_taps(
         jnp.concatenate([grad_query_short, next_rows[0]]), short_weight[0], ahead_ids, doc_ids
@@ -188,20 +214,25 @@
 
 
 def solution(mesh):
+    zl, y, core = 4, 8, 2
+    split_mesh = Mesh(
+        mesh.devices.reshape(zl, y, core, mesh.devices.shape[1] // 4, 4),
+        ("zl", "y", "core", "zh", "x"),
+    )
     return jax.shard_map(
         local,
-        mesh=mesh,
+        mesh=split_mesh,
         in_specs=(
-            P("ctx", "ch"),
-            P("ctx", "ch"),
-            P("ctx", "ch"),
-            P(None, None, "ch"),
-            P("ch", None),
-            P("ch"),
-            P("ctx", "ch"),
-            P("ctx"),
-            P("ctx", "ch"),
+            P(CTX, CH),
+            P(CTX, CH),
+            P(CTX, CH),
+            P(None, None, CH),
+            P(CH, None),
+            P(CH),
+            P(CTX, CH),
+            P(CTX),
+            P(CTX, CH),
         ),
-        out_specs=(P("ctx", "ch"), P("ctx", "ch"), P("ctx", "ch"), P("ctx", "ch")),
+        out_specs=(P(CTX, CH), P(CTX, CH), P(CTX, CH), P(CTX, CH)),
         check_vma=False,
     )

time: 381 us -> 316 us (0.83)
  the two profiles are of different devices: /device:TPU:1 before, /device:TPU:125 now
where the time goes in v1:
time: 316 us; the launch traced here: 315 us
  waiting for transfers between devices  85.8 us (27%)
  blocking collectives  58.3 us (18%)
  starting transfers between devices  50 us (16%)
  local copies, waits for them, and re-layouts  49.7 us (16%)
  other arithmetic  31.6 us (10%)
  matrix products  20.5 us (6%)
  between operations  18.7 us (6%)
    all_to_all x1, blocking collectives, gather_weight(): lax.all_to_all(spread, CHIPS, 0, 0, tiled=True)  58.3 us
    reduce_scatter x1, waiting for transfers between devices, local(): grad_cols = lax.psum_scatter(partial, CH, scatter_dimension=0, tiled=True)  45.6 us
    ppermute x14, starting transfers between devices, shifted(): return lax.ppermute(array, axis, pairs)  40 us
    ppermute x14, waiting for transfers between devices, shifted(): return lax.ppermute(array, axis, pairs)  37.1 us
    unnamed x66, local copies, waits for them, and re-layouts  17.6 us
    reshape x4, local copies, waits for them, and re-layouts, toeplitz_tiles(): repeated.reshape(group_count, row_count, 2 * row_count - 1)  15.2 us
    dot_general x4, matrix products, apply_forward(): jnp.einsum('gst,sgc->tgc', band_tile, grouped, preferred_element_type=jnp...  8.34 us
  transfers between devices with their start and end apart: 17, of which 9 were waited for; matrix products, arithmetic and copies ran while one was open for 27% of the time, Pallas kernels for 0%

profile of v1, /device:TPU:125, one launch (start us, length us, event | category | flops | bytes accessed | tf_op | source)
XLA Modules:
  0.0 314.6 jit_solution(5645112132023652890)
XLA Ops:
  8.3 58.3 %all_to_all.10 = bf16[32,64,512]{2,1,0:T(8,128)(2,1)S(1)} all-to-all(bf16[32,64,512]{2,1,0:T(8,128)(2,1)S(1)} %broadcast_in_dim.199), channel_id=1, replica_groups=mesh['zl'=4,'y'=8,'core'=2,'zh'=2,'x'=4] {'zl','y'}, dimensions={0} | all-to-all | bytes 4194304 | tf_op jit(solution)/shard_map/all_to_all | solution.py:14
  66.7 4.0 %collective-permute-start.8 = (bf16[2048,512]{1,0:T(8,128)(2,1)S(1)}, bf16[2048,512]{1,0:T(8,128)(2,1)}, u32[]{:S(2)}, u32[]{:S(2)}) collective-permute-start(bf16[2048,512]{1,0:T(8,128)(2,1)S(1)} %bitcast.137), channel_id=1, source_target_pairs={{0,8},{8,0},{1,9},{9,1},{2,10},{10,2},{3,11},{11,3},{4,12},{12,4},... | collective-permute-start | bytes 6291464 | tf_op jit(solution)/shard_map/ppermute | solution.py:15
  71.4 3.1 collective-permute-done.8
  83.5 5.4 %collective-permute-start = (s32[2]{0:T(128)}, s32[2]{0:T(128)}, u32[]{:S(2)}, u32[]{:S(2)}) collective-permute-start(s32[2]{0:T(128)} %get-tuple-element.52), channel_id=1, source_target_pairs={{0,8},{8,16},{16,24},{24,32},{32,40},{40,48},{48,56},{56,64},{64,7... | collective-permute-start | bytes 32 | tf_op jit(solution)/shard_map/ppermute | solution.py:22
  110.3 3.4 %select_select_fusion.1 = (bf16[256,512]{0,1:T(8,128)(2,1)}, bf16[256,512]{0,1:T(8,128)(2,1)}) fusion(pred[256]{0:T(512)(128)(4,1)} %get-tuple-element.41, pred[]{:T(512)S(6)} %eq.69, bf16[256,512]{0,1:T(8,128)(2,1)} %copy.35, bf16[2,512]{0,1:T(8,128)(2,1)S(1)} %collective-permute-done.3, f32[512]{0:T(512)} %bitcast.168, f32[512]{0:T(512)} %bitcast.170, ...), kind=kLoop, calls=%fused_computation.91 | loop fusion | flops 4718592 | bytes 1065729 | tf_op jit(solution)/shard_map/jit(_where)/select_n | solution.py:143
  113.7 3.5 %collective-permute-start.5 = (bf16[256,512]{0,1:T(8,128)(2,1)}, bf16[256,512]{0,1:T(8,128)(2,1)}, u32[]{:S(2)}, u32[]{:S(2)}) collective-permute-start(bf16[256,512]{0,1:T(8,128)(2,1)} %get-tuple-element.14), channel_id=1, source_target_pairs={{0,8},{8,16},{16,24},{24,32},{32,40},{40,48},{48,56},{56,64},{64,7... | collective-permute-start | bytes 786440 | tf_op jit(solution)/shard_map/ppermute | solution.py:22
  121.5 3.0 reshape.175
  127.9 4.1 %reshape.173 = bf16[4,256,511]{2,1,0:T(8,128)(2,1)} reshape(bf16[4,130816]{1,0:T(4,128)(2,1)} %slice.290) | data formatting | bytes 2093056 | tf_op jit(solution)/shard_map/reshape | solution.py:48
  135.4 4.0 %reshape.171 = bf16[4,256,511]{2,1,0:T(8,128)(2,1)} reshape(bf16[4,130816]{1,0:T(4,128)(2,1)} %slice.288) | data formatting | bytes 2093056 | tf_op jit(solution)/shard_map/reshape | solution.py:48
  142.8 4.0 %reshape.168 = bf16[4,256,511]{2,1,0:T(8,128)(2,1)} reshape(bf16[4,130816]{1,0:T(4,128)(2,1)} %slice.286) | data formatting | bytes 2093056 | tf_op jit(solution)/shard_map/reshape | solution.py:48
  156.4 6.6 %collective-permute-start.7 = (bf16[256,512]{0,1:T(8,128)(2,1)S(1)}, bf16[256,512]{0,1:T(8,128)(2,1)S(1)}, u32[]{:S(2)}, u32[]{:S(2)}) collective-permute-start(bf16[256,512]{0,1:T(8,128)(2,1)S(1)} %broadcast_select_fusion.10), channel_id=1, source_target_pairs={{0,8},{8,16},{16,24},{24,32},{32,40},{40,48},{48,56},{56,64},{64,7... | collective-permute-start | bytes 786440 | tf_op jit(solution)/shard_map/ppermute | solution.py:22
  169.1 45.6 %reduce-scatter.2.cloned.1.call-done = f32[512,256]{1,0:T(8,128)} async-done(((f32[4096,256]{1,0:T(8,128)}), f32[512,256]{1,0:T(8,128)}) %reduce-scatter.2.cloned.1.call-update) | async-done | bytes 524304 | tf_op jit(solution)/shard_map/reduce_scatter | solution.py:183
  214.7 2.8 fusion.7
  218.8 3.9 %collective-permute-start.9 = (bf16[2,512]{0,1:T(8,128)(2,1)}, bf16[2,512]{0,1:T(8,128)(2,1)}, u32[]{:S(2)}, u32[]{:S(2)}) collective-permute-start(bf16[2,512]{0,1:T(8,128)(2,1)} %slice.296), channel_id=1, source_target_pairs={{8,0},{16,8},{24,16},{32,24},{40,32},{48,40},{56,48},{64,56},{72,6... | collective-permute-start | bytes 6152 | tf_op jit(solution)/shard_map/ppermute | solution.py:22
  224.6 2.9 collective-permute-done.9
  227.5 3.4 %add_convert_fusion.2 = (bf16[256,512]{0,1:T(8,128)(2,1)}, bf16[256,512]{0,1:T(8,128)(2,1)S(1)}) fusion(bf16[256,512]{0,1:T(8,128)(2,1)} %copy-done.7, bf16[2,512]{0,1:T(8,128)(2,1)} %collective-permute-done.9, f32[512]{0:T(512)} %bitcast.162, f32[512]{0:T(512)} %bitcast.164, f32[512]{0:T(512)} %bitcast.160, pred[256]{0:T(512)(128)(4,1)} %get-tuple-element.38, ...), kind=kLoop, calls=%fused_computation.29 | loop fusion | flops 4587520 | bytes 1584128 | tf_op jit(solution)/shard_map/convert_element_type | solution.py:206
  232.4 6.0 %all-to-all-start = ((bf16[8,256,512]{1,2,0:T(8,128)(2,1)}), bf16[8,256,512]{1,2,0:T(8,128)(2,1)}, u32[]{:S(2)}, u32[]{:S(2)}) async-start(bf16[8,256,512]{1,2,0:T(8,128)(2,1)} %broadcast_in_dim.198), calls=%async_computation | async-start | bytes 4194304 | tf_op jit(solution)/shard_map/all_to_all | solution.py:157
  241.0 2.8 select_select_fusion
  247.3 7.6 %collective-permute-done.10 = bf16[256,512]{0,1:T(8,128)(2,1)} collective-permute-done((bf16[256,512]{0,1:T(8,128)(2,1)}, bf16[256,512]{0,1:T(8,128)(2,1)}, u32[]{:S(2)}, u32[]{:S(2)}) %collective-permute-start.10) | collective-permute-done | bytes 262176 | tf_op jit(solution)/shard_map/ppermute | solution.py:22
  261.4 5.2 %collective-permute-done.11 = bf16[256,512]{0,1:T(8,128)(2,1)S(1)} collective-permute-done((bf16[256,512]{0,1:T(8,128)(2,1)S(1)}, bf16[256,512]{0,1:T(8,128)(2,1)S(1)}, u32[]{:S(2)}, u32[]{:S(2)}) %collective-permute-start.11) | collective-permute-done | bytes 262176 | tf_op jit(solution)/shard_map/ppermute | solution.py:22
  270.3 7.3 %collective-permute-done.12 = bf16[256,512]{0,1:T(8,128)(2,1)S(1)} collective-permute-done((bf16[256,512]{0,1:T(8,128)(2,1)S(1)}, bf16[256,512]{0,1:T(8,128)(2,1)S(1)}, u32[]{:S(2)}, u32[]{:S(2)}) %collective-permute-start.12) | collective-permute-done | bytes 262176 | tf_op jit(solution)/shard_map/ppermute | solution.py:22
  283.1 7.9 %collective-permute-done.14 = bf16[2,512]{0,1:T(8,128)(2,1)S(1)} collective-permute-done((bf16[2,512]{0,1:T(8,128)(2,1)S(1)}, bf16[2,512]{0,1:T(8,128)(2,1)S(1)}, u32[]{:S(2)}, u32[]{:S(2)}) %collective-permute-start.14) | collective-permute-done | bytes 2080 | tf_op jit(solution)/shard_map/ppermute | solution.py:22
  295.5 4.8 %collective-permute-done.13 = bf16[2,512]{0,1:T(8,128)(2,1)S(1)} collective-permute-done((bf16[2,512]{0,1:T(8,128)(2,1)S(1)}, bf16[2,512]{0,1:T(8,128)(2,1)S(1)}, u32[]{:S(2)}, u32[]{:S(2)}) %collective-permute-start.13) | collective-permute-done | bytes 2080 | tf_op jit(solution)/shard_map/ppermute | solution.py:22
  304.8 3.0 fusion
  (146 shorter events, 93.1 us)
Async XLA Ops:
  7.2 63.5 %copy-start = (bf16[256,512]{1,0:T(8,128)(2,1)S(1)}, bf16[256,512]{1,0:T(8,128)(2,1)}, u32[]{:S(2)}) copy-start(bf16[256,512]{1,0:T(8,128)(2,1)} %param.17) | copy-start | bytes 786436
  7.2 207.5 %reduce-scatter.2.cloned.1.call-start = ((), (), s32[]{:S(2)}) async-start(), calls=%async_computation.3 | async-start | bytes 4718592 | tf_op jit(solution)/shard_map/reduce_scatter | solution.py:183
  66.7 7.9 %collective-permute-start.8 = (bf16[2048,512]{1,0:T(8,128)(2,1)S(1)}, bf16[2048,512]{1,0:T(8,128)(2,1)}, u32[]{:S(2)}, u32[]{:S(2)}) collective-permute-start(bf16[2048,512]{1,0:T(8,128)(2,1)S(1)} %bitcast.137), channel_id=1, source_target_pairs={{0,8},{8,0},{1,9},{9,1},{2,10},{10,2},{3,11},{11,3},{4,12},{12,4},... | collective-permute-start | bytes 6291464 | tf_op jit(solution)/shard_map/ppermute | solution.py:15
  79.9 21.5 %copy-start.13 = (bf16[4,768]{1,0:T(4,128)(2,1)S(1)}, bf16[4,768]{1,0:T(4,128)(2,1)}, u32[]{:S(2)}) copy-start(bf16[4,768]{1,0:T(4,128)(2,1)} %param.13) | copy-start | bytes 18436
  79.9 21.6 %copy-start.19 = (f32[3,3,512]{2,1,0:T(4,128)S(1)}, f32[3,3,512]{2,1,0:T(4,128)}, u32[]{:S(2)}) copy-start(f32[3,3,512]{2,1,0:T(4,128)} %param.12) | copy-start | bytes 55300
  81.2 24.2 %collective-permute-start.4 = (s32[2]{0:T(128)}, s32[2]{0:T(128)}, u32[]{:S(2)}, u32[]{:S(2)}) collective-permute-start(s32[2]{0:T(128)} %get-tuple-element.53), channel_id=1, source_target_pairs={{8,0},{16,8},{24,16},{32,24},{40,32},{48,40},{56,48},{64,56},{72,6... | collective-permute-start | bytes 32 | tf_op jit(solution)/shard_map/ppermute | solution.py:22
  83.5 22.6 %collective-permute-start = (s32[2]{0:T(128)}, s32[2]{0:T(128)}, u32[]{:S(2)}, u32[]{:S(2)}) collective-permute-start(s32[2]{0:T(128)} %get-tuple-element.52), channel_id=1, source_target_pairs={{0,8},{8,16},{16,24},{24,32},{32,40},{40,48},{48,56},{56,64},{64,7... | collective-permute-start | bytes 32 | tf_op jit(solution)/shard_map/ppermute | solution.py:22
  90.4 134.2 %collective-permute-start.1 = (bf16[2,512]{0,1:T(8,128)(2,1)}, bf16[2,512]{0,1:T(8,128)(2,1)}, u32[]{:S(2)}, u32[]{:S(2)}) collective-permute-start(bf16[2,512]{0,1:T(8,128)(2,1)} %copy.30), channel_id=1, source_target_pairs={{0,8},{8,16},{16,24},{24,32},{32,40},{40,48},{48,56},{56,64},{64,7... | collective-permute-start | bytes 6152 | tf_op jit(solution)/shard_map/ppermute | solution.py:22
  93.2 17.1 %collective-permute-start.2 = (bf16[2,512]{0,1:T(8,128)(2,1)}, bf16[2,512]{0,1:T(8,128)(2,1)}, u32[]{:S(2)}, u32[]{:S(2)}) collective-permute-start(bf16[2,512]{0,1:T(8,128)(2,1)} %copy.33), channel_id=1, source_target_pairs={{0,8},{8,16},{16,24},{24,32},{32,40},{40,48},{48,56},{56,64},{64,7... | collective-permute-start | bytes 6152 | tf_op jit(solution)/shard_map/ppermute | solution.py:22
  96.6 13.8 %collective-permute-start.3 = (bf16[2,512]{0,1:T(8,128)(2,1)}, bf16[2,512]{0,1:T(8,128)(2,1)S(1)}, u32[]{:S(2)}, u32[]{:S(2)}) collective-permute-start(bf16[2,512]{0,1:T(8,128)(2,1)} %copy.36), channel_id=1, source_target_pairs={{0,8},{8,16},{16,24},{24,32},{32,40},{40,48},{48,56},{56,64},{64,7... | collective-permute-start | bytes 6152 | tf_op jit(solution)/shard_map/ppermute | solution.py:22
  113.7 35.4 %collective-permute-start.5 = (bf16[256,512]{0,1:T(8,128)(2,1)}, bf16[256,512]{0,1:T(8,128)(2,1)}, u32[]{:S(2)}, u32[]{:S(2)}) collective-permute-start(bf16[256,512]{0,1:T(8,128)(2,1)} %get-tuple-element.14), channel_id=1, source_target_pairs={{0,8},{8,16},{16,24},{24,32},{32,40},{40,48},{48,56},{56,64},{64,7... | collective-permute-start | bytes 786440 | tf_op jit(solution)/shard_map/ppermute | solution.py:22
  150.2 6.2 %collective-permute-start.6 = (bf16[256,512]{0,1:T(8,128)(2,1)S(1)}, bf16[256,512]{0,1:T(8,128)(2,1)S(1)}, u32[]{:S(2)}, u32[]{:S(2)}) collective-permute-start(bf16[256,512]{0,1:T(8,128)(2,1)S(1)} %broadcast_select_fusion.11), channel_id=1, source_target_pairs={{0,8},{8,16},{16,24},{24,32},{32,40},{40,48},{48,56},{56,64},{64,7... | collective-permute-start | bytes 786440 | tf_op jit(solution)/shard_map/ppermute | solution.py:22
  156.4 10.3 %collective-permute-start.7 = (bf16[256,512]{0,1:T(8,128)(2,1)S(1)}, bf16[256,512]{0,1:T(8,128)(2,1)S(1)}, u32[]{:S(2)}, u32[]{:S(2)}) collective-permute-start(bf16[256,512]{0,1:T(8,128)(2,1)S(1)} %broadcast_select_fusion.10), channel_id=1, source_target_pairs={{0,8},{8,16},{16,24},{24,32},{32,40},{40,48},{48,56},{56,64},{64,7... | collective-permute-start | bytes 786440 | tf_op jit(solution)/shard_map/ppermute | solution.py:22
  218.8 8.7 %collective-permute-start.9 = (bf16[2,512]{0,1:T(8,128)(2,1)}, bf16[2,512]{0,1:T(8,128)(2,1)}, u32[]{:S(2)}, u32[]{:S(2)}) collective-permute-start(bf16[2,512]{0,1:T(8,128)(2,1)} %slice.296), channel_id=1, source_target_pairs={{8,0},{16,8},{24,16},{32,24},{40,32},{48,40},{56,48},{64,56},{72,6... | collective-permute-start | bytes 6152 | tf_op jit(solution)/shard_map/ppermute | solution.py:22
  232.4 69.9 %all-to-all-start = ((bf16[8,256,512]{1,2,0:T(8,128)(2,1)}), bf16[8,256,512]{1,2,0:T(8,128)(2,1)}, u32[]{:S(2)}, u32[]{:S(2)}) async-start(bf16[8,256,512]{1,2,0:T(8,128)(2,1)} %broadcast_in_dim.198), calls=%async_computation | async-start | bytes 4194304 | tf_op jit(solution)/shard_map/all_to_all | solution.py:157
  243.8 11.1 %collective-permute-start.10 = (bf16[256,512]{0,1:T(8,128)(2,1)}, bf16[256,512]{0,1:T(8,128)(2,1)}, u32[]{:S(2)}, u32[]{:S(2)}) collective-permute-start(bf16[256,512]{0,1:T(8,128)(2,1)} %get-tuple-element.10), channel_id=1, source_target_pairs={{8,0},{16,8},{24,16},{32,24},{40,32},{48,40},{56,48},{64,56},{72,6... | collective-permute-start | bytes 786440 | tf_op jit(solution)/shard_map/ppermute | solution.py:22
  245.7 23.6 %copy-start.2 = (bf16[4,256,511]{2,1,0:T(8,128)(2,1)S(1)}, bf16[4,256,511]{2,1,0:T(8,128)(2,1)}, u32[]{:S(2)}) copy-start(bf16[4,256,511]{2,1,0:T(8,128)(2,1)} %reshape.173) | copy-start | bytes 3139588
  255.8 10.8 %collective-permute-start.11 = (bf16[256,512]{0,1:T(8,128)(2,1)S(1)}, bf16[256,512]{0,1:T(8,128)(2,1)S(1)}, u32[]{:S(2)}, u32[]{:S(2)}) collective-permute-start(bf16[256,512]{0,1:T(8,128)(2,1)S(1)} %broadcast_select_fusion.9), channel_id=1, source_target_pairs={{8,0},{16,8},{24,16},{32,24},{40,32},{48,40},{56,48},{64,56},{72,6... | collective-permute-start | bytes 786440 | tf_op jit(solution)/shard_map/ppermute | solution.py:22
  261.3 17.9 %copy-start.6 = (bf16[256,512]{0,1:T(8,128)(2,1)S(1)}, bf16[256,512]{0,1:T(8,128)(2,1)}, u32[]{:S(2)}) copy-start(bf16[256,512]{0,1:T(8,128)(2,1)} %copy.32) | copy-start | bytes 786436
  261.4 17.9 %copy-start.9 = (bf16[256,512]{0,1:T(8,128)(2,1)S(1)}, bf16[256,512]{0,1:T(8,128)(2,1)}, u32[]{:S(2)}) copy-start(bf16[256,512]{0,1:T(8,128)(2,1)} %get-tuple-element.11) | copy-start | bytes 786436
  261.4 17.9 %copy-start.15 = (pred[256]{0:T(512)(128)(4,1)S(1)}, pred[256]{0:T(512)(128)(4,1)}, u32[]{:S(2)}) copy-start(pred[256]{0:T(512)(128)(4,1)} %get-tuple-element.44) | copy-start | bytes 772
  266.7 10.9 %collective-permute-start.12 = (bf16[256,512]{0,1:T(8,128)(2,1)S(1)}, bf16[256,512]{0,1:T(8,128)(2,1)S(1)}, u32[]{:S(2)}, u32[]{:S(2)}) collective-permute-start(bf16[256,512]{0,1:T(8,128)(2,1)S(1)} %broadcast_select_fusion.8), channel_id=1, source_target_pairs={{8,0},{16,8},{24,16},{32,24},{40,32},{48,40},{56,48},{64,56},{72,6... | collective-permute-start | bytes 786440 | tf_op jit(solution)/shard_map/ppermute | solution.py:22
  281.1 9.8 %collective-permute-start.14 = (bf16[2,512]{0,1:T(8,128)(2,1)S(1)}, bf16[2,512]{0,1:T(8,128)(2,1)S(1)}, u32[]{:S(2)}, u32[]{:S(2)}) collective-permute-start(bf16[2,512]{0,1:T(8,128)(2,1)S(1)} %slice.302), channel_id=1, source_target_pairs={{8,0},{16,8},{24,16},{32,24},{40,32},{48,40},{56,48},{64,56},{72,6... | collective-permute-start | bytes 6152 | tf_op jit(solution)/shard_map/ppermute | solution.py:22
  291.9 8.4 %collective-permute-start.13 = (bf16[2,512]{0,1:T(8,128)(2,1)S(1)}, bf16[2,512]{0,1:T(8,128)(2,1)S(1)}, u32[]{:S(2)}, u32[]{:S(2)}) collective-permute-start(bf16[2,512]{0,1:T(8,128)(2,1)S(1)} %slice.299), channel_id=1, source_target_pairs={{8,0},{16,8},{24,16},{32,24},{40,32},{48,40},{56,48},{64,56},{72,6... | collective-permute-start | bytes 6152 | tf_op jit(solution)/shard_map/ppermute | solution.py:22
  (19 other events, 205.1 us)
Sparse Core Ops, SparseCore 0:
  80.1 134.5 reduce-scatter.1

commit v2 on v1

--- a/solution.py
+++ b/solution.py
@@ -169,18 +169,21 @@
         pre_other, weight_rows_other, preferred_element_type=jnp.float32
     )
     dims = (((1,), (1,)), ((), ()))
+    block_chips = chip_count // ch_count
     part_mine = lax.dot_general(
         weight_rows, out_grad, dims, preferred_element_type=jnp.float32
-    ).reshape(chip_count, 1, -1, row_count)
+    ).reshape(ch_count, 1, block_chips, -1, row_count)
     part_other = lax.dot_general(
         weight_rows_other, out_grad, dims, preferred_element_type=jnp.float32
-    ).reshape(chip_count, 1, -1, row_count)
-    partial = jnp.where(
+    ).reshape(ch_count, 1, block_chips, -1, row_count)
+    sent = jnp.concatenate([part_mine, part_other], axis=1)
+    summed = jnp.sum(lax.all_to_all(sent, CH, 0, 0, tiled=True), axis=0)
+    cols_mine, cols_other = summed[0][:, None], summed[1][:, None]
+    grad_cols = jnp.where(
         on_first,
-        jnp.concatenate([part_mine, part_other], axis=1),
-        jnp.concatenate([part_other, part_mine], axis=1),
+        jnp.concatenate([cols_mine, cols_other], axis=1),
+        jnp.concatenate([cols_other, cols_mine], axis=1),
     ).reshape(-1, row_count)
-    grad_cols = lax.psum_scatter(partial, CH, scatter_dimension=0, tiled=True)
     layer_out = out_sum.astype(jnp.bfloat16)
     grad_pre = jnp.transpose(grad_cols)
     grad_query_short = (grad_pre * mixed).astype(jnp.bfloat16)

time: 316 us -> 275 us (0.87)
  the two profiles are of different devices: /device:TPU:125 before, /device:TPU:1 now
where the time goes in v2:
time: 275 us; the launch traced here: 273 us
  blocking collectives  61.7 us (22%)
  starting transfers between devices  58.4 us (21%)
  local copies, waits for them, and re-layouts  50.2 us (18%)
  waiting for transfers between devices  48.3 us (18%)
  other arithmetic  31.9 us (12%)
  matrix products  17.2 us (6%)
  between operations  5.31 us (2%)
    all_to_all x1, blocking collectives, gather_weight(): lax.all_to_all(spread, CHIPS, 0, 0, tiled=True)  61.7 us
    ppermute x14, starting transfers between devices, shifted(): return lax.ppermute(array, axis, pairs)  34.6 us
    all_to_all x1, waiting for transfers between devices, local(): summed = jnp.sum(lax.all_to_all(sent, CH, 0, 0, tiled=True), axis=0)  23.6 us
    ppermute x14, waiting for transfers between devices, shifted(): return lax.ppermute(array, axis, pairs)  21.6 us
    unnamed x96, local copies, waits for them, and re-layouts  18.8 us
    reshape x4, local copies, waits for them, and re-layouts, toeplitz_tiles(): repeated.reshape(group_count, row_count, 2 * row_count - 1)  15.2 us
    all_to_all x1, starting transfers between devices, local(): summed = jnp.sum(lax.all_to_all(sent, CH, 0, 0, tiled=True), axis=0)  9.91 us
    dot_general x4, matrix products, apply_forward(): jnp.einsum('gst,sgc->tgc', band_tile, grouped, preferred_element_type=jnp...  8.28 us
  transfers between devices with their start and end apart: 17, of which 9 were waited for; matrix products, arithmetic and copies ran while one was open for 31% of the time, Pallas kernels for 0%

profile of v2, /device:TPU:1, one launch (start us, length us, event | category | flops | bytes accessed | tf_op | source)
XLA Modules:
  0.0 272.9 jit_solution(8821903708061084857)
XLA Ops:
  1.8 61.7 %all_to_all.15 = bf16[32,64,512]{2,1,0:T(8,128)(2,1)S(1)} all-to-all(bf16[32,64,512]{2,1,0:T(8,128)(2,1)S(1)} %broadcast_in_dim.199), channel_id=1, replica_groups=mesh['zl'=4,'y'=8,'core'=2,'zh'=2,'x'=4] {'zl','y'}, dimensions={0} | all-to-all | bytes 4194304 | tf_op jit(solution)/shard_map/all_to_all | solution.py:14
  63.4 6.2 %collective-permute-start.8 = (bf16[2048,512]{1,0:T(8,128)(2,1)S(1)}, bf16[2048,512]{1,0:T(8,128)(2,1)S(1)}, u32[]{:S(2)}, u32[]{:S(2)}) collective-permute-start(bf16[2048,512]{1,0:T(8,128)(2,1)S(1)} %bitcast.144), channel_id=1, source_target_pairs={{0,8},{8,0},{1,9},{9,1},{2,10},{10,2},{3,11},{11,3},{4,12},{12,4},... | collective-permute-start | bytes 6291464 | tf_op jit(solution)/shard_map/ppermute | solution.py:15
  70.3 3.0 %collective-permute-done.8 = bf16[2048,512]{1,0:T(8,128)(2,1)S(1)} collective-permute-done((bf16[2048,512]{1,0:T(8,128)(2,1)S(1)}, bf16[2048,512]{1,0:T(8,128)(2,1)S(1)}, u32[]{:S(2)}, u32[]{:S(2)}) %collective-permute-start.8) | collective-permute-done | bytes 2097184 | tf_op jit(solution)/shard_map/ppermute | solution.py:15
  77.5 9.9 %all-to-all-start.2 = ((f32[8,2,4,64,256]{4,3,2,1,0:T(8,128)}), f32[8,2,4,64,256]{4,3,2,1,0:T(8,128)}, u32[]{:S(2)}, u32[]{:S(2)}) async-start(f32[8,2,4,64,256]{4,3,2,1,0:T(8,128)} %copy.50), calls=%async_computation.2 | async-start | bytes 8388608 | tf_op jit(solution)/shard_map/all_to_all | solution.py:180
  88.1 2.6 collective-permute-start.4
  90.6 3.0 %collective-permute-start = (s32[2]{0:T(128)}, s32[2]{0:T(128)}, u32[]{:S(2)}, u32[]{:S(2)}) collective-permute-start(s32[2]{0:T(128)} %get-tuple-element.58), channel_id=1, source_target_pairs={{0,8},{8,16},{16,24},{24,32},{32,40},{40,48},{48,56},{56,64},{64,7... | collective-permute-start | bytes 32 | tf_op jit(solution)/shard_map/ppermute | solution.py:22
  98.1 3.0 %collective-permute-start.2 = (bf16[2,512]{0,1:T(8,128)(2,1)}, bf16[2,512]{0,1:T(8,128)(2,1)}, u32[]{:S(2)}, u32[]{:S(2)}) collective-permute-start(bf16[2,512]{0,1:T(8,128)(2,1)} %copy.45), channel_id=1, source_target_pairs={{0,8},{8,16},{16,24},{24,32},{32,40},{40,48},{48,56},{56,64},{64,7... | collective-permute-start | bytes 6152 | tf_op jit(solution)/shard_map/ppermute | solution.py:22
  115.1 3.2 %select_select_fusion.1 = (bf16[256,512]{0,1:T(8,128)(2,1)}, bf16[256,512]{0,1:T(8,128)(2,1)}) fusion(pred[256]{0:T(512)(128)(4,1)} %get-tuple-element.47, pred[]{:T(512)S(6)} %eq.69, bf16[256,512]{0,1:T(8,128)(2,1)} %copy.47, bf16[2,512]{0,1:T(8,128)(2,1)S(1)} %collective-permute-done.3, f32[512]{0:T(512)} %bitcast.176, f32[512]{0:T(512)} %bitcast.178, ...), kind=kLoop, calls=%fused_computation.94 | loop fusion | flops 4718592 | bytes 1065729 | tf_op jit(solution)/shard_map/jit(_where)/select_n | solution.py:143
  118.3 2.7 collective-permute-start.5
  125.2 3.0 %reshape.177 = bf16[4,256,511]{2,1,0:T(8,128)(2,1)S(1)} reshape(bf16[4,130816]{1,0:T(4,128)(2,1)} %slice.300) | data formatting | bytes 2093056 | tf_op jit(solution)/shard_map/reshape | solution.py:48
  132.0 4.1 %reshape.175 = bf16[4,256,511]{2,1,0:T(8,128)(2,1)} reshape(bf16[4,130816]{1,0:T(4,128)(2,1)} %slice.298) | data formatting | bytes 2093056 | tf_op jit(solution)/shard_map/reshape | solution.py:48
  139.5 4.0 %reshape.173 = bf16[4,256,511]{2,1,0:T(8,128)(2,1)} reshape(bf16[4,130816]{1,0:T(4,128)(2,1)} %slice.296) | data formatting | bytes 2093056 | tf_op jit(solution)/shard_map/reshape | solution.py:48
  146.9 4.0 %reshape.170 = bf16[4,256,511]{2,1,0:T(8,128)(2,1)} reshape(bf16[4,130816]{1,0:T(4,128)(2,1)} %slice.294) | data formatting | bytes 2093056 | tf_op jit(solution)/shard_map/reshape | solution.py:48
  158.3 2.6 broadcast_select_fusion.7
  161.0 3.6 %collective-permute-start.7 = (bf16[256,512]{0,1:T(8,128)(2,1)S(1)}, bf16[256,512]{0,1:T(8,128)(2,1)S(1)}, u32[]{:S(2)}, u32[]{:S(2)}) collective-permute-start(bf16[256,512]{0,1:T(8,128)(2,1)S(1)} %broadcast_select_fusion.10), channel_id=1, source_target_pairs={{0,8},{8,16},{16,24},{24,32},{32,40},{40,48},{48,56},{56,64},{64,7... | collective-permute-start | bytes 786440 | tf_op jit(solution)/shard_map/ppermute | solution.py:22
  170.1 23.6 %all-to-all-done.2 = f32[8,2,4,64,256]{4,3,2,1,0:T(8,128)} async-done(((f32[8,2,4,64,256]{4,3,2,1,0:T(8,128)}), f32[8,2,4,64,256]{4,3,2,1,0:T(8,128)}, u32[]{:S(2)}, u32[]{:S(2)}) %all-to-all-start.2) | async-done | bytes 4194336 | tf_op jit(solution)/shard_map/all_to_all | solution.py:180
  200.6 3.5 %collective-permute-start.9 = (bf16[2,512]{0,1:T(8,128)(2,1)}, bf16[2,512]{0,1:T(8,128)(2,1)}, u32[]{:S(2)}, u32[]{:S(2)}) collective-permute-start(bf16[2,512]{0,1:T(8,128)(2,1)} %slice.306), channel_id=1, source_target_pairs={{8,0},{16,8},{24,16},{32,24},{40,32},{48,40},{56,48},{64,56},{72,6... | collective-permute-start | bytes 6152 | tf_op jit(solution)/shard_map/ppermute | solution.py:22
  207.1 2.7 %add_convert_fusion.2 = (bf16[256,512]{0,1:T(8,128)(2,1)}, bf16[256,512]{0,1:T(8,128)(2,1)S(1)}) fusion(bf16[256,512]{0,1:T(8,128)(2,1)S(1)} %get-tuple-element.16, bf16[2,512]{0,1:T(8,128)(2,1)} %collective-permute-done.9, f32[512]{0:T(512)} %bitcast.170, f32[512]{0:T(512)} %bitcast.172, f32[512]{0:T(512)} %bitcast.168, ...), kind=kLoop, calls=%fused_computation.30 | loop fusion | flops 4587520 | bytes 1584128 | tf_op jit(solution)/shard_map/convert_element_type | solution.py:209
  211.4 7.7 %all-to-all-start = ((bf16[8,256,512]{1,2,0:T(8,128)(2,1)}), bf16[8,256,512]{1,2,0:T(8,128)(2,1)}, u32[]{:S(2)}, u32[]{:S(2)}) async-start(bf16[8,256,512]{1,2,0:T(8,128)(2,1)} %broadcast_in_dim.198), calls=%async_computation | async-start | bytes 4194304 | tf_op jit(solution)/shard_map/all_to_all | solution.py:157
  226.9 4.8 %collective-permute-done.10 = bf16[256,512]{0,1:T(8,128)(2,1)} collective-permute-done((bf16[256,512]{0,1:T(8,128)(2,1)}, bf16[256,512]{0,1:T(8,128)(2,1)}, u32[]{:S(2)}, u32[]{:S(2)}) %collective-permute-start.10) | collective-permute-done | bytes 262176 | tf_op jit(solution)/shard_map/ppermute | solution.py:22
  238.5 2.5 collective-permute-done.11
  244.6 4.5 %collective-permute-done.12 = bf16[256,512]{0,1:T(8,128)(2,1)S(1)} collective-permute-done((bf16[256,512]{0,1:T(8,128)(2,1)S(1)}, bf16[256,512]{0,1:T(8,128)(2,1)S(1)}, u32[]{:S(2)}, u32[]{:S(2)}) %collective-permute-start.12) | collective-permute-done | bytes 262176 | tf_op jit(solution)/shard_map/ppermute | solution.py:22
  254.6 4.4 %collective-permute-done.14 = bf16[2,512]{0,1:T(8,128)(2,1)S(1)} collective-permute-done((bf16[2,512]{0,1:T(8,128)(2,1)S(1)}, bf16[2,512]{0,1:T(8,128)(2,1)S(1)}, u32[]{:S(2)}, u32[]{:S(2)}) %collective-permute-start.14) | collective-permute-done | bytes 2080 | tf_op jit(solution)/shard_map/ppermute | solution.py:22
  263.5 2.7 collective-permute-done.13
  (178 shorter events, 94.5 us)
Async XLA Ops:
  0.6 69.0 %copy-start = (bf16[256,512]{1,0:T(8,128)(2,1)S(1)}, bf16[256,512]{1,0:T(8,128)(2,1)}, u32[]{:S(2)}) copy-start(bf16[256,512]{1,0:T(8,128)(2,1)} %param.17) | copy-start | bytes 786436
  63.4 9.9 %collective-permute-start.8 = (bf16[2048,512]{1,0:T(8,128)(2,1)S(1)}, bf16[2048,512]{1,0:T(8,128)(2,1)S(1)}, u32[]{:S(2)}, u32[]{:S(2)}) collective-permute-start(bf16[2048,512]{1,0:T(8,128)(2,1)S(1)} %bitcast.144), channel_id=1, source_target_pairs={{0,8},{8,0},{1,9},{9,1},{2,10},{10,2},{3,11},{11,3},{4,12},{12,4},... | collective-permute-start | bytes 6291464 | tf_op jit(solution)/shard_map/ppermute | solution.py:15
  77.5 19.7 %copy-start.17 = (bf16[256,512]{1,0:T(8,128)(2,1)S(1)}, bf16[256,512]{1,0:T(8,128)(2,1)}, u32[]{:S(2)}) copy-start(bf16[256,512]{1,0:T(8,128)(2,1)} %param.10) | copy-start | bytes 786436
  77.5 23.6 %copy-start.18 = (bf16[256,512]{1,0:T(8,128)(2,1)S(1)}, bf16[256,512]{1,0:T(8,128)(2,1)}, u32[]{:S(2)}) copy-start(bf16[256,512]{1,0:T(8,128)(2,1)} %param.11) | copy-start | bytes 786436
  77.5 28.8 %copy-start.20 = (bf16[4,768]{1,0:T(4,128)(2,1)S(1)}, bf16[4,768]{1,0:T(4,128)(2,1)}, u32[]{:S(2)}) copy-start(bf16[4,768]{1,0:T(4,128)(2,1)} %param.13) | copy-start | bytes 18436
  77.5 28.9 %copy-start.30 = (f32[3,3,512]{2,1,0:T(4,128)S(1)}, f32[3,3,512]{2,1,0:T(4,128)}, u32[]{:S(2)}) copy-start(f32[3,3,512]{2,1,0:T(4,128)} %param.12) | copy-start | bytes 55300
  77.5 116.2 %all-to-all-start.2 = ((f32[8,2,4,64,256]{4,3,2,1,0:T(8,128)}), f32[8,2,4,64,256]{4,3,2,1,0:T(8,128)}, u32[]{:S(2)}, u32[]{:S(2)}) async-start(f32[8,2,4,64,256]{4,3,2,1,0:T(8,128)} %copy.50), calls=%async_computation.2 | async-start | bytes 8388608 | tf_op jit(solution)/shard_map/all_to_all | solution.py:180
  88.1 22.3 %collective-permute-start.4 = (s32[2]{0:T(128)}, s32[2]{0:T(128)}, u32[]{:S(2)}, u32[]{:S(2)}) collective-permute-start(s32[2]{0:T(128)} %get-tuple-element.59), channel_id=1, source_target_pairs={{8,0},{16,8},{24,16},{32,24},{40,32},{48,40},{56,48},{64,56},{72,6... | collective-permute-start | bytes 32 | tf_op jit(solution)/shard_map/ppermute | solution.py:22
  90.6 20.4 %collective-permute-start = (s32[2]{0:T(128)}, s32[2]{0:T(128)}, u32[]{:S(2)}, u32[]{:S(2)}) collective-permute-start(s32[2]{0:T(128)} %get-tuple-element.58), channel_id=1, source_target_pairs={{0,8},{8,16},{16,24},{24,32},{32,40},{40,48},{48,56},{56,64},{64,7... | collective-permute-start | bytes 32 | tf_op jit(solution)/shard_map/ppermute | solution.py:22
  95.1 110.0 %collective-permute-start.1 = (bf16[2,512]{0,1:T(8,128)(2,1)}, bf16[2,512]{0,1:T(8,128)(2,1)}, u32[]{:S(2)}, u32[]{:S(2)}) collective-permute-start(bf16[2,512]{0,1:T(8,128)(2,1)} %copy.42), channel_id=1, source_target_pairs={{0,8},{8,16},{16,24},{24,32},{32,40},{40,48},{48,56},{56,64},{64,7... | collective-permute-start | bytes 6152 | tf_op jit(solution)/shard_map/ppermute | solution.py:22
  98.1 17.0 %collective-permute-start.2 = (bf16[2,512]{0,1:T(8,128)(2,1)}, bf16[2,512]{0,1:T(8,128)(2,1)}, u32[]{:S(2)}, u32[]{:S(2)}) collective-permute-start(bf16[2,512]{0,1:T(8,128)(2,1)} %copy.45), channel_id=1, source_target_pairs={{0,8},{8,16},{16,24},{24,32},{32,40},{40,48},{48,56},{56,64},{64,7... | collective-permute-start | bytes 6152 | tf_op jit(solution)/shard_map/ppermute | solution.py:22
  101.9 13.2 %collective-permute-start.3 = (bf16[2,512]{0,1:T(8,128)(2,1)}, bf16[2,512]{0,1:T(8,128)(2,1)S(1)}, u32[]{:S(2)}, u32[]{:S(2)}) collective-permute-start(bf16[2,512]{0,1:T(8,128)(2,1)} %copy.48), channel_id=1, source_target_pairs={{0,8},{8,16},{16,24},{24,32},{32,40},{40,48},{48,56},{56,64},{64,7... | collective-permute-start | bytes 6152 | tf_op jit(solution)/shard_map/ppermute | solution.py:22
  118.3 35.0 %collective-permute-start.5 = (bf16[256,512]{0,1:T(8,128)(2,1)}, bf16[256,512]{0,1:T(8,128)(2,1)}, u32[]{:S(2)}, u32[]{:S(2)}) collective-permute-start(bf16[256,512]{0,1:T(8,128)(2,1)} %get-tuple-element.18), channel_id=1, source_target_pairs={{0,8},{8,16},{16,24},{24,32},{32,40},{40,48},{48,56},{56,64},{64,7... | collective-permute-start | bytes 786440 | tf_op jit(solution)/shard_map/ppermute | solution.py:22
  128.2 40.1 %copy-start.3 = (bf16[4,256,511]{2,1,0:T(8,128)(2,1)}, bf16[4,256,511]{2,1,0:T(8,128)(2,1)S(1)}, u32[]{:S(2)}) copy-start(bf16[4,256,511]{2,1,0:T(8,128)(2,1)S(1)} %reshape.177) | copy-start | bytes 3139588
  154.3 6.7 %collective-permute-start.6 = (bf16[256,512]{0,1:T(8,128)(2,1)S(1)}, bf16[256,512]{0,1:T(8,128)(2,1)S(1)}, u32[]{:S(2)}, u32[]{:S(2)}) collective-permute-start(bf16[256,512]{0,1:T(8,128)(2,1)S(1)} %broadcast_select_fusion.11), channel_id=1, source_target_pairs={{0,8},{8,16},{16,24},{24,32},{32,40},{40,48},{48,56},{56,64},{64,7... | collective-permute-start | bytes 786440 | tf_op jit(solution)/shard_map/ppermute | solution.py:22
  161.0 6.7 %collective-permute-start.7 = (bf16[256,512]{0,1:T(8,128)(2,1)S(1)}, bf16[256,512]{0,1:T(8,128)(2,1)S(1)}, u32[]{:S(2)}, u32[]{:S(2)}) collective-permute-start(bf16[256,512]{0,1:T(8,128)(2,1)S(1)} %broadcast_select_fusion.10), channel_id=1, source_target_pairs={{0,8},{8,16},{16,24},{24,32},{32,40},{40,48},{48,56},{56,64},{64,7... | collective-permute-start | bytes 786440 | tf_op jit(solution)/shard_map/ppermute | solution.py:22
  200.6 6.6 %collective-permute-start.9 = (bf16[2,512]{0,1:T(8,128)(2,1)}, bf16[2,512]{0,1:T(8,128)(2,1)}, u32[]{:S(2)}, u32[]{:S(2)}) collective-permute-start(bf16[2,512]{0,1:T(8,128)(2,1)} %slice.306), channel_id=1, source_target_pairs={{8,0},{16,8},{24,16},{32,24},{40,32},{48,40},{56,48},{64,56},{72,6... | collective-permute-start | bytes 6152 | tf_op jit(solution)/shard_map/ppermute | solution.py:22
  211.4 56.8 %all-to-all-start = ((bf16[8,256,512]{1,2,0:T(8,128)(2,1)}), bf16[8,256,512]{1,2,0:T(8,128)(2,1)}, u32[]{:S(2)}, u32[]{:S(2)}) async-start(bf16[8,256,512]{1,2,0:T(8,128)(2,1)} %broadcast_in_dim.198), calls=%async_computation | async-start | bytes 4194304 | tf_op jit(solution)/shard_map/all_to_all | solution.py:157
  223.4 8.4 %collective-permute-start.10 = (bf16[256,512]{0,1:T(8,128)(2,1)}, bf16[256,512]{0,1:T(8,128)(2,1)}, u32[]{:S(2)}, u32[]{:S(2)}) collective-permute-start(bf16[256,512]{0,1:T(8,128)(2,1)} %get-tuple-element.14), channel_id=1, source_target_pairs={{8,0},{16,8},{24,16},{32,24},{40,32},{48,40},{56,48},{64,56},{72,6... | collective-permute-start | bytes 786440 | tf_op jit(solution)/shard_map/ppermute | solution.py:22
  225.4 18.2 %copy-start.6 = (bf16[4,256,511]{2,1,0:T(8,128)(2,1)S(1)}, bf16[4,256,511]{2,1,0:T(8,128)(2,1)}, u32[]{:S(2)}) copy-start(bf16[4,256,511]{2,1,0:T(8,128)(2,1)} %reshape.175) | copy-start | bytes 3139588
  232.8 8.2 %collective-permute-start.11 = (bf16[256,512]{0,1:T(8,128)(2,1)S(1)}, bf16[256,512]{0,1:T(8,128)(2,1)S(1)}, u32[]{:S(2)}, u32[]{:S(2)}) collective-permute-start(bf16[256,512]{0,1:T(8,128)(2,1)S(1)} %broadcast_select_fusion.9), channel_id=1, source_target_pairs={{8,0},{16,8},{24,16},{32,24},{40,32},{48,40},{56,48},{64,56},{72,6... | collective-permute-start | bytes 786440 | tf_op jit(solution)/shard_map/ppermute | solution.py:22
  241.0 8.1 %collective-permute-start.12 = (bf16[256,512]{0,1:T(8,128)(2,1)S(1)}, bf16[256,512]{0,1:T(8,128)(2,1)S(1)}, u32[]{:S(2)}, u32[]{:S(2)}) collective-permute-start(bf16[256,512]{0,1:T(8,128)(2,1)S(1)} %broadcast_select_fusion.8), channel_id=1, source_target_pairs={{8,0},{16,8},{24,16},{32,24},{40,32},{48,40},{56,48},{64,56},{72,6... | collective-permute-start | bytes 786440 | tf_op jit(solution)/shard_map/ppermute | solution.py:22
  252.7 6.3 %collective-permute-start.14 = (bf16[2,512]{0,1:T(8,128)(2,1)S(1)}, bf16[2,512]{0,1:T(8,128)(2,1)S(1)}, u32[]{:S(2)}, u32[]{:S(2)}) collective-permute-start(bf16[2,512]{0,1:T(8,128)(2,1)S(1)} %slice.312), channel_id=1, source_target_pairs={{8,0},{16,8},{24,16},{32,24},{40,32},{48,40},{56,48},{64,56},{72,6... | collective-permute-start | bytes 6152 | tf_op jit(solution)/shard_map/ppermute | solution.py:22
  259.9 6.3 %collective-permute-start.13 = (bf16[2,512]{0,1:T(8,128)(2,1)S(1)}, bf16[2,512]{0,1:T(8,128)(2,1)S(1)}, u32[]{:S(2)}, u32[]{:S(2)}) collective-permute-start(bf16[2,512]{0,1:T(8,128)(2,1)S(1)} %slice.309), channel_id=1, source_target_pairs={{8,0},{16,8},{24,16},{32,24},{40,32},{48,40},{56,48},{64,56},{72,6... | collective-permute-start | bytes 6152 | tf_op jit(solution)/shard_map/ppermute | solution.py:22
  (34 other events, 264.2 us)

commit v3 on v2

--- a/solution.py
+++ b/solution.py
@@ -176,8 +176,9 @@
     part_other = lax.dot_general(
         weight_rows_other, out_grad, dims, preferred_element_type=jnp.float32
     ).reshape(ch_count, 1, block_chips, -1, row_count)
-    sent = jnp.concatenate([part_mine, part_other], axis=1)
-    summed = jnp.sum(lax.all_to_all(sent, CH, 0, 0, tiled=True), axis=0)
+    sent = jnp.concatenate([part_mine, part_other], axis=1).astype(jnp.bfloat16)
+    received = lax.all_to_all(sent, CH, 0, 0, tiled=True)
+    summed = jnp.sum(received.astype(jnp.float32), axis=0)
     cols_mine, cols_other = summed[0][:, None], summed[1][:, None]
     grad_cols = jnp.where(
         on_first,

time: 275 us -> 265 us (0.964)
  the two profiles are of different devices: /device:TPU:1 before, /device:TPU:127 now
where the time goes in v3:
time: 265 us; the launch traced here: 263 us
  starting transfers between devices  61 us (23%)
  blocking collectives  58.5 us (22%)
  local copies, waits for them, and re-layouts  52.2 us (20%)
  waiting for transfers between devices  41.7 us (16%)
  other arithmetic  24.3 us (9%)
  matrix products  20.4 us (8%)
  between operations  5.27 us (2%)
    all_to_all x1, blocking collectives, gather_weight(): lax.all_to_all(spread, CHIPS, 0, 0, tiled=True)  58.5 us
    ppermute x14, waiting for transfers between devices, shifted(): return lax.ppermute(array, axis, pairs)  41.7 us
    ppermute x14, starting transfers between devices, shifted(): return lax.ppermute(array, axis, pairs)  38 us
    unnamed x108, local copies, waits for them, and re-layouts  21 us
    reshape x4, local copies, waits for them, and re-layouts, toeplitz_tiles(): repeated.reshape(group_count, row_count, 2 * row_count - 1)  15.2 us
    all_to_all x1, starting transfers between devices, local(): received = lax.all_to_all(sent, CH, 0, 0, tiled=True)  9.96 us
    all_to_all x1, starting transfers between devices, local(): lax.all_to_all(spread, CH, 0, 0, tiled=True)  9.06 us
    dot_general x4, matrix products, apply_forward(): jnp.einsum('gst,sgc->tgc', band_tile, grouped, preferred_element_type=jnp...  8.35 us
  transfers between devices with their start and end apart: 17, of which 7 were waited for; matrix products, arithmetic and copies ran while one was open for 32% of the time, Pallas kernels for 0%

profile of v3, /device:TPU:127, one launch (start us, length us, event | category | flops | bytes accessed | tf_op | source)
XLA Modules:
  0.0 263.4 jit_solution(1883507808977729717)
XLA Ops:
  1.8 58.5 %all_to_all.15 = bf16[32,64,512]{2,1,0:T(8,128)(2,1)S(1)} all-to-all(bf16[32,64,512]{2,1,0:T(8,128)(2,1)S(1)} %broadcast_in_dim.199), channel_id=1, replica_groups=mesh['zl'=4,'y'=8,'core'=2,'zh'=2,'x'=4] {'zl','y'}, dimensions={0} | all-to-all | bytes 4194304 | tf_op jit(solution)/shard_map/all_to_all | solution.py:14
  60.3 4.0 %collective-permute-start.8 = (bf16[2048,512]{1,0:T(8,128)(2,1)S(1)}, bf16[2048,512]{1,0:T(8,128)(2,1)}, u32[]{:S(2)}, u32[]{:S(2)}) collective-permute-start(bf16[2048,512]{1,0:T(8,128)(2,1)S(1)} %bitcast.143), channel_id=1, source_target_pairs={{0,8},{8,0},{1,9},{9,1},{2,10},{10,2},{3,11},{11,3},{4,12},{12,4},... | collective-permute-start | bytes 6291464 | tf_op jit(solution)/shard_map/ppermute | solution.py:15
  66.8 5.8 %collective-permute-start = (s32[2]{0:T(128)}, s32[2]{0:T(128)}, u32[]{:S(2)}, u32[]{:S(2)}) collective-permute-start(s32[2]{0:T(128)} %get-tuple-element.58), channel_id=1, source_target_pairs={{0,8},{8,16},{16,24},{24,32},{32,40},{40,48},{48,56},{56,64},{64,7... | collective-permute-start | bytes 32 | tf_op jit(solution)/shard_map/ppermute | solution.py:22
  84.7 2.4 collective-permute-start.3
  87.1 2.3 convolution_convert_fusion
  91.1 10.0 %all-to-all-start.2 = ((bf16[8,2,4,64,256]{4,3,2,1,0:T(8,128)(2,1)}), bf16[8,2,4,64,256]{4,3,2,1,0:T(8,128)(2,1)S(1)}, u32[]{:S(2)}, u32[]{:S(2)}) async-start(bf16[8,2,4,64,256]{4,3,2,1,0:T(8,128)(2,1)} %copy.50), calls=%async_computation.2 | async-start | bytes 4194304 | tf_op jit(solution)/shard_map/all_to_all | solution.py:180
  113.3 3.2 %select_select_fusion.1 = (bf16[256,512]{0,1:T(8,128)(2,1)}, bf16[256,512]{0,1:T(8,128)(2,1)}) fusion(pred[256]{0:T(512)(128)(4,1)} %get-tuple-element.47, pred[]{:T(512)S(6)} %eq.69, bf16[256,512]{0,1:T(8,128)(2,1)} %copy.47, bf16[2,512]{0,1:T(8,128)(2,1)S(1)} %collective-permute-done.3, f32[512]{0:T(512)} %bitcast.177, f32[512]{0:T(512)} %bitcast.179, ...), kind=kLoop, calls=%fused_computation.97 | loop fusion | flops 4718592 | bytes 1065729 | tf_op jit(solution)/shard_map/jit(_where)/select_n | solution.py:143
  116.6 4.4 %collective-permute-start.5 = (bf16[256,512]{0,1:T(8,128)(2,1)}, bf16[256,512]{0,1:T(8,128)(2,1)}, u32[]{:S(2)}, u32[]{:S(2)}) collective-permute-start(bf16[256,512]{0,1:T(8,128)(2,1)} %get-tuple-element.18), channel_id=1, source_target_pairs={{0,8},{8,16},{16,24},{24,32},{32,40},{40,48},{48,56},{56,64},{64,7... | collective-permute-start | bytes 786440 | tf_op jit(solution)/shard_map/ppermute | solution.py:22
  125.1 3.0 %reshape.179 = bf16[4,256,511]{2,1,0:T(8,128)(2,1)S(1)} reshape(bf16[4,130816]{1,0:T(4,128)(2,1)} %slice.300) | data formatting | bytes 2093056 | tf_op jit(solution)/shard_map/reshape | solution.py:48
  128.2 2.4 copy.57
  131.9 4.1 %reshape.177 = bf16[4,256,511]{2,1,0:T(8,128)(2,1)} reshape(bf16[4,130816]{1,0:T(4,128)(2,1)} %slice.298) | data formatting | bytes 2093056 | tf_op jit(solution)/shard_map/reshape | solution.py:48
  139.4 4.0 %reshape.175 = bf16[4,256,511]{2,1,0:T(8,128)(2,1)} reshape(bf16[4,130816]{1,0:T(4,128)(2,1)} %slice.296) | data formatting | bytes 2093056 | tf_op jit(solution)/shard_map/reshape | solution.py:48
  146.8 4.0 %reshape.172 = bf16[4,256,511]{2,1,0:T(8,128)(2,1)} reshape(bf16[4,130816]{1,0:T(4,128)(2,1)} %slice.294) | data formatting | bytes 2093056 | tf_op jit(solution)/shard_map/reshape | solution.py:48
  156.8 2.6 broadcast_select_fusion.7
  159.4 5.7 %collective-permute-start.7 = (bf16[256,512]{0,1:T(8,128)(2,1)S(1)}, bf16[256,512]{0,1:T(8,128)(2,1)S(1)}, u32[]{:S(2)}, u32[]{:S(2)}) collective-permute-start(bf16[256,512]{0,1:T(8,128)(2,1)S(1)} %broadcast_select_fusion.10), channel_id=1, source_target_pairs={{0,8},{8,16},{16,24},{24,32},{32,40},{40,48},{48,56},{56,64},{64,7... | collective-permute-start | bytes 786440 | tf_op jit(solution)/shard_map/ppermute | solution.py:22
  174.7 7.1 %collective-permute-done.9 = bf16[2,512]{0,1:T(8,128)(2,1)S(1)} collective-permute-done((bf16[2,512]{0,1:T(8,128)(2,1)S(1)}, bf16[2,512]{0,1:T(8,128)(2,1)S(1)}, u32[]{:S(2)}, u32[]{:S(2)}) %collective-permute-start.9) | collective-permute-done | bytes 2080 | tf_op jit(solution)/shard_map/ppermute | solution.py:22
  181.8 2.5 add_convert_fusion.2
  185.8 9.1 %all-to-all-start = ((bf16[8,256,512]{1,2,0:T(8,128)(2,1)}), bf16[8,256,512]{1,2,0:T(8,128)(2,1)S(1)}, u32[]{:S(2)}, u32[]{:S(2)}) async-start(bf16[8,256,512]{1,2,0:T(8,128)(2,1)} %broadcast_in_dim.198), calls=%async_computation | async-start | bytes 4194304 | tf_op jit(solution)/shard_map/all_to_all | solution.py:157
  202.7 7.0 %collective-permute-done.10 = bf16[256,512]{0,1:T(8,128)(2,1)} collective-permute-done((bf16[256,512]{0,1:T(8,128)(2,1)}, bf16[256,512]{0,1:T(8,128)(2,1)}, u32[]{:S(2)}, u32[]{:S(2)}) %collective-permute-start.10) | collective-permute-done | bytes 262176 | tf_op jit(solution)/shard_map/ppermute | solution.py:22
  215.4 6.0 %collective-permute-done.11 = bf16[256,512]{0,1:T(8,128)(2,1)S(1)} collective-permute-done((bf16[256,512]{0,1:T(8,128)(2,1)S(1)}, bf16[256,512]{0,1:T(8,128)(2,1)S(1)}, u32[]{:S(2)}, u32[]{:S(2)}) %collective-permute-start.11) | collective-permute-done | bytes 262176 | tf_op jit(solution)/shard_map/ppermute | solution.py:22
  225.0 8.7 %collective-permute-done.12 = bf16[256,512]{0,1:T(8,128)(2,1)S(1)} collective-permute-done((bf16[256,512]{0,1:T(8,128)(2,1)S(1)}, bf16[256,512]{0,1:T(8,128)(2,1)S(1)}, u32[]{:S(2)}, u32[]{:S(2)}) %collective-permute-start.12) | collective-permute-done | bytes 262176 | tf_op jit(solution)/shard_map/ppermute | solution.py:22
  239.2 7.5 %collective-permute-done.14 = bf16[2,512]{0,1:T(8,128)(2,1)S(1)} collective-permute-done((bf16[2,512]{0,1:T(8,128)(2,1)S(1)}, bf16[2,512]{0,1:T(8,128)(2,1)S(1)}, u32[]{:S(2)}, u32[]{:S(2)}) %collective-permute-start.14) | collective-permute-done | bytes 2080 | tf_op jit(solution)/shard_map/ppermute | solution.py:22
  251.2 4.8 %collective-permute-done.13 = bf16[2,512]{0,1:T(8,128)(2,1)S(1)} collective-permute-done((bf16[2,512]{0,1:T(8,128)(2,1)S(1)}, bf16[2,512]{0,1:T(8,128)(2,1)S(1)}, u32[]{:S(2)}, u32[]{:S(2)}) %collective-permute-start.13) | collective-permute-done | bytes 2080 | tf_op jit(solution)/shard_map/ppermute | solution.py:22
  260.4 3.0 %fusion.1 = bf16[256,512]{1,0:T(8,128)(2,1)} fusion(f32[256,512]{1,0:T(8,128)S(1)} %fusion.42, bf16[256,2048]{0,1:T(8,128)(2,1)S(1)} %bitcast.154, bf16[2048,512]{1,0:T(8,128)(2,1)} %collective-permute-done.8), kind=kOutput, calls=%fused_computation.6 | convolution fusion | flops 537133056 | bytes 3932160 | tf_op jit(solution)/shard_map/dot_general | solution.py:168
  (190 shorter events, 86.0 us)
Async XLA Ops:
  0.6 83.3 %copy-start = (bf16[256,512]{1,0:T(8,128)(2,1)S(1)}, bf16[256,512]{1,0:T(8,128)(2,1)}, u32[]{:S(2)}) copy-start(bf16[256,512]{1,0:T(8,128)(2,1)} %param.17) | copy-start | bytes 786436
  1.8 62.5 %copy-start.19 = (s32[256]{0:T(256)S(1)}, s32[256]{0:T(256)}, u32[]{:S(2)}) copy-start(s32[256]{0:T(256)} %param.16) | copy-start | bytes 3076
  1.8 79.5 %copy-start.20 = (bf16[4,768]{1,0:T(4,128)(2,1)S(1)}, bf16[4,768]{1,0:T(4,128)(2,1)}, u32[]{:S(2)}) copy-start(bf16[4,768]{1,0:T(4,128)(2,1)} %param.13) | copy-start | bytes 18436
  1.8 80.3 %copy-start.34 = (f32[3,3,512]{2,1,0:T(4,128)S(1)}, f32[3,3,512]{2,1,0:T(4,128)}, u32[]{:S(2)}) copy-start(f32[3,3,512]{2,1,0:T(4,128)} %param.12) | copy-start | bytes 55300
  60.3 24.4 %copy-start.1 = (bf16[32,64,512]{2,1,0:T(8,128)(2,1)}, bf16[32,64,512]{2,1,0:T(8,128)(2,1)S(1)}, u32[]{:S(2)}) copy-start(bf16[32,64,512]{2,1,0:T(8,128)(2,1)S(1)} %all_to_all.15) | copy-start | bytes 6291460
  60.3 24.4 %collective-permute-start.8 = (bf16[2048,512]{1,0:T(8,128)(2,1)S(1)}, bf16[2048,512]{1,0:T(8,128)(2,1)}, u32[]{:S(2)}, u32[]{:S(2)}) collective-permute-start(bf16[2048,512]{1,0:T(8,128)(2,1)S(1)} %bitcast.143), channel_id=1, source_target_pairs={{0,8},{8,0},{1,9},{9,1},{2,10},{10,2},{3,11},{11,3},{4,12},{12,4},... | collective-permute-start | bytes 6291464 | tf_op jit(solution)/shard_map/ppermute | solution.py:15
  64.8 43.9 %collective-permute-start.4 = (s32[2]{0:T(128)}, s32[2]{0:T(128)}, u32[]{:S(2)}, u32[]{:S(2)}) collective-permute-start(s32[2]{0:T(128)} %get-tuple-element.59), channel_id=1, source_target_pairs={{8,0},{16,8},{24,16},{32,24},{40,32},{48,40},{56,48},{64,56},{72,6... | collective-permute-start | bytes 32 | tf_op jit(solution)/shard_map/ppermute | solution.py:22
  66.8 42.6 %collective-permute-start = (s32[2]{0:T(128)}, s32[2]{0:T(128)}, u32[]{:S(2)}, u32[]{:S(2)}) collective-permute-start(s32[2]{0:T(128)} %get-tuple-element.58), channel_id=1, source_target_pairs={{0,8},{8,16},{16,24},{24,32},{32,40},{40,48},{48,56},{56,64},{64,7... | collective-permute-start | bytes 32 | tf_op jit(solution)/shard_map/ppermute | solution.py:22
  74.0 100.7 %collective-permute-start.1 = (bf16[2,512]{0,1:T(8,128)(2,1)}, bf16[2,512]{0,1:T(8,128)(2,1)}, u32[]{:S(2)}, u32[]{:S(2)}) collective-permute-start(bf16[2,512]{0,1:T(8,128)(2,1)} %copy.42), channel_id=1, source_target_pairs={{0,8},{8,16},{16,24},{24,32},{32,40},{40,48},{48,56},{56,64},{64,7... | collective-permute-start | bytes 6152 | tf_op jit(solution)/shard_map/ppermute | solution.py:22
  77.5 35.8 %collective-permute-start.2 = (bf16[2,512]{0,1:T(8,128)(2,1)}, bf16[2,512]{0,1:T(8,128)(2,1)}, u32[]{:S(2)}, u32[]{:S(2)}) collective-permute-start(bf16[2,512]{0,1:T(8,128)(2,1)} %copy.45), channel_id=1, source_target_pairs={{0,8},{8,16},{16,24},{24,32},{32,40},{40,48},{48,56},{56,64},{64,7... | collective-permute-start | bytes 6152 | tf_op jit(solution)/shard_map/ppermute | solution.py:22
  84.7 28.7 %collective-permute-start.3 = (bf16[2,512]{0,1:T(8,128)(2,1)}, bf16[2,512]{0,1:T(8,128)(2,1)S(1)}, u32[]{:S(2)}, u32[]{:S(2)}) collective-permute-start(bf16[2,512]{0,1:T(8,128)(2,1)} %copy.48), channel_id=1, source_target_pairs={{0,8},{8,16},{16,24},{24,32},{32,40},{40,48},{48,56},{56,64},{64,7... | collective-permute-start | bytes 6152 | tf_op jit(solution)/shard_map/ppermute | solution.py:22
  91.1 79.5 %all-to-all-start.2 = ((bf16[8,2,4,64,256]{4,3,2,1,0:T(8,128)(2,1)}), bf16[8,2,4,64,256]{4,3,2,1,0:T(8,128)(2,1)S(1)}, u32[]{:S(2)}, u32[]{:S(2)}) async-start(bf16[8,2,4,64,256]{4,3,2,1,0:T(8,128)(2,1)} %copy.50), calls=%async_computation.2 | async-start | bytes 4194304 | tf_op jit(solution)/shard_map/all_to_all | solution.py:180
  116.6 36.6 %collective-permute-start.5 = (bf16[256,512]{0,1:T(8,128)(2,1)}, bf16[256,512]{0,1:T(8,128)(2,1)}, u32[]{:S(2)}, u32[]{:S(2)}) collective-permute-start(bf16[256,512]{0,1:T(8,128)(2,1)} %get-tuple-element.18), channel_id=1, source_target_pairs={{0,8},{8,16},{16,24},{24,32},{32,40},{40,48},{48,56},{56,64},{64,7... | collective-permute-start | bytes 786440 | tf_op jit(solution)/shard_map/ppermute | solution.py:22
  128.2 40.8 %copy-start.3 = (bf16[4,256,511]{2,1,0:T(8,128)(2,1)}, bf16[4,256,511]{2,1,0:T(8,128)(2,1)S(1)}, u32[]{:S(2)}) copy-start(bf16[4,256,511]{2,1,0:T(8,128)(2,1)S(1)} %reshape.179) | copy-start | bytes 3139588
  153.2 6.2 %collective-permute-start.6 = (bf16[256,512]{0,1:T(8,128)(2,1)S(1)}, bf16[256,512]{0,1:T(8,128)(2,1)S(1)}, u32[]{:S(2)}, u32[]{:S(2)}) collective-permute-start(bf16[256,512]{0,1:T(8,128)(2,1)S(1)} %broadcast_select_fusion.11), channel_id=1, source_target_pairs={{0,8},{8,16},{16,24},{24,32},{32,40},{40,48},{48,56},{56,64},{64,7... | collective-permute-start | bytes 786440 | tf_op jit(solution)/shard_map/ppermute | solution.py:22
  159.4 8.8 %collective-permute-start.7 = (bf16[256,512]{0,1:T(8,128)(2,1)S(1)}, bf16[256,512]{0,1:T(8,128)(2,1)S(1)}, u32[]{:S(2)}, u32[]{:S(2)}) collective-permute-start(bf16[256,512]{0,1:T(8,128)(2,1)S(1)} %broadcast_select_fusion.10), channel_id=1, source_target_pairs={{0,8},{8,16},{16,24},{24,32},{32,40},{40,48},{48,56},{56,64},{64,7... | collective-permute-start | bytes 786440 | tf_op jit(solution)/shard_map/ppermute | solution.py:22
  172.6 9.1 %collective-permute-start.9 = (bf16[2,512]{0,1:T(8,128)(2,1)S(1)}, bf16[2,512]{0,1:T(8,128)(2,1)S(1)}, u32[]{:S(2)}, u32[]{:S(2)}) collective-permute-start(bf16[2,512]{0,1:T(8,128)(2,1)S(1)} %slice.306), channel_id=1, source_target_pairs={{8,0},{16,8},{24,16},{32,24},{40,32},{48,40},{56,48},{64,56},{72,6... | collective-permute-start | bytes 6152 | tf_op jit(solution)/shard_map/ppermute | solution.py:22
  185.8 72.2 %all-to-all-start = ((bf16[8,256,512]{1,2,0:T(8,128)(2,1)}), bf16[8,256,512]{1,2,0:T(8,128)(2,1)S(1)}, u32[]{:S(2)}, u32[]{:S(2)}) async-start(bf16[8,256,512]{1,2,0:T(8,128)(2,1)} %broadcast_in_dim.198), calls=%async_computation | async-start | bytes 4194304 | tf_op jit(solution)/shard_map/all_to_all | solution.py:157
  199.1 10.6 %collective-permute-start.10 = (bf16[256,512]{0,1:T(8,128)(2,1)}, bf16[256,512]{0,1:T(8,128)(2,1)}, u32[]{:S(2)}, u32[]{:S(2)}) collective-permute-start(bf16[256,512]{0,1:T(8,128)(2,1)} %get-tuple-element.14), channel_id=1, source_target_pairs={{8,0},{16,8},{24,16},{32,24},{40,32},{48,40},{56,48},{64,56},{72,6... | collective-permute-start | bytes 786440 | tf_op jit(solution)/shard_map/ppermute | solution.py:22
  209.7 24.7 %copy-start.4 = (bf16[4,256,511]{2,1,0:T(8,128)(2,1)S(1)}, bf16[4,256,511]{2,1,0:T(8,128)(2,1)}, u32[]{:S(2)}) copy-start(bf16[4,256,511]{2,1,0:T(8,128)(2,1)} %copy-done.3) | copy-start | bytes 3139588
  209.7 11.7 %collective-permute-start.11 = (bf16[256,512]{0,1:T(8,128)(2,1)S(1)}, bf16[256,512]{0,1:T(8,128)(2,1)S(1)}, u32[]{:S(2)}, u32[]{:S(2)}) collective-permute-start(bf16[256,512]{0,1:T(8,128)(2,1)S(1)} %broadcast_select_fusion.9), channel_id=1, source_target_pairs={{8,0},{16,8},{24,16},{32,24},{40,32},{48,40},{56,48},{64,56},{72,6... | collective-permute-start | bytes 786440 | tf_op jit(solution)/shard_map/ppermute | solution.py:22
  221.4 12.3 %collective-permute-start.12 = (bf16[256,512]{0,1:T(8,128)(2,1)S(1)}, bf16[256,512]{0,1:T(8,128)(2,1)S(1)}, u32[]{:S(2)}, u32[]{:S(2)}) collective-permute-start(bf16[256,512]{0,1:T(8,128)(2,1)S(1)} %broadcast_select_fusion.8), channel_id=1, source_target_pairs={{8,0},{16,8},{24,16},{32,24},{40,32},{48,40},{56,48},{64,56},{72,6... | collective-permute-start | bytes 786440 | tf_op jit(solution)/shard_map/ppermute | solution.py:22
  237.2 9.4 %collective-permute-start.14 = (bf16[2,512]{0,1:T(8,128)(2,1)S(1)}, bf16[2,512]{0,1:T(8,128)(2,1)S(1)}, u32[]{:S(2)}, u32[]{:S(2)}) collective-permute-start(bf16[2,512]{0,1:T(8,128)(2,1)S(1)} %slice.312), channel_id=1, source_target_pairs={{8,0},{16,8},{24,16},{32,24},{40,32},{48,40},{56,48},{64,56},{72,6... | collective-permute-start | bytes 6152 | tf_op jit(solution)/shard_map/ppermute | solution.py:22
  247.6 8.4 %collective-permute-start.13 = (bf16[2,512]{0,1:T(8,128)(2,1)S(1)}, bf16[2,512]{0,1:T(8,128)(2,1)S(1)}, u32[]{:S(2)}, u32[]{:S(2)}) collective-permute-start(bf16[2,512]{0,1:T(8,128)(2,1)S(1)} %slice.309), channel_id=1, source_target_pairs={{8,0},{16,8},{24,16},{32,24},{40,32},{48,40},{56,48},{64,56},{72,6... | collective-permute-start | bytes 6152 | tf_op jit(solution)/shard_map/ppermute | solution.py:22
  (40 other events, 389.5 us)

commit v4 on v2

--- a/solution.py
+++ b/solution.py
@@ -9,9 +9,17 @@
 CH = ("zh", "x")
 
 
+def gather_along(block, axis):
+    size = lax.axis_size(axis)
+    parts = [block]
+    for step in range(1, size):
+        parts.append(lax.ppermute(block, axis, [(i, (i - step) % size) for i in range(size)]))
+    return jnp.roll(jnp.stack(parts), lax.axis_index(axis), axis=0)
+
+
 def gather_weight(out_weight, chip_count):
-    spread = jnp.broadcast_to(out_weight[None], (chip_count,) + out_weight.shape)
-    mine = lax.all_to_all(spread, CHIPS, 0, 0, tiled=True).reshape(-1, out_weight.shape[1])
+    along_y = gather_along(out_weight, "y")
+    mine = gather_along(along_y, "zl").reshape(-1, out_weight.shape[1])
     other = lax.ppermute(mine, "core", [(0, 1), (1, 0)])
     return mine, other, lax.axis_index("core")
 

time: 275 us -> 318 us (1.16)
  the two profiles are of different devices: /device:TPU:1 before, /device:TPU:125 now
where the time goes in v4:
time: 318 us; the launch traced here: 316 us
  waiting for transfers between devices  108 us (34%)
  starting transfers between devices  99.2 us (31%)
  local copies, waits for them, and re-layouts  57.8 us (18%)
  other arithmetic  28.4 us (9%)
  matrix products  17.4 us (5%)
  between operations  5.14 us (2%)
    ppermute x14, waiting for transfers between devices, shifted(): return lax.ppermute(array, axis, pairs)  61.4 us
    ppermute x10, waiting for transfers between devices, gather_along(): lax.ppermute(block, axis, [(i, (i - step) % size) for i in range(size)])  41.7 us
    ppermute x14, starting transfers between devices, shifted(): return lax.ppermute(array, axis, pairs)  40.7 us
    ppermute x10, starting transfers between devices, gather_along(): lax.ppermute(block, axis, [(i, (i - step) % size) for i in range(size)])  37.5 us
    unnamed x104, local copies, waits for them, and re-layouts  25.6 us
    reshape x4, local copies, waits for them, and re-layouts, toeplitz_tiles(): repeated.reshape(group_count, row_count, 2 * row_count - 1)  15.2 us
    all_to_all x1, starting transfers between devices, local(): summed = jnp.sum(lax.all_to_all(sent, CH, 0, 0, tiled=True), axis=0)  10.1 us
    all_to_all x1, starting transfers between devices, local(): lax.all_to_all(spread, CH, 0, 0, tiled=True)  8.43 us
  transfers between devices with their start and end apart: 27, of which 15 were waited for; matrix products, arithmetic and copies ran while one was open for 26% of the time, Pallas kernels for 0%

profile of v4, /device:TPU:125, one launch (start us, length us, event | category | flops | bytes accessed | tf_op | source)
XLA Modules:
  0.0 315.7 jit_solution(688407409580383663)
XLA Ops:
  0.6 3.1 collective-permute-start.8
  3.8 3.8 %collective-permute-start.9 = (bf16[64,512]{1,0:T(8,128)(2,1)}, bf16[64,512]{1,0:T(8,128)(2,1)S(1)}, u32[]{:S(2)}, u32[]{:S(2)}) collective-permute-start(bf16[64,512]{1,0:T(8,128)(2,1)} %param.15), channel_id=1, source_target_pairs={{0,96},{16,112},{32,0},{48,16},{64,32},{80,48},{96,64},{112,80},{1... | collective-permute-start | bytes 196616 | tf_op jit(solution)/shard_map/ppermute | solution.py:16
  9.5 6.5 %collective-permute-start.11 = (bf16[64,512]{1,0:T(8,128)(2,1)}, bf16[64,512]{1,0:T(8,128)(2,1)S(1)}, u32[]{:S(2)}, u32[]{:S(2)}) collective-permute-start(bf16[64,512]{1,0:T(8,128)(2,1)} %param.15), channel_id=1, source_target_pairs={{0,64},{16,80},{32,96},{48,112},{64,0},{80,16},{96,32},{112,48},{1... | collective-permute-start | bytes 196616 | tf_op jit(solution)/shard_map/ppermute | solution.py:16
  18.8 5.1 %collective-permute-start.13 = (bf16[64,512]{1,0:T(8,128)(2,1)}, bf16[64,512]{1,0:T(8,128)(2,1)S(1)}, u32[]{:S(2)}, u32[]{:S(2)}) collective-permute-start(bf16[64,512]{1,0:T(8,128)(2,1)} %param.15), channel_id=1, source_target_pairs={{0,32},{16,48},{32,64},{48,80},{64,96},{80,112},{96,0},{112,16},{1... | collective-permute-start | bytes 196616 | tf_op jit(solution)/shard_map/ppermute | solution.py:16
  23.9 3.2 %collective-permute-start.14 = (bf16[64,512]{1,0:T(8,128)(2,1)}, bf16[64,512]{1,0:T(8,128)(2,1)S(1)}, u32[]{:S(2)}, u32[]{:S(2)}) collective-permute-start(bf16[64,512]{1,0:T(8,128)(2,1)} %param.15), channel_id=1, source_target_pairs={{0,16},{16,32},{32,48},{48,64},{64,80},{80,96},{96,112},{112,0},{1... | collective-permute-start | bytes 196616 | tf_op jit(solution)/shard_map/ppermute | solution.py:16
  34.3 5.8 %collective-permute-start.16 = (bf16[8,64,512]{2,1,0:T(8,128)(2,1)S(1)}, bf16[8,64,512]{2,1,0:T(8,128)(2,1)S(1)}, u32[]{:S(2)}, u32[]{:S(2)}) collective-permute-start(bf16[8,64,512]{2,1,0:T(8,128)(2,1)S(1)} %get-tuple-element.19), channel_id=1, source_target_pairs={{0,256},{128,384},{256,0},{384,128},{1,257},{129,385},{257,1},{385... | collective-permute-start | bytes 1572872 | tf_op jit(solution)/shard_map/ppermute | solution.py:16
  40.1 4.3 %collective-permute-start.17 = (bf16[8,64,512]{2,1,0:T(8,128)(2,1)S(1)}, bf16[8,64,512]{2,1,0:T(8,128)(2,1)S(1)}, u32[]{:S(2)}, u32[]{:S(2)}) collective-permute-start(bf16[8,64,512]{2,1,0:T(8,128)(2,1)S(1)} %get-tuple-element.19), channel_id=1, source_target_pairs={{0,128},{128,256},{256,384},{384,0},{1,129},{129,257},{257,385},{3... | collective-permute-start | bytes 1572872 | tf_op jit(solution)/shard_map/ppermute | solution.py:16
  47.3 25.9 %collective-permute-done.16 = bf16[8,64,512]{2,1,0:T(8,128)(2,1)S(1)} collective-permute-done((bf16[8,64,512]{2,1,0:T(8,128)(2,1)S(1)}, bf16[8,64,512]{2,1,0:T(8,128)(2,1)S(1)}, u32[]{:S(2)}, u32[]{:S(2)}) %collective-permute-start.16) | collective-permute-done | bytes 524320 | tf_op jit(solution)/shard_map/ppermute | solution.py:16
  74.0 10.4 %collective-permute-done.17 = bf16[8,64,512]{2,1,0:T(8,128)(2,1)S(1)} collective-permute-done((bf16[8,64,512]{2,1,0:T(8,128)(2,1)S(1)}, bf16[8,64,512]{2,1,0:T(8,128)(2,1)S(1)}, u32[]{:S(2)}, u32[]{:S(2)}) %collective-permute-start.17) | collective-permute-done | bytes 524320 | tf_op jit(solution)/shard_map/ppermute | solution.py:16
  93.6 3.0 collective-permute-done.18
  100.7 10.1 %all-to-all-start.1 = ((f32[8,2,4,64,256]{4,3,2,1,0:T(8,128)}), f32[8,2,4,64,256]{4,3,2,1,0:T(8,128)}, u32[]{:S(2)}, u32[]{:S(2)}) async-start(f32[8,2,4,64,256]{4,3,2,1,0:T(8,128)} %copy.50), calls=%async_computation.1 | async-start | bytes 8388608 | tf_op jit(solution)/shard_map/all_to_all | solution.py:188
  114.3 5.0 %collective-permute-start = (s32[2]{0:T(128)}, s32[2]{0:T(128)}, u32[]{:S(2)}, u32[]{:S(2)}) collective-permute-start(s32[2]{0:T(128)} %get-tuple-element.60), channel_id=1, source_target_pairs={{0,8},{8,16},{16,24},{24,32},{32,40},{40,48},{48,56},{56,64},{64,7... | collective-permute-start | bytes 32 | tf_op jit(solution)/shard_map/ppermute | solution.py:30
  151.2 4.0 %reshape.172 = bf16[4,256,511]{2,1,0:T(8,128)(2,1)} reshape(bf16[4,130816]{1,0:T(4,128)(2,1)} %slice.296) | data formatting | bytes 2093056 | tf_op jit(solution)/shard_map/reshape | solution.py:56
  158.6 4.1 %reshape.174 = bf16[4,256,511]{2,1,0:T(8,128)(2,1)} reshape(bf16[4,130816]{1,0:T(4,128)(2,1)} %slice.298) | data formatting | bytes 2093056 | tf_op jit(solution)/shard_map/reshape | solution.py:56
  164.9 3.0 reshape.176
  171.7 4.0 %reshape.169 = bf16[4,256,511]{2,1,0:T(8,128)(2,1)} reshape(bf16[4,130816]{1,0:T(4,128)(2,1)} %slice.294) | data formatting | bytes 2093056 | tf_op jit(solution)/shard_map/reshape | solution.py:56
  184.0 8.2 %collective-permute-start.7 = (bf16[256,512]{0,1:T(8,128)(2,1)S(1)}, bf16[256,512]{0,1:T(8,128)(2,1)S(1)}, u32[]{:S(2)}, u32[]{:S(2)}) collective-permute-start(bf16[256,512]{0,1:T(8,128)(2,1)S(1)} %broadcast_select_fusion.10), channel_id=1, source_target_pairs={{0,8},{8,16},{16,24},{24,32},{32,40},{40,48},{48,56},{56,64},{64,7... | collective-permute-start | bytes 786440 | tf_op jit(solution)/shard_map/ppermute | solution.py:30
  209.2 24.8 %collective-permute-done.19 = bf16[2,512]{0,1:T(8,128)(2,1)S(1)} collective-permute-done((bf16[2,512]{0,1:T(8,128)(2,1)S(1)}, bf16[2,512]{0,1:T(8,128)(2,1)S(1)}, u32[]{:S(2)}, u32[]{:S(2)}) %collective-permute-start.19) | collective-permute-done | bytes 2080 | tf_op jit(solution)/shard_map/ppermute | solution.py:30
  238.5 8.4 %all-to-all-start = ((bf16[8,256,512]{1,2,0:T(8,128)(2,1)}), bf16[8,256,512]{1,2,0:T(8,128)(2,1)}, u32[]{:S(2)}, u32[]{:S(2)}) async-start(bf16[8,256,512]{1,2,0:T(8,128)(2,1)} %broadcast_in_dim.192), calls=%async_computation | async-start | bytes 4194304 | tf_op jit(solution)/shard_map/all_to_all | solution.py:165
  254.8 10.2 %collective-permute-done.20 = bf16[256,512]{0,1:T(8,128)(2,1)S(1)} collective-permute-done((bf16[256,512]{0,1:T(8,128)(2,1)}, bf16[256,512]{0,1:T(8,128)(2,1)S(1)}, u32[]{:S(2)}, u32[]{:S(2)}) %collective-permute-start.20) | collective-permute-done | bytes 262176 | tf_op jit(solution)/shard_map/ppermute | solution.py:30
  269.7 8.6 %collective-permute-done.21 = bf16[256,512]{0,1:T(8,128)(2,1)S(1)} collective-permute-done((bf16[256,512]{0,1:T(8,128)(2,1)S(1)}, bf16[256,512]{0,1:T(8,128)(2,1)S(1)}, u32[]{:S(2)}, u32[]{:S(2)}) %collective-permute-start.21) | collective-permute-done | bytes 262176 | tf_op jit(solution)/shard_map/ppermute | solution.py:30
  281.9 6.2 %collective-permute-done.22 = bf16[256,512]{0,1:T(8,128)(2,1)S(1)} collective-permute-done((bf16[256,512]{0,1:T(8,128)(2,1)S(1)}, bf16[256,512]{0,1:T(8,128)(2,1)S(1)}, u32[]{:S(2)}, u32[]{:S(2)}) %collective-permute-start.22) | collective-permute-done | bytes 262176 | tf_op jit(solution)/shard_map/ppermute | solution.py:30
  293.5 6.5 %collective-permute-done.24 = bf16[2,512]{0,1:T(8,128)(2,1)S(1)} collective-permute-done((bf16[2,512]{0,1:T(8,128)(2,1)S(1)}, bf16[2,512]{0,1:T(8,128)(2,1)S(1)}, u32[]{:S(2)}, u32[]{:S(2)}) %collective-permute-start.24) | collective-permute-done | bytes 2080 | tf_op jit(solution)/shard_map/ppermute | solution.py:30
  305.5 3.8 %collective-permute-done.23 = bf16[2,512]{0,1:T(8,128)(2,1)S(1)} collective-permute-done((bf16[2,512]{0,1:T(8,128)(2,1)S(1)}, bf16[2,512]{0,1:T(8,128)(2,1)S(1)}, u32[]{:S(2)}, u32[]{:S(2)}) %collective-permute-start.23) | collective-permute-done | bytes 2080 | tf_op jit(solution)/shard_map/ppermute | solution.py:30
  (207 shorter events, 132.5 us)
Async XLA Ops:
  0.6 18.1 %collective-permute-start.8 = (bf16[64,512]{1,0:T(8,128)(2,1)}, bf16[64,512]{1,0:T(8,128)(2,1)S(1)}, u32[]{:S(2)}, u32[]{:S(2)}) collective-permute-start(bf16[64,512]{1,0:T(8,128)(2,1)} %param.15), channel_id=1, source_target_pairs={{0,112},{16,0},{32,16},{48,32},{64,48},{80,64},{96,80},{112,96},{1... | collective-permute-start | bytes 196616 | tf_op jit(solution)/shard_map/ppermute | solution.py:16
  3.8 20.1 %collective-permute-start.9 = (bf16[64,512]{1,0:T(8,128)(2,1)}, bf16[64,512]{1,0:T(8,128)(2,1)S(1)}, u32[]{:S(2)}, u32[]{:S(2)}) collective-permute-start(bf16[64,512]{1,0:T(8,128)(2,1)} %param.15), channel_id=1, source_target_pairs={{0,96},{16,112},{32,0},{48,16},{64,32},{80,48},{96,64},{112,80},{1... | collective-permute-start | bytes 196616 | tf_op jit(solution)/shard_map/ppermute | solution.py:16
  7.5 19.6 %collective-permute-start.10 = (bf16[64,512]{1,0:T(8,128)(2,1)}, bf16[64,512]{1,0:T(8,128)(2,1)S(1)}, u32[]{:S(2)}, u32[]{:S(2)}) collective-permute-start(bf16[64,512]{1,0:T(8,128)(2,1)} %param.15), channel_id=1, source_target_pairs={{0,80},{16,96},{32,112},{48,0},{64,16},{80,32},{96,48},{112,64},{1... | collective-permute-start | bytes 196616 | tf_op jit(solution)/shard_map/ppermute | solution.py:16
  9.5 17.7 %collective-permute-start.11 = (bf16[64,512]{1,0:T(8,128)(2,1)}, bf16[64,512]{1,0:T(8,128)(2,1)S(1)}, u32[]{:S(2)}, u32[]{:S(2)}) collective-permute-start(bf16[64,512]{1,0:T(8,128)(2,1)} %param.15), channel_id=1, source_target_pairs={{0,64},{16,80},{32,96},{48,112},{64,0},{80,16},{96,32},{112,48},{1... | collective-permute-start | bytes 196616 | tf_op jit(solution)/shard_map/ppermute | solution.py:16
  16.0 11.2 %collective-permute-start.12 = (bf16[64,512]{1,0:T(8,128)(2,1)}, bf16[64,512]{1,0:T(8,128)(2,1)S(1)}, u32[]{:S(2)}, u32[]{:S(2)}) collective-permute-start(bf16[64,512]{1,0:T(8,128)(2,1)} %param.15), channel_id=1, source_target_pairs={{0,48},{16,64},{32,80},{48,96},{64,112},{80,0},{96,16},{112,32},{1... | collective-permute-start | bytes 196616 | tf_op jit(solution)/shard_map/ppermute | solution.py:16
  18.8 10.9 %collective-permute-start.13 = (bf16[64,512]{1,0:T(8,128)(2,1)}, bf16[64,512]{1,0:T(8,128)(2,1)S(1)}, u32[]{:S(2)}, u32[]{:S(2)}) collective-permute-start(bf16[64,512]{1,0:T(8,128)(2,1)} %param.15), channel_id=1, source_target_pairs={{0,32},{16,48},{32,64},{48,80},{64,96},{80,112},{96,0},{112,16},{1... | collective-permute-start | bytes 196616 | tf_op jit(solution)/shard_map/ppermute | solution.py:16
  32.4 14.1 %collective-permute-start.15 = (bf16[8,64,512]{2,1,0:T(8,128)(2,1)S(1)}, bf16[8,64,512]{2,1,0:T(8,128)(2,1)S(1)}, u32[]{:S(2)}, u32[]{:S(2)}) collective-permute-start(bf16[8,64,512]{2,1,0:T(8,128)(2,1)S(1)} %get-tuple-element.19), channel_id=1, source_target_pairs={{0,384},{128,0},{256,128},{384,256},{1,385},{129,1},{257,129},{385... | collective-permute-start | bytes 1572872 | tf_op jit(solution)/shard_map/ppermute | solution.py:16
  34.3 38.9 %collective-permute-start.16 = (bf16[8,64,512]{2,1,0:T(8,128)(2,1)S(1)}, bf16[8,64,512]{2,1,0:T(8,128)(2,1)S(1)}, u32[]{:S(2)}, u32[]{:S(2)}) collective-permute-start(bf16[8,64,512]{2,1,0:T(8,128)(2,1)S(1)} %get-tuple-element.19), channel_id=1, source_target_pairs={{0,256},{128,384},{256,0},{384,128},{1,257},{129,385},{257,1},{385... | collective-permute-start | bytes 1572872 | tf_op jit(solution)/shard_map/ppermute | solution.py:16
  40.1 44.3 %collective-permute-start.17 = (bf16[8,64,512]{2,1,0:T(8,128)(2,1)S(1)}, bf16[8,64,512]{2,1,0:T(8,128)(2,1)S(1)}, u32[]{:S(2)}, u32[]{:S(2)}) collective-permute-start(bf16[8,64,512]{2,1,0:T(8,128)(2,1)S(1)} %get-tuple-element.19), channel_id=1, source_target_pairs={{0,128},{128,256},{256,384},{384,0},{1,129},{129,257},{257,385},{3... | collective-permute-start | bytes 1572872 | tf_op jit(solution)/shard_map/ppermute | solution.py:16
  100.7 99.1 %all-to-all-start.1 = ((f32[8,2,4,64,256]{4,3,2,1,0:T(8,128)}), f32[8,2,4,64,256]{4,3,2,1,0:T(8,128)}, u32[]{:S(2)}, u32[]{:S(2)}) async-start(f32[8,2,4,64,256]{4,3,2,1,0:T(8,128)} %copy.50), calls=%async_computation.1 | async-start | bytes 8388608 | tf_op jit(solution)/shard_map/all_to_all | solution.py:188
  111.4 24.2 %collective-permute-start.4 = (s32[2]{0:T(128)}, s32[2]{0:T(128)}, u32[]{:S(2)}, u32[]{:S(2)}) collective-permute-start(s32[2]{0:T(128)} %get-tuple-element.61), channel_id=1, source_target_pairs={{8,0},{16,8},{24,16},{32,24},{40,32},{48,40},{56,48},{64,56},{72,6... | collective-permute-start | bytes 32 | tf_op jit(solution)/shard_map/ppermute | solution.py:30
  114.3 22.0 %collective-permute-start = (s32[2]{0:T(128)}, s32[2]{0:T(128)}, u32[]{:S(2)}, u32[]{:S(2)}) collective-permute-start(s32[2]{0:T(128)} %get-tuple-element.60), channel_id=1, source_target_pairs={{0,8},{8,16},{16,24},{24,32},{32,40},{40,48},{48,56},{56,64},{64,7... | collective-permute-start | bytes 32 | tf_op jit(solution)/shard_map/ppermute | solution.py:30
  120.8 88.4 %collective-permute-start.1 = (bf16[2,512]{0,1:T(8,128)(2,1)}, bf16[2,512]{0,1:T(8,128)(2,1)}, u32[]{:S(2)}, u32[]{:S(2)}) collective-permute-start(bf16[2,512]{0,1:T(8,128)(2,1)} %copy.42), channel_id=1, source_target_pairs={{0,8},{8,16},{16,24},{24,32},{32,40},{40,48},{48,56},{56,64},{64,7... | collective-permute-start | bytes 6152 | tf_op jit(solution)/shard_map/ppermute | solution.py:30
  124.1 15.9 %collective-permute-start.2 = (bf16[2,512]{0,1:T(8,128)(2,1)}, bf16[2,512]{0,1:T(8,128)(2,1)}, u32[]{:S(2)}, u32[]{:S(2)}) collective-permute-start(bf16[2,512]{0,1:T(8,128)(2,1)} %copy.45), channel_id=1, source_target_pairs={{0,8},{8,16},{16,24},{24,32},{32,40},{40,48},{48,56},{56,64},{64,7... | collective-permute-start | bytes 6152 | tf_op jit(solution)/shard_map/ppermute | solution.py:30
  127.6 12.4 %collective-permute-start.3 = (bf16[2,512]{0,1:T(8,128)(2,1)}, bf16[2,512]{0,1:T(8,128)(2,1)S(1)}, u32[]{:S(2)}, u32[]{:S(2)}) collective-permute-start(bf16[2,512]{0,1:T(8,128)(2,1)} %copy.48), channel_id=1, source_target_pairs={{0,8},{8,16},{16,24},{24,32},{32,40},{40,48},{48,56},{56,64},{64,7... | collective-permute-start | bytes 6152 | tf_op jit(solution)/shard_map/ppermute | solution.py:30
  143.0 35.0 %collective-permute-start.5 = (bf16[256,512]{0,1:T(8,128)(2,1)}, bf16[256,512]{0,1:T(8,128)(2,1)S(1)}, u32[]{:S(2)}, u32[]{:S(2)}) collective-permute-start(bf16[256,512]{0,1:T(8,128)(2,1)} %get-tuple-element.20), channel_id=1, source_target_pairs={{0,8},{8,16},{16,24},{24,32},{32,40},{40,48},{48,56},{56,64},{64,7... | collective-permute-start | bytes 786440 | tf_op jit(solution)/shard_map/ppermute | solution.py:30
  184.0 11.6 %collective-permute-start.7 = (bf16[256,512]{0,1:T(8,128)(2,1)S(1)}, bf16[256,512]{0,1:T(8,128)(2,1)S(1)}, u32[]{:S(2)}, u32[]{:S(2)}) collective-permute-start(bf16[256,512]{0,1:T(8,128)(2,1)S(1)} %broadcast_select_fusion.10), channel_id=1, source_target_pairs={{0,8},{8,16},{16,24},{24,32},{32,40},{40,48},{48,56},{56,64},{64,7... | collective-permute-start | bytes 786440 | tf_op jit(solution)/shard_map/ppermute | solution.py:30
  205.7 28.4 %collective-permute-start.19 = (bf16[2,512]{0,1:T(8,128)(2,1)S(1)}, bf16[2,512]{0,1:T(8,128)(2,1)S(1)}, u32[]{:S(2)}, u32[]{:S(2)}) collective-permute-start(bf16[2,512]{0,1:T(8,128)(2,1)S(1)} %slice.306), channel_id=1, source_target_pairs={{8,0},{16,8},{24,16},{32,24},{40,32},{48,40},{56,48},{64,56},{72,6... | collective-permute-start | bytes 6152 | tf_op jit(solution)/shard_map/ppermute | solution.py:30
  238.5 72.8 %all-to-all-start = ((bf16[8,256,512]{1,2,0:T(8,128)(2,1)}), bf16[8,256,512]{1,2,0:T(8,128)(2,1)}, u32[]{:S(2)}, u32[]{:S(2)}) async-start(bf16[8,256,512]{1,2,0:T(8,128)(2,1)} %broadcast_in_dim.192), calls=%async_computation | async-start | bytes 4194304 | tf_op jit(solution)/shard_map/all_to_all | solution.py:165
  251.2 13.8 %collective-permute-start.20 = (bf16[256,512]{0,1:T(8,128)(2,1)}, bf16[256,512]{0,1:T(8,128)(2,1)S(1)}, u32[]{:S(2)}, u32[]{:S(2)}) collective-permute-start(bf16[256,512]{0,1:T(8,128)(2,1)} %get-tuple-element.14), channel_id=1, source_target_pairs={{8,0},{16,8},{24,16},{32,24},{40,32},{48,40},{56,48},{64,56},{72,6... | collective-permute-start | bytes 786440 | tf_op jit(solution)/shard_map/ppermute | solution.py:30
  265.0 13.3 %collective-permute-start.21 = (bf16[256,512]{0,1:T(8,128)(2,1)S(1)}, bf16[256,512]{0,1:T(8,128)(2,1)S(1)}, u32[]{:S(2)}, u32[]{:S(2)}) collective-permute-start(bf16[256,512]{0,1:T(8,128)(2,1)S(1)} %broadcast_select_fusion.9), channel_id=1, source_target_pairs={{8,0},{16,8},{24,16},{32,24},{40,32},{48,40},{56,48},{64,56},{72,6... | collective-permute-start | bytes 786440 | tf_op jit(solution)/shard_map/ppermute | solution.py:30
  278.3 9.8 %collective-permute-start.22 = (bf16[256,512]{0,1:T(8,128)(2,1)S(1)}, bf16[256,512]{0,1:T(8,128)(2,1)S(1)}, u32[]{:S(2)}, u32[]{:S(2)}) collective-permute-start(bf16[256,512]{0,1:T(8,128)(2,1)S(1)} %broadcast_select_fusion.8), channel_id=1, source_target_pairs={{8,0},{16,8},{24,16},{32,24},{40,32},{48,40},{56,48},{64,56},{72,6... | collective-permute-start | bytes 786440 | tf_op jit(solution)/shard_map/ppermute | solution.py:30
  291.6 8.4 %collective-permute-start.24 = (bf16[2,512]{0,1:T(8,128)(2,1)S(1)}, bf16[2,512]{0,1:T(8,128)(2,1)S(1)}, u32[]{:S(2)}, u32[]{:S(2)}) collective-permute-start(bf16[2,512]{0,1:T(8,128)(2,1)S(1)} %slice.312), channel_id=1, source_target_pairs={{8,0},{16,8},{24,16},{32,24},{40,32},{48,40},{56,48},{64,56},{72,6... | collective-permute-start | bytes 6152 | tf_op jit(solution)/shard_map/ppermute | solution.py:30
  300.9 8.4 %collective-permute-start.23 = (bf16[2,512]{0,1:T(8,128)(2,1)S(1)}, bf16[2,512]{0,1:T(8,128)(2,1)S(1)}, u32[]{:S(2)}, u32[]{:S(2)}) collective-permute-start(bf16[2,512]{0,1:T(8,128)(2,1)S(1)} %slice.309), channel_id=1, source_target_pairs={{8,0},{16,8},{24,16},{32,24},{40,32},{48,40},{56,48},{64,56},{72,6... | collective-permute-start | bytes 6152 | tf_op jit(solution)/shard_map/ppermute | solution.py:30
  (37 other events, 788.4 us)

commit v5 on v2

--- a/solution.py
+++ b/solution.py
@@ -153,10 +153,15 @@
     chip_count = lax.axis_size(CHIPS)
     weight_rows, weight_rows_other, core_index = gather_weight(out_weight, chip_count)
     ch_count = lax.axis_size(CH)
-    spread = jnp.broadcast_to(pre_gate[None], (ch_count,) + pre_gate.shape)
-    gathered = lax.all_to_all(spread, CH, 0, 0, tiled=True).reshape(
-        ch_count, row_count, channels
-    )
+    far_count = lax.axis_size("zh")
+    near_count = lax.axis_size("x")
+    paired = lax.all_to_all(
+        jnp.broadcast_to(pre_gate[None], (far_count,) + pre_gate.shape), "zh", 0, 0, tiled=True
+    )
+    gathered = lax.all_to_all(
+        jnp.broadcast_to(paired[None], (near_count,) + paired.shape), "x", 0, 0, tiled=True
+    )
+    gathered = jnp.transpose(gathered, (1, 0, 2, 3)).reshape(ch_count, row_count, channels)
     full_pre = jnp.transpose(gathered, (1, 0, 2)).reshape(
         row_count, chip_count, pair_size, out_weight.shape[0]
     )
@@ -176,8 +181,11 @@
     part_other = lax.dot_general(
         weight_rows_other, out_grad, dims, preferred_element_type=jnp.float32
     ).reshape(ch_count, 1, block_chips, -1, row_count)
-    sent = jnp.concatenate([part_mine, part_other], axis=1)
-    summed = jnp.sum(lax.all_to_all(sent, CH, 0, 0, tiled=True), axis=0)
+    sent = jnp.concatenate([part_mine, part_other], axis=1).reshape(
+        far_count, near_count, 2, block_chips, -1, row_count
+    )
+    near_sum = jnp.sum(lax.all_to_all(sent, "x", 1, 1, tiled=True), axis=1)
+    summed = jnp.sum(lax.all_to_all(near_sum, "zh", 0, 0, tiled=True), axis=0)
     cols_mine, cols_other = summed[0][:, None], summed[1][:, None]
     grad_cols = jnp.where(
         on_first,

time: 275 us -> 280 us (1.018)
  waiting for transfers between devices: 48.3 us -> 24.2 us
  starting transfers between devices: 58.4 us -> 70.9 us
  local copies, waits for them, and re-layouts: 50.2 us -> 57 us
  matrix products: 17.2 us -> 23.9 us
    all_to_all x2 -> x4, waiting for transfers between devices: 23.6 us -> 10.7 us  [the longest x1 6.43 us: local(): summed = jnp.sum(lax.all_to_all(near_sum, 'zh', 0, 0, tiled=True), axis=0)]
    ppermute x14, starting transfers between devices: 34.6 us -> 43.6 us  [shifted(): return lax.ppermute(array, axis, pairs)]
    ppermute x14, waiting for transfers between devices: 21.6 us -> 13.6 us  [shifted(): return lax.ppermute(array, axis, pairs)]
    all_to_all x2 -> x4, starting transfers between devices: 17.6 us -> 21.2 us  [the longest x1 7.31 us: local(): summed = jnp.sum(lax.all_to_all(near_sum, 'zh', 0, 0, tiled=True), axis=0)]
    reduce_sum x1 -> x2, other arithmetic: 2.53 us -> 5.76 us  [the longest x1 3.62 us: local(): near_sum = jnp.sum(lax.all_to_all(sent, 'x', 1, 1, tiled=True), axis=1)]
    ppermute x1, waiting for transfers between devices: 3.01 us -> 0.01 us  [gather_weight(): other = lax.ppermute(mine, 'core', [(0, 1), (1, 0)])]
    unnamed x96 -> x108, local copies, waits for them, and re-layouts: 18.8 us -> 19.2 us
  transfers between devices with their start and end apart: 17 -> 19, of which waited for: 9 -> 6; matrix products, arithmetic and copies ran while one was open for 31% -> 37% of each run, Pallas kernels for 0% -> 0%
where the time goes in v5:
time: 280 us; the launch traced here: 275 us
  starting transfers between devices  70.9 us (25%)
  blocking collectives  61.8 us (22%)
  local copies, waits for them, and re-layouts  57 us (20%)
  other arithmetic  32.1 us (11%)
  waiting for transfers between devices  24.2 us (9%)
  matrix products  23.9 us (9%)
  between operations  5.36 us (2%)
    all_to_all x1, blocking collectives, gather_weight(): lax.all_to_all(spread, CHIPS, 0, 0, tiled=True)  61.8 us
    ppermute x14, starting transfers between devices, shifted(): return lax.ppermute(array, axis, pairs)  43.6 us
    unnamed x108, local copies, waits for them, and re-layouts  19.2 us
    reshape x4, local copies, waits for them, and re-layouts, toeplitz_tiles(): repeated.reshape(group_count, row_count, 2 * row_count - 1)  15.2 us
    ppermute x14, waiting for transfers between devices, shifted(): return lax.ppermute(array, axis, pairs)  13.6 us
    dot_general x4, matrix products, apply_forward(): jnp.einsum('gst,sgc->tgc', band_tile, grouped, preferred_element_type=jnp...  9.29 us
    dot_general x4, matrix products, apply_adjoint(): jnp.einsum('gst,tgc->sgc', band_tile, grouped, preferred_element_type=jnp...  7.81 us
    all_to_all x1, starting transfers between devices, local(): summed = jnp.sum(lax.all_to_all(near_sum, 'zh', 0, 0, tiled=True), axis=0)  7.31 us
  transfers between devices with their start and end apart: 19, of which 6 were waited for; matrix products, arithmetic and copies ran while one was open for 37% of the time, Pallas kernels for 0%

profile of v5, /device:TPU:1, one launch (start us, length us, event | category | flops | bytes accessed | tf_op | source)
XLA Modules:
  0.0 275.4 jit_solution(7062939893787414269)
XLA Ops:
  1.8 61.8 %all_to_all.25 = bf16[32,64,512]{2,1,0:T(8,128)(2,1)S(1)} all-to-all(bf16[32,64,512]{2,1,0:T(8,128)(2,1)S(1)} %broadcast_in_dim.206), channel_id=1, replica_groups=mesh['zl'=4,'y'=8,'core'=2,'zh'=2,'x'=4] {'zl','y'}, dimensions={0} | all-to-all | bytes 4194304 | tf_op jit(solution)/shard_map/all_to_all | solution.py:14
  63.6 6.2 %collective-permute-start.8 = (bf16[2048,512]{1,0:T(8,128)(2,1)S(1)}, bf16[2048,512]{1,0:T(8,128)(2,1)}, u32[]{:S(2)}, u32[]{:S(2)}) collective-permute-start(bf16[2048,512]{1,0:T(8,128)(2,1)S(1)} %bitcast.147), channel_id=1, source_target_pairs={{0,8},{8,0},{1,9},{9,1},{2,10},{10,2},{3,11},{11,3},{4,12},{12,4},... | collective-permute-start | bytes 6291464 | tf_op jit(solution)/shard_map/ppermute | solution.py:15
  72.3 3.6 %collective-permute-start = (s32[2]{0:T(128)}, s32[2]{0:T(128)}, u32[]{:S(2)}, u32[]{:S(2)}) collective-permute-start(s32[2]{0:T(128)} %get-tuple-element.62), channel_id=1, source_target_pairs={{0,8},{8,16},{16,24},{24,32},{32,40},{40,48},{48,56},{56,64},{64,7... | collective-permute-start | bytes 32 | tf_op jit(solution)/shard_map/ppermute | solution.py:22
  80.2 3.1 %collective-permute-start.2 = (bf16[2,512]{0,1:T(8,128)(2,1)}, bf16[2,512]{0,1:T(8,128)(2,1)}, u32[]{:S(2)}, u32[]{:S(2)}) collective-permute-start(bf16[2,512]{0,1:T(8,128)(2,1)} %copy.60), channel_id=1, source_target_pairs={{0,8},{8,16},{16,24},{24,32},{32,40},{40,48},{48,56},{56,64},{64,7... | collective-permute-start | bytes 6152 | tf_op jit(solution)/shard_map/ppermute | solution.py:22
  92.9 5.0 %all-to-all-start.3 = ((f32[2,4,2,4,64,256]{5,4,3,0,2,1:T(8,128)}), f32[2,4,2,4,64,256]{5,4,3,0,2,1:T(8,128)}, u32[]{:S(2)}, u32[]{:S(2)}) async-start(f32[2,4,2,4,64,256]{5,4,3,0,2,1:T(8,128)} %copy.66), calls=%async_computation.3 | async-start | bytes 8388608 | tf_op jit(solution)/shard_map/all_to_all | solution.py:187
  110.9 3.1 %select_select_fusion.1 = (bf16[256,512]{0,1:T(8,128)(2,1)}, bf16[256,512]{0,1:T(8,128)(2,1)}) fusion(pred[256]{0:T(512)(128)(4,1)} %get-tuple-element.51, pred[]{:T(512)S(6)} %eq.69, bf16[256,512]{0,1:T(8,128)(2,1)S(1)} %copy.62, bf16[2,512]{0,1:T(8,128)(2,1)S(1)} %collective-permute-done.3, f32[512]{0:T(512)} %bitcast.180, f32[512]{0:T(512)} %bitcast.182, ...), kind=kLoop, calls=%fused_computation.94 | loop fusion | flops 4718592 | bytes 1065729 | tf_op jit(solution)/shard_map/jit(_where)/select_n | solution.py:143
  122.0 3.0 %reshape.189 = bf16[4,256,511]{2,1,0:T(8,128)(2,1)S(1)} reshape(bf16[4,130816]{1,0:T(4,128)(2,1)} %slice.300) | data formatting | bytes 2093056 | tf_op jit(solution)/shard_map/reshape | solution.py:48
  128.4 4.0 %reshape.187 = bf16[4,256,511]{2,1,0:T(8,128)(2,1)} reshape(bf16[4,130816]{1,0:T(4,128)(2,1)} %slice.298) | data formatting | bytes 2093056 | tf_op jit(solution)/shard_map/reshape | solution.py:48
  135.8 4.1 %reshape.185 = bf16[4,256,511]{2,1,0:T(8,128)(2,1)} reshape(bf16[4,130816]{1,0:T(4,128)(2,1)} %slice.296) | data formatting | bytes 2093056 | tf_op jit(solution)/shard_map/reshape | solution.py:48
  143.3 4.0 %reshape.182 = bf16[4,256,511]{2,1,0:T(8,128)(2,1)} reshape(bf16[4,130816]{1,0:T(4,128)(2,1)} %slice.294) | data formatting | bytes 2093056 | tf_op jit(solution)/shard_map/reshape | solution.py:48
  155.4 3.6 %reduce_sum.18 = f32[2,2,4,64,256]{4,3,2,0,1:T(8,128)} reduce(f32[2,4,2,4,64,256]{5,4,3,0,2,1:T(8,128)} %all-to-all-done.3, f32[]{:T(128)} %constant.5.clone.1), dimensions={1}, to_apply=%region_3.4 | reduce | flops 786432 | bytes 5242884 | tf_op jit(solution)/shard_map/reduce_sum | solution.py:187
  161.3 7.3 %all-to-all-start.4 = ((f32[2,2,4,64,256]{4,3,2,1,0:T(8,128)}), f32[2,2,4,64,256]{4,3,2,1,0:T(8,128)}, u32[]{:S(2)}, u32[]{:S(2)}) async-start(f32[2,2,4,64,256]{4,3,2,1,0:T(8,128)} %copy.68), calls=%async_computation.4 | async-start | bytes 2097152 | tf_op jit(solution)/shard_map/all_to_all | solution.py:188
  168.6 2.8 %broadcast_select_fusion.7 = f32[4,128,256]{2,1,0:T(8,128)} fusion(pred[]{:T(512)} %compare_reduce_fusion.5, bf16[256,4,128]{0,2,1:T(8,128)(2,1)S(1)} %bitcast.155, bf16[4,256,511]{2,1,0:T(8,128)(2,1)} %reshape.185), kind=kOutput, calls=%fused_computation.93 | convolution fusion | flops 67239936 | bytes 1311232 | tf_op jit(solution)/shard_map/gst,sgc->tgc/dot_general | solution.py:56
  172.4 5.1 %collective-permute-start.7 = (bf16[256,512]{0,1:T(8,128)(2,1)S(1)}, bf16[256,512]{0,1:T(8,128)(2,1)S(1)}, u32[]{:S(2)}, u32[]{:S(2)}) collective-permute-start(bf16[256,512]{0,1:T(8,128)(2,1)S(1)} %broadcast_select_fusion.10), channel_id=1, source_target_pairs={{0,8},{8,16},{16,24},{24,32},{32,40},{40,48},{48,56},{56,64},{64,7... | collective-permute-start | bytes 786440 | tf_op jit(solution)/shard_map/ppermute | solution.py:22
  184.2 6.4 %all-to-all-done.4 = f32[2,2,4,64,256]{4,3,2,1,0:T(8,128)} async-done(((f32[2,2,4,64,256]{4,3,2,1,0:T(8,128)}), f32[2,2,4,64,256]{4,3,2,1,0:T(8,128)}, u32[]{:S(2)}, u32[]{:S(2)}) %all-to-all-start.4) | async-done | bytes 1048608 | tf_op jit(solution)/shard_map/all_to_all | solution.py:188
  196.4 11.7 %collective-permute-start.10 = (bf16[256,512]{0,1:T(8,128)(2,1)}, bf16[256,512]{0,1:T(8,128)(2,1)S(1)}, u32[]{:S(2)}, u32[]{:S(2)}) collective-permute-start(bf16[256,512]{0,1:T(8,128)(2,1)} %get-tuple-element.18), channel_id=1, source_target_pairs={{8,0},{16,8},{24,16},{32,24},{40,32},{48,40},{56,48},{64,56},{72,6... | collective-permute-start | bytes 786440 | tf_op jit(solution)/shard_map/ppermute | solution.py:22
  211.6 3.2 %collective-permute-done.9 = bf16[2,512]{0,1:T(8,128)(2,1)S(1)} collective-permute-done((bf16[2,512]{0,1:T(8,128)(2,1)S(1)}, bf16[2,512]{0,1:T(8,128)(2,1)S(1)}, u32[]{:S(2)}, u32[]{:S(2)}) %collective-permute-start.9) | collective-permute-done | bytes 2080 | tf_op jit(solution)/shard_map/ppermute | solution.py:22
  218.2 4.2 %all-to-all-start = ((bf16[2,256,512]{1,2,0:T(8,128)(2,1)}), bf16[2,256,512]{1,2,0:T(8,128)(2,1)}, u32[]{:S(2)}, u32[]{:S(2)}) async-start(bf16[2,256,512]{1,2,0:T(8,128)(2,1)} %broadcast_in_dim.204), calls=%async_computation | async-start | bytes 1048576 | tf_op jit(solution)/shard_map/all_to_all | solution.py:158
  225.1 2.8 %broadcast_select_fusion.4 = f32[4,128,256]{2,1,0:T(8,128)} fusion(pred[]{:T(512)} %compare_reduce_fusion.2, bf16[256,4,128]{0,2,1:T(8,128)(2,1)S(1)} %bitcast.156, bf16[4,256,511]{2,1,0:T(8,128)(2,1)} %reshape.185), kind=kOutput, calls=%fused_computation.90 | convolution fusion | flops 67239936 | bytes 1311232 | tf_op jit(solution)/shard_map/gst,tgc->sgc/dot_general | solution.py:64
  233.5 4.2 %all-to-all-done = bf16[2,256,512]{1,2,0:T(8,128)(2,1)} async-done(((bf16[2,256,512]{1,2,0:T(8,128)(2,1)}), bf16[2,256,512]{1,2,0:T(8,128)(2,1)}, u32[]{:S(2)}, u32[]{:S(2)}) %all-to-all-start) | async-done | bytes 524320 | tf_op jit(solution)/shard_map/all_to_all | solution.py:158
  240.3 4.6 %all-to-all-start.1 = ((bf16[4,2,256,512]{2,3,1,0:T(8,128)(2,1)}), bf16[4,2,256,512]{2,3,1,0:T(8,128)(2,1)}, u32[]{:S(2)}, u32[]{:S(2)}) async-start(bf16[4,2,256,512]{2,3,1,0:T(8,128)(2,1)} %broadcast_in_dim.205), calls=%async_computation.1 | async-start | bytes 4194304 | tf_op jit(solution)/shard_map/all_to_all | solution.py:161
  255.0 5.4 %collective-permute-done.14 = bf16[2,512]{0,1:T(8,128)(2,1)S(1)} collective-permute-done((bf16[2,512]{0,1:T(8,128)(2,1)S(1)}, bf16[2,512]{0,1:T(8,128)(2,1)S(1)}, u32[]{:S(2)}, u32[]{:S(2)}) %collective-permute-start.14) | collective-permute-done | bytes 2080 | tf_op jit(solution)/shard_map/ppermute | solution.py:22
  265.0 2.7 collective-permute-done.13
  272.3 3.1 %fusion = bf16[256,512]{1,0:T(8,128)(2,1)} fusion(f32[256,512]{1,0:T(8,128)S(1)} %fusion.41, bf16[256,2048]{0,1:T(8,128)(2,1)S(1)} %bitcast.158, bf16[2048,512]{1,0:T(8,128)(2,1)} %collective-permute-done.8), kind=kOutput, calls=%fused_computation.3 | convolution fusion | flops 537133056 | bytes 3932160 | tf_op jit(solution)/shard_map/dot_general | solution.py:173
  (198 shorter events, 104.8 us)
Async XLA Ops:
  0.6 84.5 %copy-start = (bf16[256,512]{1,0:T(8,128)(2,1)S(1)}, bf16[256,512]{1,0:T(8,128)(2,1)}, u32[]{:S(2)}) copy-start(bf16[256,512]{1,0:T(8,128)(2,1)} %param.17) | copy-start | bytes 786436
  1.8 68.0 %copy-start.24 = (s32[256]{0:T(256)S(1)}, s32[256]{0:T(256)}, u32[]{:S(2)}) copy-start(s32[256]{0:T(256)} %param.16) | copy-start | bytes 3076
  1.8 77.6 %copy-start.21 = (bf16[256,512]{1,0:T(8,128)(2,1)S(1)}, bf16[256,512]{1,0:T(8,128)(2,1)}, u32[]{:S(2)}) copy-start(bf16[256,512]{1,0:T(8,128)(2,1)} %param.10) | copy-start | bytes 786436
  1.8 81.7 %copy-start.22 = (bf16[256,512]{1,0:T(8,128)(2,1)S(1)}, bf16[256,512]{1,0:T(8,128)(2,1)}, u32[]{:S(2)}) copy-start(bf16[256,512]{1,0:T(8,128)(2,1)} %param.11) | copy-start | bytes 786436
  1.8 82.5 %copy-start.25 = (bf16[4,768]{1,0:T(4,128)(2,1)S(1)}, bf16[4,768]{1,0:T(4,128)(2,1)}, u32[]{:S(2)}) copy-start(bf16[4,768]{1,0:T(4,128)(2,1)} %param.13) | copy-start | bytes 18436
  63.6 22.2 %collective-permute-start.8 = (bf16[2048,512]{1,0:T(8,128)(2,1)S(1)}, bf16[2048,512]{1,0:T(8,128)(2,1)}, u32[]{:S(2)}, u32[]{:S(2)}) collective-permute-start(bf16[2048,512]{1,0:T(8,128)(2,1)S(1)} %bitcast.147), channel_id=1, source_target_pairs={{0,8},{8,0},{1,9},{9,1},{2,10},{10,2},{3,11},{11,3},{4,12},{12,4},... | collective-permute-start | bytes 6291464 | tf_op jit(solution)/shard_map/ppermute | solution.py:15
  70.4 35.9 %collective-permute-start.4 = (s32[2]{0:T(128)}, s32[2]{0:T(128)}, u32[]{:S(2)}, u32[]{:S(2)}) collective-permute-start(s32[2]{0:T(128)} %get-tuple-element.63), channel_id=1, source_target_pairs={{8,0},{16,8},{24,16},{32,24},{40,32},{48,40},{56,48},{64,56},{72,6... | collective-permute-start | bytes 32 | tf_op jit(solution)/shard_map/ppermute | solution.py:22
  72.3 34.6 %collective-permute-start = (s32[2]{0:T(128)}, s32[2]{0:T(128)}, u32[]{:S(2)}, u32[]{:S(2)}) collective-permute-start(s32[2]{0:T(128)} %get-tuple-element.62), channel_id=1, source_target_pairs={{0,8},{8,16},{16,24},{24,32},{32,40},{40,48},{48,56},{56,64},{64,7... | collective-permute-start | bytes 32 | tf_op jit(solution)/shard_map/ppermute | solution.py:22
  77.4 116.6 %collective-permute-start.1 = (bf16[2,512]{0,1:T(8,128)(2,1)}, bf16[2,512]{0,1:T(8,128)(2,1)}, u32[]{:S(2)}, u32[]{:S(2)}) collective-permute-start(bf16[2,512]{0,1:T(8,128)(2,1)} %copy.57), channel_id=1, source_target_pairs={{0,8},{8,16},{16,24},{24,32},{32,40},{40,48},{48,56},{56,64},{64,7... | collective-permute-start | bytes 6152 | tf_op jit(solution)/shard_map/ppermute | solution.py:22
  80.2 30.6 %collective-permute-start.2 = (bf16[2,512]{0,1:T(8,128)(2,1)}, bf16[2,512]{0,1:T(8,128)(2,1)}, u32[]{:S(2)}, u32[]{:S(2)}) collective-permute-start(bf16[2,512]{0,1:T(8,128)(2,1)} %copy.60), channel_id=1, source_target_pairs={{0,8},{8,16},{16,24},{24,32},{32,40},{40,48},{48,56},{56,64},{64,7... | collective-permute-start | bytes 6152 | tf_op jit(solution)/shard_map/ppermute | solution.py:22
  85.8 25.0 %collective-permute-start.3 = (bf16[2,512]{0,1:T(8,128)(2,1)}, bf16[2,512]{0,1:T(8,128)(2,1)S(1)}, u32[]{:S(2)}, u32[]{:S(2)}) collective-permute-start(bf16[2,512]{0,1:T(8,128)(2,1)} %copy.63), channel_id=1, source_target_pairs={{0,8},{8,16},{16,24},{24,32},{32,40},{40,48},{48,56},{56,64},{64,7... | collective-permute-start | bytes 6152 | tf_op jit(solution)/shard_map/ppermute | solution.py:22
  92.9 62.4 %all-to-all-start.3 = ((f32[2,4,2,4,64,256]{5,4,3,0,2,1:T(8,128)}), f32[2,4,2,4,64,256]{5,4,3,0,2,1:T(8,128)}, u32[]{:S(2)}, u32[]{:S(2)}) async-start(f32[2,4,2,4,64,256]{5,4,3,0,2,1:T(8,128)} %copy.66), calls=%async_computation.3 | async-start | bytes 8388608 | tf_op jit(solution)/shard_map/all_to_all | solution.py:187
  114.0 37.4 %collective-permute-start.5 = (bf16[256,512]{0,1:T(8,128)(2,1)}, bf16[256,512]{0,1:T(8,128)(2,1)S(1)}, u32[]{:S(2)}, u32[]{:S(2)}) collective-permute-start(bf16[256,512]{0,1:T(8,128)(2,1)} %get-tuple-element.22), channel_id=1, source_target_pairs={{0,8},{8,16},{16,24},{24,32},{32,40},{40,48},{48,56},{56,64},{64,7... | collective-permute-start | bytes 786440 | tf_op jit(solution)/shard_map/ppermute | solution.py:22
  152.1 19.3 %collective-permute-start.6 = (bf16[256,512]{0,1:T(8,128)(2,1)}, bf16[256,512]{0,1:T(8,128)(2,1)}, u32[]{:S(2)}, u32[]{:S(2)}) collective-permute-start(bf16[256,512]{0,1:T(8,128)(2,1)} %broadcast_select_fusion.11), channel_id=1, source_target_pairs={{0,8},{8,16},{16,24},{24,32},{32,40},{40,48},{48,56},{56,64},{64,7... | collective-permute-start | bytes 786440 | tf_op jit(solution)/shard_map/ppermute | solution.py:22
  161.3 29.3 %all-to-all-start.4 = ((f32[2,2,4,64,256]{4,3,2,1,0:T(8,128)}), f32[2,2,4,64,256]{4,3,2,1,0:T(8,128)}, u32[]{:S(2)}, u32[]{:S(2)}) async-start(f32[2,2,4,64,256]{4,3,2,1,0:T(8,128)} %copy.68), calls=%async_computation.4 | async-start | bytes 2097152 | tf_op jit(solution)/shard_map/all_to_all | solution.py:188
  172.4 9.4 %collective-permute-start.7 = (bf16[256,512]{0,1:T(8,128)(2,1)S(1)}, bf16[256,512]{0,1:T(8,128)(2,1)S(1)}, u32[]{:S(2)}, u32[]{:S(2)}) collective-permute-start(bf16[256,512]{0,1:T(8,128)(2,1)S(1)} %broadcast_select_fusion.10), channel_id=1, source_target_pairs={{0,8},{8,16},{16,24},{24,32},{32,40},{40,48},{48,56},{56,64},{64,7... | collective-permute-start | bytes 786440 | tf_op jit(solution)/shard_map/ppermute | solution.py:22
  196.4 26.0 %collective-permute-start.10 = (bf16[256,512]{0,1:T(8,128)(2,1)}, bf16[256,512]{0,1:T(8,128)(2,1)S(1)}, u32[]{:S(2)}, u32[]{:S(2)}) collective-permute-start(bf16[256,512]{0,1:T(8,128)(2,1)} %get-tuple-element.18), channel_id=1, source_target_pairs={{8,0},{16,8},{24,16},{32,24},{40,32},{48,40},{56,48},{64,56},{72,6... | collective-permute-start | bytes 786440 | tf_op jit(solution)/shard_map/ppermute | solution.py:22
  208.5 6.3 %collective-permute-start.9 = (bf16[2,512]{0,1:T(8,128)(2,1)S(1)}, bf16[2,512]{0,1:T(8,128)(2,1)S(1)}, u32[]{:S(2)}, u32[]{:S(2)}) collective-permute-start(bf16[2,512]{0,1:T(8,128)(2,1)S(1)} %slice.306), channel_id=1, source_target_pairs={{8,0},{16,8},{24,16},{32,24},{40,32},{48,40},{56,48},{64,56},{72,6... | collective-permute-start | bytes 6152 | tf_op jit(solution)/shard_map/ppermute | solution.py:22
  218.2 19.6 %all-to-all-start = ((bf16[2,256,512]{1,2,0:T(8,128)(2,1)}), bf16[2,256,512]{1,2,0:T(8,128)(2,1)}, u32[]{:S(2)}, u32[]{:S(2)}) async-start(bf16[2,256,512]{1,2,0:T(8,128)(2,1)} %broadcast_in_dim.204), calls=%async_computation | async-start | bytes 1048576 | tf_op jit(solution)/shard_map/all_to_all | solution.py:158
  222.4 7.7 %collective-permute-start.11 = (bf16[256,512]{0,1:T(8,128)(2,1)S(1)}, bf16[256,512]{0,1:T(8,128)(2,1)S(1)}, u32[]{:S(2)}, u32[]{:S(2)}) collective-permute-start(bf16[256,512]{0,1:T(8,128)(2,1)S(1)} %broadcast_select_fusion.9), channel_id=1, source_target_pairs={{8,0},{16,8},{24,16},{32,24},{40,32},{48,40},{56,48},{64,56},{72,6... | collective-permute-start | bytes 786440 | tf_op jit(solution)/shard_map/ppermute | solution.py:22
  231.6 16.1 %collective-permute-start.12 = (bf16[256,512]{0,1:T(8,128)(2,1)}, bf16[256,512]{0,1:T(8,128)(2,1)}, u32[]{:S(2)}, u32[]{:S(2)}) collective-permute-start(bf16[256,512]{0,1:T(8,128)(2,1)} %broadcast_select_fusion.8), channel_id=1, source_target_pairs={{8,0},{16,8},{24,16},{32,24},{40,32},{48,40},{56,48},{64,56},{72,6... | collective-permute-start | bytes 786440 | tf_op jit(solution)/shard_map/ppermute | solution.py:22
  240.3 29.4 %all-to-all-start.1 = ((bf16[4,2,256,512]{2,3,1,0:T(8,128)(2,1)}), bf16[4,2,256,512]{2,3,1,0:T(8,128)(2,1)}, u32[]{:S(2)}, u32[]{:S(2)}) async-start(bf16[4,2,256,512]{2,3,1,0:T(8,128)(2,1)} %broadcast_in_dim.205), calls=%async_computation.1 | async-start | bytes 4194304 | tf_op jit(solution)/shard_map/all_to_all | solution.py:161
  253.1 7.3 %collective-permute-start.14 = (bf16[2,512]{0,1:T(8,128)(2,1)S(1)}, bf16[2,512]{0,1:T(8,128)(2,1)S(1)}, u32[]{:S(2)}, u32[]{:S(2)}) collective-permute-start(bf16[2,512]{0,1:T(8,128)(2,1)S(1)} %slice.312), channel_id=1, source_target_pairs={{8,0},{16,8},{24,16},{32,24},{40,32},{48,40},{56,48},{64,56},{72,6... | collective-permute-start | bytes 6152 | tf_op jit(solution)/shard_map/ppermute | solution.py:22
  261.4 6.3 %collective-permute-start.13 = (bf16[2,512]{0,1:T(8,128)(2,1)S(1)}, bf16[2,512]{0,1:T(8,128)(2,1)S(1)}, u32[]{:S(2)}, u32[]{:S(2)}) collective-permute-start(bf16[2,512]{0,1:T(8,128)(2,1)S(1)} %slice.309), channel_id=1, source_target_pairs={{8,0},{16,8},{24,16},{32,24},{40,32},{48,40},{56,48},{64,56},{72,6... | collective-permute-start | bytes 6152 | tf_op jit(solution)/shard_map/ppermute | solution.py:22
  (42 other events, 457.6 us)

commit v6 on v2

--- a/solution.py
+++ b/solution.py
@@ -170,14 +170,15 @@
     )
     dims = (((1,), (1,)), ((), ()))
     block_chips = chip_count // ch_count
-    part_mine = lax.dot_general(
-        weight_rows, out_grad, dims, preferred_element_type=jnp.float32
-    ).reshape(ch_count, 1, block_chips, -1, row_count)
-    part_other = lax.dot_general(
-        weight_rows_other, out_grad, dims, preferred_element_type=jnp.float32
-    ).reshape(ch_count, 1, block_chips, -1, row_count)
-    sent = jnp.concatenate([part_mine, part_other], axis=1)
-    summed = jnp.sum(lax.all_to_all(sent, CH, 0, 0, tiled=True), axis=0)
+
+    def summed_over_ch(weight_half):
+        part = lax.dot_general(weight_half, out_grad, dims, preferred_element_type=jnp.float32)
+        received = lax.all_to_all(
+            part.reshape(ch_count, block_chips, -1, row_count), CH, 0, 0, tiled=True
+        )
+        return jnp.sum(received, axis=0)
+
+    summed = (summed_over_ch(weight_rows), summed_over_ch(weight_rows_other))
     cols_mine, cols_other = summed[0][:, None], summed[1][:, None]
     grad_cols = jnp.where(
         on_first,

time: 275 us -> 302 us (1.098)
  the two profiles are of different devices: /device:TPU:1 before, /device:TPU:443 now
where the time goes in v6:
time: 302 us; the launch traced here: 300 us
  starting transfers between devices  69.4 us (23%)
  waiting for transfers between devices  66.6 us (22%)
  blocking collectives  56.7 us (19%)
  local copies, waits for them, and re-layouts  50.9 us (17%)
  other arithmetic  28.6 us (9%)
  matrix products  23.2 us (8%)
  between operations  5.1 us (2%)
    all_to_all x1, blocking collectives, gather_weight(): lax.all_to_all(spread, CHIPS, 0, 0, tiled=True)  56.7 us
    ppermute x14, waiting for transfers between devices, shifted(): return lax.ppermute(array, axis, pairs)  49.1 us
    ppermute x14, starting transfers between devices, shifted(): return lax.ppermute(array, axis, pairs)  37.4 us
    unnamed x90, local copies, waits for them, and re-layouts  21.1 us
    all_to_all x2, starting transfers between devices, summed_over_ch(): lax.all_to_all(part.reshape(ch_count, block_chips, -1, row_count), CH, 0,...  18.6 us
    all_to_all x2, waiting for transfers between devices, summed_over_ch(): lax.all_to_all(part.reshape(ch_count, block_chips, -1, row_count), CH, 0,...  17.4 us
    reshape x4, local copies, waits for them, and re-layouts, toeplitz_tiles(): repeated.reshape(group_count, row_count, 2 * row_count - 1)  15.2 us
    all_to_all x1, starting transfers between devices, local(): lax.all_to_all(spread, CH, 0, 0, tiled=True)  9.07 us
  transfers between devices with their start and end apart: 18, of which 9 were waited for; matrix products, arithmetic and copies ran while one was open for 29% of the time, Pallas kernels for 0%

profile of v6, /device:TPU:443, one launch (start us, length us, event | category | flops | bytes accessed | tf_op | source)
XLA Modules:
  0.0 300.4 jit_solution(12587565506313541508)
XLA Ops:
  1.8 56.7 %all_to_all.20 = bf16[32,64,512]{2,1,0:T(8,128)(2,1)S(1)} all-to-all(bf16[32,64,512]{2,1,0:T(8,128)(2,1)S(1)} %broadcast_in_dim.205), channel_id=1, replica_groups=mesh['zl'=4,'y'=8,'core'=2,'zh'=2,'x'=4] {'zl','y'}, dimensions={0} | all-to-all | bytes 4194304 | tf_op jit(solution)/shard_map/all_to_all | solution.py:14
  60.6 9.2 %all-to-all-start.2 = ((f32[8,4,64,256]{3,2,1,0:T(8,128)}), f32[8,4,64,256]{3,2,1,0:T(8,128)S(1)}, u32[]{:S(2)}, u32[]{:S(2)}) async-start(f32[8,4,64,256]{3,2,1,0:T(8,128)} %fusion.29), calls=%async_computation.2 | async-start | bytes 4194304 | tf_op jit(solution)/shard_map/all_to_all | solution.py:176
  69.8 4.4 %collective-permute-start.8 = (bf16[2048,512]{1,0:T(8,128)(2,1)}, bf16[2048,512]{1,0:T(8,128)(2,1)}, u32[]{:S(2)}, u32[]{:S(2)}) collective-permute-start(bf16[2048,512]{1,0:T(8,128)(2,1)} %bitcast.140), channel_id=1, source_target_pairs={{0,8},{8,0},{1,9},{9,1},{2,10},{10,2},{3,11},{11,3},{4,12},{12,4},... | collective-permute-start | bytes 6291464 | tf_op jit(solution)/shard_map/ppermute | solution.py:15
  76.7 5.8 %collective-permute-start = (s32[2]{0:T(128)}, s32[2]{0:T(128)}, u32[]{:S(2)}, u32[]{:S(2)}) collective-permute-start(s32[2]{0:T(128)} %get-tuple-element.52), channel_id=1, source_target_pairs={{0,8},{8,16},{16,24},{24,32},{32,40},{40,48},{48,56},{56,64},{64,7... | collective-permute-start | bytes 32 | tf_op jit(solution)/shard_map/ppermute | solution.py:22
  95.4 3.7 %fusion.43 = f32[2048,256]{1,0:T(8,128)} fusion(bf16[2048,512]{1,0:T(8,128)(2,1)} %collective-permute-done.8, bf16[256,512]{1,0:T(8,128)(2,1)S(1)} %copy-done), kind=kOutput, calls=%fused_computation.123 | convolution fusion | flops 536870912 | bytes 4456448 | tf_op jit(solution)/shard_map/dot_general | solution.py:175
  99.1 17.4 %all-to-all-done.2 = f32[8,4,64,256]{3,2,1,0:T(8,128)S(1)} async-done(((f32[8,4,64,256]{3,2,1,0:T(8,128)}), f32[8,4,64,256]{3,2,1,0:T(8,128)S(1)}, u32[]{:S(2)}, u32[]{:S(2)}) %all-to-all-start.2) | async-done | bytes 2097184 | tf_op jit(solution)/shard_map/all_to_all | solution.py:176
  116.5 9.4 %all-to-all-start.3 = ((f32[8,4,64,256]{3,2,1,0:T(8,128)}), f32[8,4,64,256]{3,2,1,0:T(8,128)}, u32[]{:S(2)}, u32[]{:S(2)}) async-start(f32[8,4,64,256]{3,2,1,0:T(8,128)} %bitcast.34), calls=%async_computation.3 | async-start | bytes 4194304 | tf_op jit(solution)/shard_map/all_to_all | solution.py:176
  138.1 3.3 %select_select_fusion.1 = (bf16[256,512]{0,1:T(8,128)(2,1)}, bf16[256,512]{0,1:T(8,128)(2,1)}) fusion(pred[256]{0:T(512)(128)(4,1)} %get-tuple-element.41, pred[]{:T(512)S(6)} %eq.69, bf16[256,512]{0,1:T(8,128)(2,1)} %copy.35, bf16[2,512]{0,1:T(8,128)(2,1)S(1)} %collective-permute-done.3, f32[512]{0:T(512)} %bitcast.174, f32[512]{0:T(512)} %bitcast.176, ...), kind=kLoop, calls=%fused_computation.91 | loop fusion | flops 4718592 | bytes 1065729 | tf_op jit(solution)/shard_map/jit(_where)/select_n | solution.py:143
  147.7 3.0 %reshape.172 = bf16[4,256,511]{2,1,0:T(8,128)(2,1)S(1)} reshape(bf16[4,130816]{1,0:T(4,128)(2,1)} %slice.292) | data formatting | bytes 2093056 | tf_op jit(solution)/shard_map/reshape | solution.py:48
  154.5 4.0 %reshape.170 = bf16[4,256,511]{2,1,0:T(8,128)(2,1)} reshape(bf16[4,130816]{1,0:T(4,128)(2,1)} %slice.290) | data formatting | bytes 2093056 | tf_op jit(solution)/shard_map/reshape | solution.py:48
  161.9 4.0 %reshape.168 = bf16[4,256,511]{2,1,0:T(8,128)(2,1)} reshape(bf16[4,130816]{1,0:T(4,128)(2,1)} %slice.288) | data formatting | bytes 2093056 | tf_op jit(solution)/shard_map/reshape | solution.py:48
  169.3 4.1 %reshape.165 = bf16[4,256,511]{2,1,0:T(8,128)(2,1)} reshape(bf16[4,130816]{1,0:T(4,128)(2,1)} %slice.286) | data formatting | bytes 2093056 | tf_op jit(solution)/shard_map/reshape | solution.py:48
  179.4 2.6 broadcast_select_fusion.7
  182.0 9.2 %collective-permute-done.6 = bf16[256,512]{0,1:T(8,128)(2,1)S(1)} collective-permute-done((bf16[256,512]{0,1:T(8,128)(2,1)S(1)}, bf16[256,512]{0,1:T(8,128)(2,1)S(1)}, u32[]{:S(2)}, u32[]{:S(2)}) %collective-permute-start.6) | collective-permute-done | bytes 262176 | tf_op jit(solution)/shard_map/ppermute | solution.py:22
  195.8 4.1 %collective-permute-done.7 = bf16[256,512]{0,1:T(8,128)(2,1)S(1)} collective-permute-done((bf16[256,512]{0,1:T(8,128)(2,1)S(1)}, bf16[256,512]{0,1:T(8,128)(2,1)S(1)}, u32[]{:S(2)}, u32[]{:S(2)}) %collective-permute-start.7) | collective-permute-done | bytes 262176 | tf_op jit(solution)/shard_map/ppermute | solution.py:22
  205.9 6.7 %collective-permute-start.9 = (bf16[2,512]{0,1:T(8,128)(2,1)S(1)}, bf16[2,512]{0,1:T(8,128)(2,1)S(1)}, u32[]{:S(2)}, u32[]{:S(2)}) collective-permute-start(bf16[2,512]{0,1:T(8,128)(2,1)S(1)} %slice.296), channel_id=1, source_target_pairs={{8,0},{16,8},{24,16},{32,24},{40,32},{48,40},{56,48},{64,56},{72,6... | collective-permute-start | bytes 6152 | tf_op jit(solution)/shard_map/ppermute | solution.py:22
  218.4 9.1 %all-to-all-start = ((bf16[8,256,512]{1,2,0:T(8,128)(2,1)}), bf16[8,256,512]{1,2,0:T(8,128)(2,1)S(1)}, u32[]{:S(2)}, u32[]{:S(2)}) async-start(bf16[8,256,512]{1,2,0:T(8,128)(2,1)} %broadcast_in_dim.204), calls=%async_computation | async-start | bytes 4194304 | tf_op jit(solution)/shard_map/all_to_all | solution.py:157
  231.6 3.4 %collective-permute-start.10 = (bf16[256,512]{0,1:T(8,128)(2,1)}, bf16[256,512]{0,1:T(8,128)(2,1)}, u32[]{:S(2)}, u32[]{:S(2)}) collective-permute-start(bf16[256,512]{0,1:T(8,128)(2,1)} %get-tuple-element.10), channel_id=1, source_target_pairs={{8,0},{16,8},{24,16},{32,24},{40,32},{48,40},{56,48},{64,56},{72,6... | collective-permute-start | bytes 786440 | tf_op jit(solution)/shard_map/ppermute | solution.py:22
  236.5 8.1 %collective-permute-done.10 = bf16[256,512]{0,1:T(8,128)(2,1)} collective-permute-done((bf16[256,512]{0,1:T(8,128)(2,1)}, bf16[256,512]{0,1:T(8,128)(2,1)}, u32[]{:S(2)}, u32[]{:S(2)}) %collective-permute-start.10) | collective-permute-done | bytes 262176 | tf_op jit(solution)/shard_map/ppermute | solution.py:22
  250.3 6.6 %collective-permute-done.11 = bf16[256,512]{0,1:T(8,128)(2,1)S(1)} collective-permute-done((bf16[256,512]{0,1:T(8,128)(2,1)S(1)}, bf16[256,512]{0,1:T(8,128)(2,1)S(1)}, u32[]{:S(2)}, u32[]{:S(2)}) %collective-permute-start.11) | collective-permute-done | bytes 262176 | tf_op jit(solution)/shard_map/ppermute | solution.py:22
  260.6 9.2 %collective-permute-done.12 = bf16[256,512]{0,1:T(8,128)(2,1)S(1)} collective-permute-done((bf16[256,512]{0,1:T(8,128)(2,1)S(1)}, bf16[256,512]{0,1:T(8,128)(2,1)S(1)}, u32[]{:S(2)}, u32[]{:S(2)}) %collective-permute-start.12) | collective-permute-done | bytes 262176 | tf_op jit(solution)/shard_map/ppermute | solution.py:22
  275.3 6.5 %collective-permute-done.14 = bf16[2,512]{0,1:T(8,128)(2,1)S(1)} collective-permute-done((bf16[2,512]{0,1:T(8,128)(2,1)S(1)}, bf16[2,512]{0,1:T(8,128)(2,1)S(1)}, u32[]{:S(2)}, u32[]{:S(2)}) %collective-permute-start.14) | collective-permute-done | bytes 2080 | tf_op jit(solution)/shard_map/ppermute | solution.py:22
  286.3 4.8 %collective-permute-done.13 = bf16[2,512]{0,1:T(8,128)(2,1)S(1)} collective-permute-done((bf16[2,512]{0,1:T(8,128)(2,1)S(1)}, bf16[2,512]{0,1:T(8,128)(2,1)S(1)}, u32[]{:S(2)}, u32[]{:S(2)}) %collective-permute-start.13) | collective-permute-done | bytes 2080 | tf_op jit(solution)/shard_map/ppermute | solution.py:22
  297.4 3.0 %fusion = bf16[256,512]{1,0:T(8,128)(2,1)} fusion(f32[256,512]{1,0:T(8,128)S(1)} %fusion.42, bf16[256,2048]{0,1:T(8,128)(2,1)S(1)} %bitcast.149, bf16[2048,512]{1,0:T(8,128)(2,1)} %collective-permute-done.8), kind=kOutput, calls=%fused_computation.1 | convolution fusion | flops 537133056 | bytes 3932160 | tf_op jit(solution)/shard_map/dot_general | solution.py:168
  (172 shorter events, 97.0 us)
Async XLA Ops:
  0.6 57.8 %copy-start = (bf16[256,512]{1,0:T(8,128)(2,1)S(1)}, bf16[256,512]{1,0:T(8,128)(2,1)}, u32[]{:S(2)}) copy-start(bf16[256,512]{1,0:T(8,128)(2,1)} %param.17) | copy-start | bytes 786436
  60.6 30.4 %copy-start.19 = (bf16[4,768]{1,0:T(4,128)(2,1)S(1)}, bf16[4,768]{1,0:T(4,128)(2,1)}, u32[]{:S(2)}) copy-start(bf16[4,768]{1,0:T(4,128)(2,1)} %param.13) | copy-start | bytes 18436
  60.6 31.1 %copy-start.29 = (f32[3,3,512]{2,1,0:T(4,128)S(1)}, f32[3,3,512]{2,1,0:T(4,128)}, u32[]{:S(2)}) copy-start(f32[3,3,512]{2,1,0:T(4,128)} %param.12) | copy-start | bytes 55300
  60.6 55.9 %all-to-all-start.2 = ((f32[8,4,64,256]{3,2,1,0:T(8,128)}), f32[8,4,64,256]{3,2,1,0:T(8,128)S(1)}, u32[]{:S(2)}, u32[]{:S(2)}) async-start(f32[8,4,64,256]{3,2,1,0:T(8,128)} %fusion.29), calls=%async_computation.2 | async-start | bytes 4194304 | tf_op jit(solution)/shard_map/all_to_all | solution.py:176
  69.8 23.6 %collective-permute-start.8 = (bf16[2048,512]{1,0:T(8,128)(2,1)}, bf16[2048,512]{1,0:T(8,128)(2,1)}, u32[]{:S(2)}, u32[]{:S(2)}) collective-permute-start(bf16[2048,512]{1,0:T(8,128)(2,1)} %bitcast.140), channel_id=1, source_target_pairs={{0,8},{8,0},{1,9},{9,1},{2,10},{10,2},{3,11},{11,3},{4,12},{12,4},... | collective-permute-start | bytes 6291464 | tf_op jit(solution)/shard_map/ppermute | solution.py:15
  74.8 58.9 %collective-permute-start.4 = (s32[2]{0:T(128)}, s32[2]{0:T(128)}, u32[]{:S(2)}, u32[]{:S(2)}) collective-permute-start(s32[2]{0:T(128)} %get-tuple-element.53), channel_id=1, source_target_pairs={{8,0},{16,8},{24,16},{32,24},{40,32},{48,40},{56,48},{64,56},{72,6... | collective-permute-start | bytes 32 | tf_op jit(solution)/shard_map/ppermute | solution.py:22
  76.7 57.6 %collective-permute-start = (s32[2]{0:T(128)}, s32[2]{0:T(128)}, u32[]{:S(2)}, u32[]{:S(2)}) collective-permute-start(s32[2]{0:T(128)} %get-tuple-element.52), channel_id=1, source_target_pairs={{0,8},{8,16},{16,24},{24,32},{32,40},{40,48},{48,56},{56,64},{64,7... | collective-permute-start | bytes 32 | tf_op jit(solution)/shard_map/ppermute | solution.py:22
  83.9 129.8 %collective-permute-start.1 = (bf16[2,512]{0,1:T(8,128)(2,1)}, bf16[2,512]{0,1:T(8,128)(2,1)}, u32[]{:S(2)}, u32[]{:S(2)}) collective-permute-start(bf16[2,512]{0,1:T(8,128)(2,1)} %copy.30), channel_id=1, source_target_pairs={{0,8},{8,16},{16,24},{24,32},{32,40},{40,48},{48,56},{56,64},{64,7... | collective-permute-start | bytes 6152 | tf_op jit(solution)/shard_map/ppermute | solution.py:22
  87.4 50.7 %collective-permute-start.2 = (bf16[2,512]{0,1:T(8,128)(2,1)}, bf16[2,512]{0,1:T(8,128)(2,1)}, u32[]{:S(2)}, u32[]{:S(2)}) collective-permute-start(bf16[2,512]{0,1:T(8,128)(2,1)} %copy.33), channel_id=1, source_target_pairs={{0,8},{8,16},{16,24},{24,32},{32,40},{40,48},{48,56},{56,64},{64,7... | collective-permute-start | bytes 6152 | tf_op jit(solution)/shard_map/ppermute | solution.py:22
  93.5 44.7 %collective-permute-start.3 = (bf16[2,512]{0,1:T(8,128)(2,1)}, bf16[2,512]{0,1:T(8,128)(2,1)S(1)}, u32[]{:S(2)}, u32[]{:S(2)}) collective-permute-start(bf16[2,512]{0,1:T(8,128)(2,1)} %copy.36), channel_id=1, source_target_pairs={{0,8},{8,16},{16,24},{24,32},{32,40},{40,48},{48,56},{56,64},{64,7... | collective-permute-start | bytes 6152 | tf_op jit(solution)/shard_map/ppermute | solution.py:22
  116.5 86.0 %all-to-all-start.3 = ((f32[8,4,64,256]{3,2,1,0:T(8,128)}), f32[8,4,64,256]{3,2,1,0:T(8,128)}, u32[]{:S(2)}, u32[]{:S(2)}) async-start(f32[8,4,64,256]{3,2,1,0:T(8,128)} %bitcast.34), calls=%async_computation.3 | async-start | bytes 4194304 | tf_op jit(solution)/shard_map/all_to_all | solution.py:176
  141.5 34.3 %collective-permute-start.5 = (bf16[256,512]{0,1:T(8,128)(2,1)}, bf16[256,512]{0,1:T(8,128)(2,1)}, u32[]{:S(2)}, u32[]{:S(2)}) collective-permute-start(bf16[256,512]{0,1:T(8,128)(2,1)} %get-tuple-element.14), channel_id=1, source_target_pairs={{0,8},{8,16},{16,24},{24,32},{32,40},{40,48},{48,56},{56,64},{64,7... | collective-permute-start | bytes 786440 | tf_op jit(solution)/shard_map/ppermute | solution.py:22
  150.8 49.8 %copy-start.4 = (bf16[4,256,511]{2,1,0:T(8,128)(2,1)}, bf16[4,256,511]{2,1,0:T(8,128)(2,1)S(1)}, u32[]{:S(2)}) copy-start(bf16[4,256,511]{2,1,0:T(8,128)(2,1)S(1)} %reshape.172) | copy-start | bytes 3139588
  175.8 15.5 %collective-permute-start.6 = (bf16[256,512]{0,1:T(8,128)(2,1)S(1)}, bf16[256,512]{0,1:T(8,128)(2,1)S(1)}, u32[]{:S(2)}, u32[]{:S(2)}) collective-permute-start(bf16[256,512]{0,1:T(8,128)(2,1)S(1)} %broadcast_select_fusion.11), channel_id=1, source_target_pairs={{0,8},{8,16},{16,24},{24,32},{32,40},{40,48},{48,56},{56,64},{64,7... | collective-permute-start | bytes 786440 | tf_op jit(solution)/shard_map/ppermute | solution.py:22
  191.3 8.6 %collective-permute-start.7 = (bf16[256,512]{0,1:T(8,128)(2,1)S(1)}, bf16[256,512]{0,1:T(8,128)(2,1)S(1)}, u32[]{:S(2)}, u32[]{:S(2)}) collective-permute-start(bf16[256,512]{0,1:T(8,128)(2,1)S(1)} %broadcast_select_fusion.10), channel_id=1, source_target_pairs={{0,8},{8,16},{16,24},{24,32},{32,40},{40,48},{48,56},{56,64},{64,7... | collective-permute-start | bytes 786440 | tf_op jit(solution)/shard_map/ppermute | solution.py:22
  205.9 8.4 %collective-permute-start.9 = (bf16[2,512]{0,1:T(8,128)(2,1)S(1)}, bf16[2,512]{0,1:T(8,128)(2,1)S(1)}, u32[]{:S(2)}, u32[]{:S(2)}) collective-permute-start(bf16[2,512]{0,1:T(8,128)(2,1)S(1)} %slice.296), channel_id=1, source_target_pairs={{8,0},{16,8},{24,16},{32,24},{40,32},{48,40},{56,48},{64,56},{72,6... | collective-permute-start | bytes 6152 | tf_op jit(solution)/shard_map/ppermute | solution.py:22
  218.4 74.7 %all-to-all-start = ((bf16[8,256,512]{1,2,0:T(8,128)(2,1)}), bf16[8,256,512]{1,2,0:T(8,128)(2,1)S(1)}, u32[]{:S(2)}, u32[]{:S(2)}) async-start(bf16[8,256,512]{1,2,0:T(8,128)(2,1)} %broadcast_in_dim.204), calls=%async_computation | async-start | bytes 4194304 | tf_op jit(solution)/shard_map/all_to_all | solution.py:157
  231.6 13.0 %collective-permute-start.10 = (bf16[256,512]{0,1:T(8,128)(2,1)}, bf16[256,512]{0,1:T(8,128)(2,1)}, u32[]{:S(2)}, u32[]{:S(2)}) collective-permute-start(bf16[256,512]{0,1:T(8,128)(2,1)} %get-tuple-element.10), channel_id=1, source_target_pairs={{8,0},{16,8},{24,16},{32,24},{40,32},{48,40},{56,48},{64,56},{72,6... | collective-permute-start | bytes 786440 | tf_op jit(solution)/shard_map/ppermute | solution.py:22
  235.0 24.6 %copy-start.7 = (bf16[4,256,511]{2,1,0:T(8,128)(2,1)S(1)}, bf16[4,256,511]{2,1,0:T(8,128)(2,1)}, u32[]{:S(2)}) copy-start(bf16[4,256,511]{2,1,0:T(8,128)(2,1)} %reshape.170) | copy-start | bytes 3139588
  244.6 25.8 %copy-start.5 = (bf16[4,256,511]{2,1,0:T(8,128)(2,1)S(1)}, bf16[4,256,511]{2,1,0:T(8,128)(2,1)}, u32[]{:S(2)}) copy-start(bf16[4,256,511]{2,1,0:T(8,128)(2,1)} %copy-done.4) | copy-start | bytes 3139588
  244.7 12.3 %collective-permute-start.11 = (bf16[256,512]{0,1:T(8,128)(2,1)S(1)}, bf16[256,512]{0,1:T(8,128)(2,1)S(1)}, u32[]{:S(2)}, u32[]{:S(2)}) collective-permute-start(bf16[256,512]{0,1:T(8,128)(2,1)S(1)} %broadcast_select_fusion.9), channel_id=1, source_target_pairs={{8,0},{16,8},{24,16},{32,24},{40,32},{48,40},{56,48},{64,56},{72,6... | collective-permute-start | bytes 786440 | tf_op jit(solution)/shard_map/ppermute | solution.py:22
  257.0 12.8 %collective-permute-start.12 = (bf16[256,512]{0,1:T(8,128)(2,1)S(1)}, bf16[256,512]{0,1:T(8,128)(2,1)S(1)}, u32[]{:S(2)}, u32[]{:S(2)}) collective-permute-start(bf16[256,512]{0,1:T(8,128)(2,1)S(1)} %broadcast_select_fusion.8), channel_id=1, source_target_pairs={{8,0},{16,8},{24,16},{32,24},{40,32},{48,40},{56,48},{64,56},{72,6... | collective-permute-start | bytes 786440 | tf_op jit(solution)/shard_map/ppermute | solution.py:22
  273.3 8.4 %collective-permute-start.14 = (bf16[2,512]{0,1:T(8,128)(2,1)S(1)}, bf16[2,512]{0,1:T(8,128)(2,1)S(1)}, u32[]{:S(2)}, u32[]{:S(2)}) collective-permute-start(bf16[2,512]{0,1:T(8,128)(2,1)S(1)} %slice.302), channel_id=1, source_target_pairs={{8,0},{16,8},{24,16},{32,24},{40,32},{48,40},{56,48},{64,56},{72,6... | collective-permute-start | bytes 6152 | tf_op jit(solution)/shard_map/ppermute | solution.py:22
  282.7 8.4 %collective-permute-start.13 = (bf16[2,512]{0,1:T(8,128)(2,1)S(1)}, bf16[2,512]{0,1:T(8,128)(2,1)S(1)}, u32[]{:S(2)}, u32[]{:S(2)}) collective-permute-start(bf16[2,512]{0,1:T(8,128)(2,1)S(1)} %slice.299), channel_id=1, source_target_pairs={{8,0},{16,8},{24,16},{32,24},{40,32},{48,40},{56,48},{64,56},{72,6... | collective-permute-start | bytes 6152 | tf_op jit(solution)/shard_map/ppermute | solution.py:22
  (32 other events, 329.0 us)

commit v7 on v2

--- a/solution.py
+++ b/solution.py
@@ -64,6 +64,15 @@
     return jnp.einsum(
         "gst,tgc->sgc", band_tile, grouped, preferred_element_type=jnp.float32
     ).reshape(row_count, channels)
+
+
+def tagged(rows, doc_id):
+    tag = jnp.full((1, rows.shape[1]), doc_id + 1, rows.dtype)
+    return jnp.concatenate([rows, tag])
+
+
+def untagged(block):
+    return block[:-1], block[-1, 0].astype(jnp.int32) - 1
 
 
 def causal_taps(extended, weights, ext_ids, doc_ids):
@@ -139,15 +148,14 @@
         return summand
 
     mixed = apply_forward(diagonal, gated) + skip_weight[None, :] * gated.astype(jnp.float32)
-    own_tail = jnp.where(tail_rows, gated, zero_half)
-    moving = jnp.where(joins_next, own_tail, zero_half)
+    own_tail = tagged(jnp.where(tail_rows, gated, zero_half), last_id)
     for distance in range(1, HOPS + 1):
-        moving = shifted(moving, CTX, 1)
-        is_live = jnp.any(moving != 0)
+        moving, source_id = untagged(shifted(own_tail, CTX, distance))
         mixed = mixed + jnp.where(
-            head_rows, cross_term(is_live, apply_forward, tiles_list[distance], moving), 0.0
-        )
-        moving = jnp.where(single_doc & joins_next, moving, zero_half)
+            head_rows & (source_id == first_id),
+            apply_forward(tiles_list[distance], moving),
+            0.0,
+        )
     pre_gate = (query_short * mixed).astype(jnp.bfloat16)
     pair_size = lax.axis_size("core")
     chip_count = lax.axis_size(CHIPS)
@@ -192,14 +200,14 @@
     grad_gated = apply_adjoint(diagonal, grad_mixed) + skip_weight[None, :] * grad_mixed.astype(
         jnp.float32
     )
-    moving_back = jnp.where(joins_prev, own_head, zero_half)
+    own_head = tagged(own_head, first_id)
     for distance in range(1, HOPS + 1):
-        moving_back = shifted(moving_back, CTX, -1)
-        is_live = jnp.any(moving_back != 0)
+        moving_back, source_id = untagged(shifted(own_head, CTX, -distance))
         grad_gated = grad_gated + jnp.where(
-            tail_rows, cross_term(is_live, apply_adjoint, tiles_list[distance], moving_back), 0.0
-        )
-        moving_back = jnp.where(single_doc & joins_prev, moving_back, zero_half)
+            tail_rows & (source_id == last_id),
+            apply_adjoint(tiles_list[distance], moving_back),
+            0.0,
+        )
     grad_key_short = (grad_gated * value_short).astype(jnp.bfloat16)
     grad_value_short = (grad_gated * key_short).astype(jnp.bfloat16)
     next_rows = shifted((grad_query_short[:2], grad_key_short[:2], grad_value_short[:2]), CTX, -1)

time: 275 us -> 345 us (1.25)
  the two profiles are of different devices: /device:TPU:1 before, /device:TPU:123 now
where the time goes in v7:
time: 345 us; the launch traced here: 343 us
  waiting for transfers between devices  117 us (34%)
  local copies, waits for them, and re-layouts  65.8 us (19%)
  starting transfers between devices  60.5 us (18%)
  blocking collectives  58.3 us (17%)
  other arithmetic  20.3 us (6%)
  matrix products  10.8 us (3%)
  between operations  10.6 us (3%)
    all_to_all x1, waiting for transfers between devices, local(): summed = jnp.sum(lax.all_to_all(sent, CH, 0, 0, tiled=True), axis=0)  69.3 us
    all_to_all x1, blocking collectives, gather_weight(): lax.all_to_all(spread, CHIPS, 0, 0, tiled=True)  58.3 us
    ppermute x14, starting transfers between devices, shifted(): return lax.ppermute(array, axis, pairs)  41.8 us
    ppermute x14, waiting for transfers between devices, shifted(): return lax.ppermute(array, axis, pairs)  34.3 us
    unnamed x114, local copies, waits for them, and re-layouts  19.7 us
    reshape x4, local copies, waits for them, and re-layouts, toeplitz_tiles(): repeated.reshape(group_count, row_count, 2 * row_count - 1)  16.3 us
    slice x12, local copies, waits for them, and re-layouts, untagged(): return (block[:-1], block[-1, 0].astype(jnp.int32) - 1)  12.7 us
    all_to_all x1, waiting for transfers between devices, local(): lax.all_to_all(spread, CH, 0, 0, tiled=True)  10.5 us
  transfers between devices with their start and end apart: 17, of which 9 were waited for; matrix products, arithmetic and copies ran while one was open for 21% of the time, Pallas kernels for 0%

profile of v7, /device:TPU:123, one launch (start us, length us, event | category | flops | bytes accessed | tf_op | source)
XLA Modules:
  0.0 343.4 jit_solution(518432941629793053)
XLA Ops:
  1.8 58.3 %all_to_all.15 = bf16[32,64,512]{2,1,0:T(8,128)(2,1)S(1)} all-to-all(bf16[32,64,512]{2,1,0:T(8,128)(2,1)S(1)} %broadcast_in_dim.198), channel_id=1, replica_groups=mesh['zl'=4,'y'=8,'core'=2,'zh'=2,'x'=4] {'zl','y'}, dimensions={0} | all-to-all | bytes 4194304 | tf_op jit(solution)/shard_map/all_to_all | solution.py:14
  60.1 4.0 %collective-permute-start.7 = (bf16[2048,512]{1,0:T(8,128)(2,1)S(1)}, bf16[2048,512]{1,0:T(8,128)(2,1)S(1)}, u32[]{:S(2)}, u32[]{:S(2)}) collective-permute-start(bf16[2048,512]{1,0:T(8,128)(2,1)S(1)} %bitcast.147), channel_id=1, source_target_pairs={{0,8},{8,0},{1,9},{9,1},{2,10},{10,2},{3,11},{11,3},{4,12},{12,4},... | collective-permute-start | bytes 6291464 | tf_op jit(solution)/shard_map/ppermute | solution.py:15
  64.8 3.0 collective-permute-done.7
  72.0 10.2 %all-to-all-start.2 = ((f32[8,2,4,64,256]{4,3,2,1,0:T(8,128)}), f32[8,2,4,64,256]{4,3,2,1,0:T(8,128)}, u32[]{:S(2)}, u32[]{:S(2)}) async-start(f32[8,2,4,64,256]{4,3,2,1,0:T(8,128)} %copy.50), calls=%async_computation.2 | async-start | bytes 8388608 | tf_op jit(solution)/shard_map/all_to_all | solution.py:188
  82.2 2.8 collective-permute-start.8
  85.1 4.8 %collective-permute-start = (s32[2]{0:T(128)S(1)}, s32[2]{0:T(128)S(1)}, u32[]{:S(2)}, u32[]{:S(2)}) collective-permute-start(s32[2]{0:T(128)S(1)} %get-tuple-element.54), channel_id=1, source_target_pairs={{0,8},{8,16},{16,24},{24,32},{32,40},{40,48},{48,56},{56,64},{64,7... | collective-permute-start | bytes 32 | tf_op jit(solution)/shard_map/ppermute | solution.py:22
  94.2 3.1 collective-permute-start.2
  108.2 69.3 %all-to-all-done.2 = f32[8,2,4,64,256]{4,3,2,1,0:T(8,128)} async-done(((f32[8,2,4,64,256]{4,3,2,1,0:T(8,128)}), f32[8,2,4,64,256]{4,3,2,1,0:T(8,128)}, u32[]{:S(2)}, u32[]{:S(2)}) %all-to-all-start.2) | async-done | bytes 4194336 | tf_op jit(solution)/shard_map/all_to_all | solution.py:188
  182.7 3.5 %collective-permute-start.10 = (bf16[257,512]{0,1:T(8,128)(2,1)}, bf16[257,512]{0,1:T(8,128)(2,1)}, u32[]{:S(2)}, u32[]{:S(2)}) collective-permute-start(bf16[257,512]{0,1:T(8,128)(2,1)} %concatenate.69), channel_id=1, source_target_pairs={{8,0},{16,8},{24,16},{32,24},{40,32},{48,40},{56,48},{64,56},{72,6... | collective-permute-start | bytes 789512 | tf_op jit(solution)/shard_map/ppermute | solution.py:22
  199.0 3.0 broadcast_select_fusion.3
  204.7 3.1 collective-permute-start.5
  207.8 4.1 %collective-permute-start.6 = (bf16[257,512]{0,1:T(8,128)(2,1)}, bf16[257,512]{0,1:T(8,128)(2,1)}, u32[]{:S(2)}, u32[]{:S(2)}) collective-permute-start(bf16[257,512]{0,1:T(8,128)(2,1)} %concatenate.60), channel_id=1, source_target_pairs={{0,24},{8,32},{16,40},{24,48},{32,56},{40,64},{48,72},{56,80},{64,... | collective-permute-start | bytes 789512 | tf_op jit(solution)/shard_map/ppermute | solution.py:22
  214.8 4.0 %reshape.200 = bf16[4,256,511]{2,1,0:T(8,128)(2,1)} reshape(bf16[4,130816]{1,0:T(4,128)(2,1)} %slice.342) | data formatting | bytes 2093056 | tf_op jit(solution)/shard_map/reshape | solution.py:48
  222.3 4.0 %reshape.197 = bf16[4,256,511]{2,1,0:T(8,128)(2,1)} reshape(bf16[4,130816]{1,0:T(4,128)(2,1)} %slice.338) | data formatting | bytes 2093056 | tf_op jit(solution)/shard_map/reshape | solution.py:48
  229.7 4.1 %reshape.203 = bf16[4,256,511]{2,1,0:T(8,128)(2,1)} reshape(bf16[4,130816]{1,0:T(4,128)(2,1)} %slice.346) | data formatting | bytes 2093056 | tf_op jit(solution)/shard_map/reshape | solution.py:48
  237.2 4.1 %reshape.194 = bf16[4,256,511]{2,1,0:T(8,128)(2,1)} reshape(bf16[4,130816]{1,0:T(4,128)(2,1)} %slice.334) | data formatting | bytes 2093056 | tf_op jit(solution)/shard_map/reshape | solution.py:48
  258.3 6.5 %collective-permute-done.9 = bf16[2,512]{0,1:T(8,128)(2,1)S(1)} collective-permute-done((bf16[2,512]{0,1:T(8,128)(2,1)S(1)}, bf16[2,512]{0,1:T(8,128)(2,1)S(1)}, u32[]{:S(2)}, u32[]{:S(2)}) %collective-permute-start.9) | collective-permute-done | bytes 2080 | tf_op jit(solution)/shard_map/ppermute | solution.py:22
  267.8 4.6 %all-to-all-start = ((bf16[8,256,512]{1,2,0:T(8,128)(2,1)}), bf16[8,256,512]{1,2,0:T(8,128)(2,1)}, u32[]{:S(2)}, u32[]{:S(2)}) async-start(bf16[8,256,512]{1,2,0:T(8,128)(2,1)} %broadcast_in_dim.197), calls=%async_computation | async-start | bytes 4194304 | tf_op jit(solution)/shard_map/all_to_all | solution.py:165
  278.7 12.7 %collective-permute-done.11 = bf16[257,512]{0,1:T(8,128)(2,1)S(1)} collective-permute-done((bf16[257,512]{0,1:T(8,128)(2,1)}, bf16[257,512]{0,1:T(8,128)(2,1)S(1)}, u32[]{:S(2)}, u32[]{:S(2)}) %collective-permute-start.11) | collective-permute-done | bytes 263200 | tf_op jit(solution)/shard_map/ppermute | solution.py:22
  294.0 3.5 %collective-permute-done.12 = bf16[257,512]{0,1:T(8,128)(2,1)} collective-permute-done((bf16[257,512]{0,1:T(8,128)(2,1)}, bf16[257,512]{0,1:T(8,128)(2,1)}, u32[]{:S(2)}, u32[]{:S(2)}) %collective-permute-start.12) | collective-permute-done | bytes 263200 | tf_op jit(solution)/shard_map/ppermute | solution.py:22
  306.0 6.3 %collective-permute-start.14 = (bf16[2,512]{0,1:T(8,128)(2,1)S(1)}, bf16[2,512]{0,1:T(8,128)(2,1)S(1)}, u32[]{:S(2)}, u32[]{:S(2)}) collective-permute-start(bf16[2,512]{0,1:T(8,128)(2,1)S(1)} %slice.364), channel_id=1, source_target_pairs={{8,0},{16,8},{24,16},{32,24},{40,32},{48,40},{56,48},{64,56},{72,6... | collective-permute-start | bytes 6152 | tf_op jit(solution)/shard_map/ppermute | solution.py:22
  312.3 2.6 collective-permute-done.14
  319.5 6.5 %collective-permute-done.13 = bf16[2,512]{0,1:T(8,128)(2,1)S(1)} collective-permute-done((bf16[2,512]{0,1:T(8,128)(2,1)S(1)}, bf16[2,512]{0,1:T(8,128)(2,1)S(1)}, u32[]{:S(2)}, u32[]{:S(2)}) %collective-permute-start.13) | collective-permute-done | bytes 2080 | tf_op jit(solution)/shard_map/ppermute | solution.py:22
  328.2 10.5 %all-to-all-done = bf16[8,256,512]{1,2,0:T(8,128)(2,1)} async-done(((bf16[8,256,512]{1,2,0:T(8,128)(2,1)}), bf16[8,256,512]{1,2,0:T(8,128)(2,1)}, u32[]{:S(2)}, u32[]{:S(2)}) %all-to-all-start) | async-done | bytes 2097184 | tf_op jit(solution)/shard_map/all_to_all | solution.py:165
  (202 shorter events, 94.1 us)
Async XLA Ops:
  0.6 63.5 %copy-start = (bf16[256,512]{1,0:T(8,128)(2,1)S(1)}, bf16[256,512]{1,0:T(8,128)(2,1)}, u32[]{:S(2)}) copy-start(bf16[256,512]{1,0:T(8,128)(2,1)} %param.17) | copy-start | bytes 786436
  60.1 7.8 %collective-permute-start.7 = (bf16[2048,512]{1,0:T(8,128)(2,1)S(1)}, bf16[2048,512]{1,0:T(8,128)(2,1)S(1)}, u32[]{:S(2)}, u32[]{:S(2)}) collective-permute-start(bf16[2048,512]{1,0:T(8,128)(2,1)S(1)} %bitcast.147), channel_id=1, source_target_pairs={{0,8},{8,0},{1,9},{9,1},{2,10},{10,2},{3,11},{11,3},{4,12},{12,4},... | collective-permute-start | bytes 6291464 | tf_op jit(solution)/shard_map/ppermute | solution.py:15
  72.0 30.7 %copy-start.22 = (bf16[4,768]{1,0:T(4,128)(2,1)S(1)}, bf16[4,768]{1,0:T(4,128)(2,1)}, u32[]{:S(2)}) copy-start(bf16[4,768]{1,0:T(4,128)(2,1)} %param.13) | copy-start | bytes 18436
  72.0 31.5 %copy-start.38 = (f32[3,3,512]{2,1,0:T(4,128)S(1)}, f32[3,3,512]{2,1,0:T(4,128)}, u32[]{:S(2)}) copy-start(f32[3,3,512]{2,1,0:T(4,128)} %param.12) | copy-start | bytes 55300
  72.0 105.5 %all-to-all-start.2 = ((f32[8,2,4,64,256]{4,3,2,1,0:T(8,128)}), f32[8,2,4,64,256]{4,3,2,1,0:T(8,128)}, u32[]{:S(2)}, u32[]{:S(2)}) async-start(f32[8,2,4,64,256]{4,3,2,1,0:T(8,128)} %copy.50), calls=%async_computation.2 | async-start | bytes 8388608 | tf_op jit(solution)/shard_map/all_to_all | solution.py:188
  82.2 24.1 %collective-permute-start.8 = (s32[2]{0:T(128)S(1)}, s32[2]{0:T(128)S(1)}, u32[]{:S(2)}, u32[]{:S(2)}) collective-permute-start(s32[2]{0:T(128)S(1)} %get-tuple-element.53), channel_id=1, source_target_pairs={{8,0},{16,8},{24,16},{32,24},{40,32},{48,40},{56,48},{64,56},{72,6... | collective-permute-start | bytes 32 | tf_op jit(solution)/shard_map/ppermute | solution.py:22
  85.1 21.2 %collective-permute-start = (s32[2]{0:T(128)S(1)}, s32[2]{0:T(128)S(1)}, u32[]{:S(2)}, u32[]{:S(2)}) collective-permute-start(s32[2]{0:T(128)S(1)} %get-tuple-element.54), channel_id=1, source_target_pairs={{0,8},{8,16},{16,24},{24,32},{32,40},{40,48},{48,56},{56,64},{64,7... | collective-permute-start | bytes 32 | tf_op jit(solution)/shard_map/ppermute | solution.py:22
  90.7 89.5 %collective-permute-start.1 = (bf16[2,512]{0,1:T(8,128)(2,1)}, bf16[2,512]{0,1:T(8,128)(2,1)S(1)}, u32[]{:S(2)}, u32[]{:S(2)}) collective-permute-start(bf16[2,512]{0,1:T(8,128)(2,1)} %copy.42), channel_id=1, source_target_pairs={{0,8},{8,16},{16,24},{24,32},{32,40},{40,48},{48,56},{56,64},{64,7... | collective-permute-start | bytes 6152 | tf_op jit(solution)/shard_map/ppermute | solution.py:22
  94.2 104.8 %collective-permute-start.2 = (bf16[2,512]{0,1:T(8,128)(2,1)}, bf16[2,512]{0,1:T(8,128)(2,1)}, u32[]{:S(2)}, u32[]{:S(2)}) collective-permute-start(bf16[2,512]{0,1:T(8,128)(2,1)} %copy.45), channel_id=1, source_target_pairs={{0,8},{8,16},{16,24},{24,32},{32,40},{40,48},{48,56},{56,64},{64,7... | collective-permute-start | bytes 6152 | tf_op jit(solution)/shard_map/ppermute | solution.py:22
  98.8 100.2 %collective-permute-start.3 = (bf16[2,512]{0,1:T(8,128)(2,1)}, bf16[2,512]{0,1:T(8,128)(2,1)}, u32[]{:S(2)}, u32[]{:S(2)}) collective-permute-start(bf16[2,512]{0,1:T(8,128)(2,1)} %copy.48), channel_id=1, source_target_pairs={{0,8},{8,16},{16,24},{24,32},{32,40},{40,48},{48,56},{56,64},{64,7... | collective-permute-start | bytes 6152 | tf_op jit(solution)/shard_map/ppermute | solution.py:22
  182.7 11.5 %collective-permute-start.10 = (bf16[257,512]{0,1:T(8,128)(2,1)}, bf16[257,512]{0,1:T(8,128)(2,1)}, u32[]{:S(2)}, u32[]{:S(2)}) collective-permute-start(bf16[257,512]{0,1:T(8,128)(2,1)} %concatenate.69), channel_id=1, source_target_pairs={{8,0},{16,8},{24,16},{32,24},{40,32},{48,40},{56,48},{64,56},{72,6... | collective-permute-start | bytes 789512 | tf_op jit(solution)/shard_map/ppermute | solution.py:22
  189.3 24.2 %copy-start.9 = (bf16[256,512]{0,1:T(8,128)(2,1)}, bf16[256,512]{0,1:T(8,128)(2,1)S(1)}, u32[]{:S(2)}) copy-start(bf16[256,512]{0,1:T(8,128)(2,1)S(1)} %copy.47) | copy-start | bytes 786436
  202.8 40.6 %collective-permute-start.4 = (bf16[257,512]{0,1:T(8,128)(2,1)}, bf16[257,512]{0,1:T(8,128)(2,1)}, u32[]{:S(2)}, u32[]{:S(2)}) collective-permute-start(bf16[257,512]{0,1:T(8,128)(2,1)} %concatenate.60), channel_id=1, source_target_pairs={{0,8},{8,16},{16,24},{24,32},{32,40},{40,48},{48,56},{56,64},{64,7... | collective-permute-start | bytes 789512 | tf_op jit(solution)/shard_map/ppermute | solution.py:22
  204.7 41.2 %collective-permute-start.5 = (bf16[257,512]{0,1:T(8,128)(2,1)}, bf16[257,512]{0,1:T(8,128)(2,1)}, u32[]{:S(2)}, u32[]{:S(2)}) collective-permute-start(bf16[257,512]{0,1:T(8,128)(2,1)} %concatenate.60), channel_id=1, source_target_pairs={{0,16},{8,24},{16,32},{24,40},{32,48},{40,56},{48,64},{56,72},{64,... | collective-permute-start | bytes 789512 | tf_op jit(solution)/shard_map/ppermute | solution.py:22
  207.8 40.5 %collective-permute-start.6 = (bf16[257,512]{0,1:T(8,128)(2,1)}, bf16[257,512]{0,1:T(8,128)(2,1)}, u32[]{:S(2)}, u32[]{:S(2)}) collective-permute-start(bf16[257,512]{0,1:T(8,128)(2,1)} %concatenate.60), channel_id=1, source_target_pairs={{0,24},{8,32},{16,40},{24,48},{32,56},{40,64},{48,72},{56,80},{64,... | collective-permute-start | bytes 789512 | tf_op jit(solution)/shard_map/ppermute | solution.py:22
  256.4 8.4 %collective-permute-start.9 = (bf16[2,512]{0,1:T(8,128)(2,1)S(1)}, bf16[2,512]{0,1:T(8,128)(2,1)S(1)}, u32[]{:S(2)}, u32[]{:S(2)}) collective-permute-start(bf16[2,512]{0,1:T(8,128)(2,1)S(1)} %slice.352), channel_id=1, source_target_pairs={{8,0},{16,8},{24,16},{32,24},{40,32},{48,40},{56,48},{64,56},{72,6... | collective-permute-start | bytes 6152 | tf_op jit(solution)/shard_map/ppermute | solution.py:22
  267.8 70.9 %all-to-all-start = ((bf16[8,256,512]{1,2,0:T(8,128)(2,1)}), bf16[8,256,512]{1,2,0:T(8,128)(2,1)}, u32[]{:S(2)}, u32[]{:S(2)}) async-start(bf16[8,256,512]{1,2,0:T(8,128)(2,1)} %broadcast_in_dim.197), calls=%async_computation | async-start | bytes 4194304 | tf_op jit(solution)/shard_map/all_to_all | solution.py:165
  272.5 30.5 %copy-start.46 = (pred[256]{0:T(512)(128)(4,1)S(1)}, pred[256]{0:T(512)(128)(4,1)}, u32[]{:S(2)}) copy-start(pred[256]{0:T(512)(128)(4,1)} %copy-done.45) | copy-start | bytes 772
  272.5 30.6 %copy-start.3 = (bf16[4,256,511]{2,1,0:T(8,128)(2,1)S(1)}, bf16[4,256,511]{2,1,0:T(8,128)(2,1)}, u32[]{:S(2)}) copy-start(bf16[4,256,511]{2,1,0:T(8,128)(2,1)} %reshape.200) | copy-start | bytes 3139588
  272.5 18.9 %collective-permute-start.11 = (bf16[257,512]{0,1:T(8,128)(2,1)}, bf16[257,512]{0,1:T(8,128)(2,1)S(1)}, u32[]{:S(2)}, u32[]{:S(2)}) collective-permute-start(bf16[257,512]{0,1:T(8,128)(2,1)} %concatenate.69), channel_id=1, source_target_pairs={{16,0},{24,8},{32,16},{40,24},{48,32},{56,40},{64,48},{72,56},{80,... | collective-permute-start | bytes 789512 | tf_op jit(solution)/shard_map/ppermute | solution.py:22
  274.5 23.0 %collective-permute-start.12 = (bf16[257,512]{0,1:T(8,128)(2,1)}, bf16[257,512]{0,1:T(8,128)(2,1)}, u32[]{:S(2)}, u32[]{:S(2)}) collective-permute-start(bf16[257,512]{0,1:T(8,128)(2,1)} %concatenate.69), channel_id=1, source_target_pairs={{24,0},{32,8},{40,16},{48,24},{56,32},{64,40},{72,48},{80,56},{88,... | collective-permute-start | bytes 789512 | tf_op jit(solution)/shard_map/ppermute | solution.py:22
  305.9 21.5 %copy-start.12 = (bf16[256,512]{0,1:T(8,128)(2,1)S(1)}, bf16[256,512]{0,1:T(8,128)(2,1)}, u32[]{:S(2)}) copy-start(bf16[256,512]{0,1:T(8,128)(2,1)} %get-tuple-element.37) | copy-start | bytes 786436
  306.0 8.9 %collective-permute-start.14 = (bf16[2,512]{0,1:T(8,128)(2,1)S(1)}, bf16[2,512]{0,1:T(8,128)(2,1)S(1)}, u32[]{:S(2)}, u32[]{:S(2)}) collective-permute-start(bf16[2,512]{0,1:T(8,128)(2,1)S(1)} %slice.364), channel_id=1, source_target_pairs={{8,0},{16,8},{24,16},{32,24},{40,32},{48,40},{56,48},{64,56},{72,6... | collective-permute-start | bytes 6152 | tf_op jit(solution)/shard_map/ppermute | solution.py:22
  316.8 9.3 %collective-permute-start.13 = (bf16[2,512]{0,1:T(8,128)(2,1)S(1)}, bf16[2,512]{0,1:T(8,128)(2,1)S(1)}, u32[]{:S(2)}, u32[]{:S(2)}) collective-permute-start(bf16[2,512]{0,1:T(8,128)(2,1)S(1)} %slice.361), channel_id=1, source_target_pairs={{8,0},{16,8},{24,16},{32,24},{40,32},{48,40},{56,48},{64,56},{72,6... | collective-permute-start | bytes 6152 | tf_op jit(solution)/shard_map/ppermute | solution.py:22
  (43 other events, 249.4 us)

commit v8 on v6

--- a/solution.py
+++ b/solution.py
@@ -153,6 +153,18 @@
     chip_count = lax.axis_size(CHIPS)
     weight_rows, weight_rows_other, core_index = gather_weight(out_weight, chip_count)
     ch_count = lax.axis_size(CH)
+    on_first = core_index == 0
+    dims = (((1,), (1,)), ((), ()))
+    block_chips = chip_count // ch_count
+    part_mine = lax.dot_general(
+        weight_rows, out_grad, dims, preferred_element_type=jnp.float32
+    ).reshape(ch_count, 1, block_chips, -1, row_count)
+    part_other = lax.dot_general(
+        weight_rows_other, out_grad, dims, preferred_element_type=jnp.float32
+    ).reshape(ch_count, 1, block_chips, -1, row_count)
+    sent = jnp.concatenate([part_mine, part_other], axis=1)
+    received = lax.all_to_all(sent, CH, 0, 0, tiled=True)
+    pre_gate, mixed, received = lax.optimization_barrier((pre_gate, mixed, received))
     spread = jnp.broadcast_to(pre_gate[None], (ch_count,) + pre_gate.shape)
     gathered = lax.all_to_all(spread, CH, 0, 0, tiled=True).reshape(
         ch_count, row_count, channels
@@ -162,23 +174,12 @@
     )
     pre_first = full_pre[:, :, 0].reshape(row_count, -1)
     pre_second = full_pre[:, :, 1].reshape(row_count, -1)
-    on_first = core_index == 0
     pre_mine = jnp.where(on_first, pre_first, pre_second)
     pre_other = jnp.where(on_first, pre_second, pre_first)
     out_sum = jnp.dot(pre_mine, weight_rows, preferred_element_type=jnp.float32) + jnp.dot(
         pre_other, weight_rows_other, preferred_element_type=jnp.float32
     )
-    dims = (((1,), (1,)), ((), ()))
-    block_chips = chip_count // ch_count
-
-    def summed_over_ch(weight_half):
-        part = lax.dot_general(weight_half, out_grad, dims, preferred_element_type=jnp.float32)
-        received = lax.all_to_all(
-            part.reshape(ch_count, block_chips, -1, row_count), CH, 0, 0, tiled=True
-        )
-        return jnp.sum(received, axis=0)
-
-    summed = (summed_over_ch(weight_rows), summed_over_ch(weight_rows_other))
+    summed = jnp.sum(received, axis=0)
     cols_mine, cols_other = summed[0][:, None], summed[1][:, None]
     grad_cols = jnp.where(
         on_first,

time: 302 us -> 280 us (0.927)
  the two profiles are of different devices: /device:TPU:443 before, /device:TPU:1 now
where the time goes in v8:
time: 280 us; the launch traced here: 279 us
  starting transfers between devices  79.9 us (29%)
  blocking collectives  61.7 us (22%)
  local copies, waits for them, and re-layouts  51.1 us (18%)
  waiting for transfers between devices  39.2 us (14%)
  other arithmetic  28.7 us (10%)
  matrix products  13 us (5%)
  between operations  5.44 us (2%)
    all_to_all x1, blocking collectives, gather_weight(): lax.all_to_all(spread, CHIPS, 0, 0, tiled=True)  61.7 us
    ppermute x14, starting transfers between devices, shifted(): return lax.ppermute(array, axis, pairs)  55.6 us
    all_to_all x1, waiting for transfers between devices, local(): received = lax.all_to_all(sent, CH, 0, 0, tiled=True)  20.7 us
    unnamed x98, local copies, waits for them, and re-layouts  19.7 us
    ppermute x14, waiting for transfers between devices, shifted(): return lax.ppermute(array, axis, pairs)  15.5 us
    reshape x4, local copies, waits for them, and re-layouts, toeplitz_tiles(): repeated.reshape(group_count, row_count, 2 * row_count - 1)  15.2 us
    all_to_all x1, starting transfers between devices, local(): received = lax.all_to_all(sent, CH, 0, 0, tiled=True)  9.91 us
    all_to_all x1, starting transfers between devices, local(): lax.all_to_all(spread, CH, 0, 0, tiled=True)  8.23 us
  transfers between devices with their start and end apart: 17, of which 7 were waited for; matrix products, arithmetic and copies ran while one was open for 29% of the time, Pallas kernels for 0%

profile of v8, /device:TPU:1, one launch (start us, length us, event | category | flops | bytes accessed | tf_op | source)
XLA Modules:
  0.0 278.9 jit_solution(4488706614611310353)
XLA Ops:
  1.8 61.7 %all_to_all.15 = bf16[32,64,512]{2,1,0:T(8,128)(2,1)S(1)} all-to-all(bf16[32,64,512]{2,1,0:T(8,128)(2,1)S(1)} %broadcast_in_dim.198), channel_id=1, replica_groups=mesh['zl'=4,'y'=8,'core'=2,'zh'=2,'x'=4] {'zl','y'}, dimensions={0} | all-to-all | bytes 4194304 | tf_op jit(solution)/shard_map/all_to_all | solution.py:14
  63.4 6.2 %collective-permute-start.8 = (bf16[2048,512]{1,0:T(8,128)(2,1)S(1)}, bf16[2048,512]{1,0:T(8,128)(2,1)S(1)}, u32[]{:S(2)}, u32[]{:S(2)}) collective-permute-start(bf16[2048,512]{1,0:T(8,128)(2,1)S(1)} %bitcast.144), channel_id=1, source_target_pairs={{0,8},{8,0},{1,9},{9,1},{2,10},{10,2},{3,11},{11,3},{4,12},{12,4},... | collective-permute-start | bytes 6291464 | tf_op jit(solution)/shard_map/ppermute | solution.py:15
  70.3 3.0 %collective-permute-done.8 = bf16[2048,512]{1,0:T(8,128)(2,1)S(1)} collective-permute-done((bf16[2048,512]{1,0:T(8,128)(2,1)S(1)}, bf16[2048,512]{1,0:T(8,128)(2,1)S(1)}, u32[]{:S(2)}, u32[]{:S(2)}) %collective-permute-start.8) | collective-permute-done | bytes 2097184 | tf_op jit(solution)/shard_map/ppermute | solution.py:15
  77.5 9.9 %all-to-all-start.1 = ((f32[8,2,4,64,256]{4,3,2,1,0:T(8,128)}), f32[8,2,4,64,256]{4,3,2,1,0:T(8,128)}, u32[]{:S(2)}, u32[]{:S(2)}) async-start(f32[8,2,4,64,256]{4,3,2,1,0:T(8,128)} %copy.50), calls=%async_computation.1 | async-start | bytes 8388608 | tf_op jit(solution)/shard_map/all_to_all | solution.py:166
  88.1 2.6 collective-permute-start.4
  90.6 3.0 %collective-permute-start = (s32[2]{0:T(128)}, s32[2]{0:T(128)}, u32[]{:S(2)}, u32[]{:S(2)}) collective-permute-start(s32[2]{0:T(128)} %get-tuple-element.65), channel_id=1, source_target_pairs={{0,8},{8,16},{16,24},{24,32},{32,40},{40,48},{48,56},{56,64},{64,7... | collective-permute-start | bytes 32 | tf_op jit(solution)/shard_map/ppermute | solution.py:22
  98.1 3.0 %collective-permute-start.2 = (bf16[2,512]{0,1:T(8,128)(2,1)}, bf16[2,512]{0,1:T(8,128)(2,1)}, u32[]{:S(2)}, u32[]{:S(2)}) collective-permute-start(bf16[2,512]{0,1:T(8,128)(2,1)} %copy.45), channel_id=1, source_target_pairs={{0,8},{8,16},{16,24},{24,32},{32,40},{40,48},{48,56},{56,64},{64,7... | collective-permute-start | bytes 6152 | tf_op jit(solution)/shard_map/ppermute | solution.py:22
  115.2 3.3 %select_select_fusion.1 = (bf16[256,512]{0,1:T(8,128)(2,1)}, bf16[256,512]{0,1:T(8,128)(2,1)}) fusion(pred[256]{0:T(512)(128)(4,1)} %get-tuple-element.53, pred[]{:T(512)S(6)} %eq.69, bf16[256,512]{0,1:T(8,128)(2,1)} %copy.47, bf16[2,512]{0,1:T(8,128)(2,1)S(1)} %collective-permute-done.3, f32[512]{0:T(512)} %bitcast.180, f32[512]{0:T(512)} %bitcast.182, ...), kind=kLoop, calls=%fused_computation.94 | loop fusion | flops 4718592 | bytes 1065729 | tf_op jit(solution)/shard_map/jit(_where)/select_n | solution.py:143
  118.5 2.7 collective-permute-start.5
  128.4 4.0 %reshape.170 = bf16[4,256,511]{2,1,0:T(8,128)(2,1)} reshape(bf16[4,130816]{1,0:T(4,128)(2,1)} %slice.294) | data formatting | bytes 2093056 | tf_op jit(solution)/shard_map/reshape | solution.py:48
  134.5 3.0 %reshape.175 = bf16[4,256,511]{2,1,0:T(8,128)(2,1)S(1)} reshape(bf16[4,130816]{1,0:T(4,128)(2,1)} %slice.298) | data formatting | bytes 2093056 | tf_op jit(solution)/shard_map/reshape | solution.py:48
  137.6 2.4 copy.56
  141.4 4.1 %reshape.173 = bf16[4,256,511]{2,1,0:T(8,128)(2,1)} reshape(bf16[4,130816]{1,0:T(4,128)(2,1)} %slice.296) | data formatting | bytes 2093056 | tf_op jit(solution)/shard_map/reshape | solution.py:48
  148.9 4.0 %reshape.177 = bf16[4,256,511]{2,1,0:T(8,128)(2,1)} reshape(bf16[4,130816]{1,0:T(4,128)(2,1)} %slice.300) | data formatting | bytes 2093056 | tf_op jit(solution)/shard_map/reshape | solution.py:48
  155.3 2.5 collective-permute-start.6
  161.5 4.3 %collective-permute-start.7 = (bf16[256,512]{0,1:T(8,128)(2,1)S(1)}, bf16[256,512]{0,1:T(8,128)(2,1)S(1)}, u32[]{:S(2)}, u32[]{:S(2)}) collective-permute-start(bf16[256,512]{0,1:T(8,128)(2,1)S(1)} %broadcast_select_fusion.10), channel_id=1, source_target_pairs={{0,8},{8,16},{16,24},{24,32},{32,40},{40,48},{48,56},{56,64},{64,7... | collective-permute-start | bytes 786440 | tf_op jit(solution)/shard_map/ppermute | solution.py:22
  170.8 2.5 multiply_convert_fusion.2
  173.2 20.7 %all-to-all-done.1 = f32[8,2,4,64,256]{4,3,2,1,0:T(8,128)} async-done(((f32[8,2,4,64,256]{4,3,2,1,0:T(8,128)}), f32[8,2,4,64,256]{4,3,2,1,0:T(8,128)}, u32[]{:S(2)}, u32[]{:S(2)}) %all-to-all-start.1) | async-done | bytes 4194336 | tf_op jit(solution)/shard_map/all_to_all | solution.py:166
  195.4 8.2 %all-to-all-start.2 = ((bf16[8,256,512]{1,2,0:T(8,128)(2,1)}), bf16[8,256,512]{1,2,0:T(8,128)(2,1)}, u32[]{:S(2)}, u32[]{:S(2)}) async-start(bf16[8,256,512]{1,2,0:T(8,128)(2,1)} %broadcast_in_dim.199), calls=%async_computation.2 | async-start | bytes 4194304 | tf_op jit(solution)/shard_map/all_to_all | solution.py:169
  205.5 2.5 reduce_sum.9
  211.2 23.6 %collective-permute-start.10 = (bf16[256,512]{0,1:T(8,128)(2,1)}, bf16[256,512]{0,1:T(8,128)(2,1)S(1)}, u32[]{:S(2)}, u32[]{:S(2)}) collective-permute-start(bf16[256,512]{0,1:T(8,128)(2,1)} %get-tuple-element.20), channel_id=1, source_target_pairs={{8,0},{16,8},{24,16},{32,24},{40,32},{48,40},{56,48},{64,56},{72,6... | collective-permute-start | bytes 786440 | tf_op jit(solution)/shard_map/ppermute | solution.py:22
  240.4 4.3 %collective-permute-done.11 = bf16[256,512]{0,1:T(8,128)(2,1)S(1)} collective-permute-done((bf16[256,512]{0,1:T(8,128)(2,1)S(1)}, bf16[256,512]{0,1:T(8,128)(2,1)S(1)}, u32[]{:S(2)}, u32[]{:S(2)}) %collective-permute-start.11) | collective-permute-done | bytes 262176 | tf_op jit(solution)/shard_map/ppermute | solution.py:22
  248.3 4.1 %collective-permute-done.12 = bf16[256,512]{0,1:T(8,128)(2,1)S(1)} collective-permute-done((bf16[256,512]{0,1:T(8,128)(2,1)S(1)}, bf16[256,512]{0,1:T(8,128)(2,1)S(1)}, u32[]{:S(2)}, u32[]{:S(2)}) %collective-permute-start.12) | collective-permute-done | bytes 262176 | tf_op jit(solution)/shard_map/ppermute | solution.py:22
  267.2 3.1 %collective-permute-done.13 = bf16[2,512]{0,1:T(8,128)(2,1)S(1)} collective-permute-done((bf16[2,512]{0,1:T(8,128)(2,1)}, bf16[2,512]{0,1:T(8,128)(2,1)S(1)}, u32[]{:S(2)}, u32[]{:S(2)}) %collective-permute-start.13) | collective-permute-done | bytes 2080 | tf_op jit(solution)/shard_map/ppermute | solution.py:22
  (180 shorter events, 84.8 us)
Async XLA Ops:
  0.6 69.0 %copy-start = (bf16[256,512]{1,0:T(8,128)(2,1)S(1)}, bf16[256,512]{1,0:T(8,128)(2,1)}, u32[]{:S(2)}) copy-start(bf16[256,512]{1,0:T(8,128)(2,1)} %param.17) | copy-start | bytes 786436
  63.4 9.9 %collective-permute-start.8 = (bf16[2048,512]{1,0:T(8,128)(2,1)S(1)}, bf16[2048,512]{1,0:T(8,128)(2,1)S(1)}, u32[]{:S(2)}, u32[]{:S(2)}) collective-permute-start(bf16[2048,512]{1,0:T(8,128)(2,1)S(1)} %bitcast.144), channel_id=1, source_target_pairs={{0,8},{8,0},{1,9},{9,1},{2,10},{10,2},{3,11},{11,3},{4,12},{12,4},... | collective-permute-start | bytes 6291464 | tf_op jit(solution)/shard_map/ppermute | solution.py:15
  77.5 19.8 %copy-start.15 = (bf16[256,512]{1,0:T(8,128)(2,1)S(1)}, bf16[256,512]{1,0:T(8,128)(2,1)}, u32[]{:S(2)}) copy-start(bf16[256,512]{1,0:T(8,128)(2,1)} %param.10) | copy-start | bytes 786436
  77.5 23.6 %copy-start.16 = (bf16[256,512]{1,0:T(8,128)(2,1)S(1)}, bf16[256,512]{1,0:T(8,128)(2,1)}, u32[]{:S(2)}) copy-start(bf16[256,512]{1,0:T(8,128)(2,1)} %param.11) | copy-start | bytes 786436
  77.5 28.8 %copy-start.22 = (bf16[4,768]{1,0:T(4,128)(2,1)S(1)}, bf16[4,768]{1,0:T(4,128)(2,1)}, u32[]{:S(2)}) copy-start(bf16[4,768]{1,0:T(4,128)(2,1)} %param.13) | copy-start | bytes 18436
  77.5 29.0 %copy-start.31 = (f32[3,3,512]{2,1,0:T(4,128)S(1)}, f32[3,3,512]{2,1,0:T(4,128)}, u32[]{:S(2)}) copy-start(f32[3,3,512]{2,1,0:T(4,128)} %param.12) | copy-start | bytes 55300
  77.5 116.4 %all-to-all-start.1 = ((f32[8,2,4,64,256]{4,3,2,1,0:T(8,128)}), f32[8,2,4,64,256]{4,3,2,1,0:T(8,128)}, u32[]{:S(2)}, u32[]{:S(2)}) async-start(f32[8,2,4,64,256]{4,3,2,1,0:T(8,128)} %copy.50), calls=%async_computation.1 | async-start | bytes 8388608 | tf_op jit(solution)/shard_map/all_to_all | solution.py:166
  88.1 22.3 %collective-permute-start.4 = (s32[2]{0:T(128)}, s32[2]{0:T(128)}, u32[]{:S(2)}, u32[]{:S(2)}) collective-permute-start(s32[2]{0:T(128)} %get-tuple-element.64), channel_id=1, source_target_pairs={{8,0},{16,8},{24,16},{32,24},{40,32},{48,40},{56,48},{64,56},{72,6... | collective-permute-start | bytes 32 | tf_op jit(solution)/shard_map/ppermute | solution.py:22
  90.6 20.4 %collective-permute-start = (s32[2]{0:T(128)}, s32[2]{0:T(128)}, u32[]{:S(2)}, u32[]{:S(2)}) collective-permute-start(s32[2]{0:T(128)} %get-tuple-element.65), channel_id=1, source_target_pairs={{0,8},{8,16},{16,24},{24,32},{32,40},{40,48},{48,56},{56,64},{64,7... | collective-permute-start | bytes 32 | tf_op jit(solution)/shard_map/ppermute | solution.py:22
  95.2 75.5 %collective-permute-start.1 = (bf16[2,512]{0,1:T(8,128)(2,1)}, bf16[2,512]{0,1:T(8,128)(2,1)}, u32[]{:S(2)}, u32[]{:S(2)}) collective-permute-start(bf16[2,512]{0,1:T(8,128)(2,1)} %copy.42), channel_id=1, source_target_pairs={{0,8},{8,16},{16,24},{24,32},{32,40},{40,48},{48,56},{56,64},{64,7... | collective-permute-start | bytes 6152 | tf_op jit(solution)/shard_map/ppermute | solution.py:22
  98.1 17.1 %collective-permute-start.2 = (bf16[2,512]{0,1:T(8,128)(2,1)}, bf16[2,512]{0,1:T(8,128)(2,1)}, u32[]{:S(2)}, u32[]{:S(2)}) collective-permute-start(bf16[2,512]{0,1:T(8,128)(2,1)} %copy.45), channel_id=1, source_target_pairs={{0,8},{8,16},{16,24},{24,32},{32,40},{40,48},{48,56},{56,64},{64,7... | collective-permute-start | bytes 6152 | tf_op jit(solution)/shard_map/ppermute | solution.py:22
  101.9 13.2 %collective-permute-start.3 = (bf16[2,512]{0,1:T(8,128)(2,1)}, bf16[2,512]{0,1:T(8,128)(2,1)S(1)}, u32[]{:S(2)}, u32[]{:S(2)}) collective-permute-start(bf16[2,512]{0,1:T(8,128)(2,1)} %copy.48), channel_id=1, source_target_pairs={{0,8},{8,16},{16,24},{24,32},{32,40},{40,48},{48,56},{56,64},{64,7... | collective-permute-start | bytes 6152 | tf_op jit(solution)/shard_map/ppermute | solution.py:22
  118.5 35.9 %collective-permute-start.5 = (bf16[256,512]{0,1:T(8,128)(2,1)}, bf16[256,512]{0,1:T(8,128)(2,1)}, u32[]{:S(2)}, u32[]{:S(2)}) collective-permute-start(bf16[256,512]{0,1:T(8,128)(2,1)} %get-tuple-element.24), channel_id=1, source_target_pairs={{0,8},{8,16},{16,24},{24,32},{32,40},{40,48},{48,56},{56,64},{64,7... | collective-permute-start | bytes 786440 | tf_op jit(solution)/shard_map/ppermute | solution.py:22
  137.6 28.9 %copy-start.3 = (bf16[4,256,511]{2,1,0:T(8,128)(2,1)}, bf16[4,256,511]{2,1,0:T(8,128)(2,1)S(1)}, u32[]{:S(2)}) copy-start(bf16[4,256,511]{2,1,0:T(8,128)(2,1)S(1)} %reshape.175) | copy-start | bytes 3139588
  155.3 6.1 %collective-permute-start.6 = (bf16[256,512]{0,1:T(8,128)(2,1)S(1)}, bf16[256,512]{0,1:T(8,128)(2,1)S(1)}, u32[]{:S(2)}, u32[]{:S(2)}) collective-permute-start(bf16[256,512]{0,1:T(8,128)(2,1)S(1)} %broadcast_select_fusion.11), channel_id=1, source_target_pairs={{0,8},{8,16},{16,24},{24,32},{32,40},{40,48},{48,56},{56,64},{64,7... | collective-permute-start | bytes 786440 | tf_op jit(solution)/shard_map/ppermute | solution.py:22
  161.5 7.6 %collective-permute-start.7 = (bf16[256,512]{0,1:T(8,128)(2,1)S(1)}, bf16[256,512]{0,1:T(8,128)(2,1)S(1)}, u32[]{:S(2)}, u32[]{:S(2)}) collective-permute-start(bf16[256,512]{0,1:T(8,128)(2,1)S(1)} %broadcast_select_fusion.10), channel_id=1, source_target_pairs={{0,8},{8,16},{16,24},{24,32},{32,40},{40,48},{48,56},{56,64},{64,7... | collective-permute-start | bytes 786440 | tf_op jit(solution)/shard_map/ppermute | solution.py:22
  195.4 78.8 %all-to-all-start.2 = ((bf16[8,256,512]{1,2,0:T(8,128)(2,1)}), bf16[8,256,512]{1,2,0:T(8,128)(2,1)}, u32[]{:S(2)}, u32[]{:S(2)}) async-start(bf16[8,256,512]{1,2,0:T(8,128)(2,1)} %broadcast_in_dim.199), calls=%async_computation.2 | async-start | bytes 4194304 | tf_op jit(solution)/shard_map/all_to_all | solution.py:169
  211.2 25.1 %collective-permute-start.10 = (bf16[256,512]{0,1:T(8,128)(2,1)}, bf16[256,512]{0,1:T(8,128)(2,1)S(1)}, u32[]{:S(2)}, u32[]{:S(2)}) collective-permute-start(bf16[256,512]{0,1:T(8,128)(2,1)} %get-tuple-element.20), channel_id=1, source_target_pairs={{8,0},{16,8},{24,16},{32,24},{40,32},{48,40},{56,48},{64,56},{72,6... | collective-permute-start | bytes 786440 | tf_op jit(solution)/shard_map/ppermute | solution.py:22
  236.4 16.7 %copy-start.6 = (bf16[4,256,511]{2,1,0:T(8,128)(2,1)S(1)}, bf16[4,256,511]{2,1,0:T(8,128)(2,1)}, u32[]{:S(2)}) copy-start(bf16[4,256,511]{2,1,0:T(8,128)(2,1)} %reshape.177) | copy-start | bytes 3139588
  236.4 8.2 %collective-permute-start.11 = (bf16[256,512]{0,1:T(8,128)(2,1)S(1)}, bf16[256,512]{0,1:T(8,128)(2,1)S(1)}, u32[]{:S(2)}, u32[]{:S(2)}) collective-permute-start(bf16[256,512]{0,1:T(8,128)(2,1)S(1)} %broadcast_select_fusion.9), channel_id=1, source_target_pairs={{8,0},{16,8},{24,16},{32,24},{40,32},{48,40},{56,48},{64,56},{72,6... | collective-permute-start | bytes 786440 | tf_op jit(solution)/shard_map/ppermute | solution.py:22
  244.7 7.7 %collective-permute-start.12 = (bf16[256,512]{0,1:T(8,128)(2,1)S(1)}, bf16[256,512]{0,1:T(8,128)(2,1)S(1)}, u32[]{:S(2)}, u32[]{:S(2)}) collective-permute-start(bf16[256,512]{0,1:T(8,128)(2,1)S(1)} %broadcast_select_fusion.8), channel_id=1, source_target_pairs={{8,0},{16,8},{24,16},{32,24},{40,32},{48,40},{56,48},{64,56},{72,6... | collective-permute-start | bytes 786440 | tf_op jit(solution)/shard_map/ppermute | solution.py:22
  255.9 6.3 %collective-permute-start.14 = (bf16[2,512]{0,1:T(8,128)(2,1)S(1)}, bf16[2,512]{0,1:T(8,128)(2,1)S(1)}, u32[]{:S(2)}, u32[]{:S(2)}) collective-permute-start(bf16[2,512]{0,1:T(8,128)(2,1)S(1)} %slice.312), channel_id=1, source_target_pairs={{8,0},{16,8},{24,16},{32,24},{40,32},{48,40},{56,48},{64,56},{72,6... | collective-permute-start | bytes 6152 | tf_op jit(solution)/shard_map/ppermute | solution.py:22
  258.0 8.6 %collective-permute-start.9 = (bf16[2,512]{0,1:T(8,128)(2,1)S(1)}, bf16[2,512]{0,1:T(8,128)(2,1)S(1)}, u32[]{:S(2)}, u32[]{:S(2)}) collective-permute-start(bf16[2,512]{0,1:T(8,128)(2,1)S(1)} %slice.306), channel_id=1, source_target_pairs={{8,0},{16,8},{24,16},{32,24},{40,32},{48,40},{56,48},{64,56},{72,6... | collective-permute-start | bytes 6152 | tf_op jit(solution)/shard_map/ppermute | solution.py:22
  263.8 6.5 %collective-permute-start.13 = (bf16[2,512]{0,1:T(8,128)(2,1)}, bf16[2,512]{0,1:T(8,128)(2,1)S(1)}, u32[]{:S(2)}, u32[]{:S(2)}) collective-permute-start(bf16[2,512]{0,1:T(8,128)(2,1)} %slice.309), channel_id=1, source_target_pairs={{8,0},{16,8},{24,16},{32,24},{40,32},{48,40},{56,48},{64,56},{72,6... | collective-permute-start | bytes 6152 | tf_op jit(solution)/shard_map/ppermute | solution.py:22
  (35 other events, 285.6 us)

commit v9 on v8

--- a/solution.py
+++ b/solution.py
@@ -64,6 +64,15 @@
     return jnp.einsum(
         "gst,tgc->sgc", band_tile, grouped, preferred_element_type=jnp.float32
     ).reshape(row_count, channels)
+
+
+def tagged(rows, doc_id):
+    tag = jnp.full((1, rows.shape[1]), doc_id + 1, rows.dtype)
+    return jnp.concatenate([rows, tag])
+
+
+def untagged(block):
+    return block[:-1], block[-1, 0].astype(jnp.int32) - 1
 
 
 def causal_taps(extended, weights, ext_ids, doc_ids):
@@ -194,14 +203,14 @@
     grad_gated = apply_adjoint(diagonal, grad_mixed) + skip_weight[None, :] * grad_mixed.astype(
         jnp.float32
     )
-    moving_back = jnp.where(joins_prev, own_head, zero_half)
+    own_head = tagged(own_head, first_id)
     for distance in range(1, HOPS + 1):
-        moving_back = shifted(moving_back, CTX, -1)
-        is_live = jnp.any(moving_back != 0)
+        moving_back, source_id = untagged(shifted(own_head, CTX, -distance))
         grad_gated = grad_gated + jnp.where(
-            tail_rows, cross_term(is_live, apply_adjoint, tiles_list[distance], moving_back), 0.0
-        )
-        moving_back = jnp.where(single_doc & joins_prev, moving_back, zero_half)
+            tail_rows & (source_id == last_id),
+            apply_adjoint(tiles_list[distance], moving_back),
+            0.0,
+        )
     grad_key_short = (grad_gated * value_short).astype(jnp.bfloat16)
     grad_value_short = (grad_gated * key_short).astype(jnp.bfloat16)
     next_rows = shifted((grad_query_short[:2], grad_key_short[:2], grad_value_short[:2]), CTX, -1)

time: 280 us -> 269 us (0.961)
  starting transfers between devices: 79.9 us -> 57.9 us
  waiting for transfers between devices: 39.2 us -> 45.2 us
  local copies, waits for them, and re-layouts: 51.1 us -> 56.8 us
  between operations: 5.44 us -> 8.76 us
  other arithmetic: 28.7 us -> 25.7 us
    ppermute x14, starting transfers between devices: 55.6 us -> 35.3 us  [shifted(): return lax.ppermute(array, axis, pairs)]
    slice x1 -> x6, local copies, waits for them, and re-layouts: 0.58 us -> 5.91 us  [untagged(): return (block[:-1], block[-1, 0].astype(jnp.int32) - 1)]
    ppermute x14, waiting for transfers between devices: 15.5 us -> 19.6 us  [shifted(): return lax.ppermute(array, axis, pairs)]
    unnamed x98 -> x106, local copies, waits for them, and re-layouts: 19.7 us -> 19.8 us
  transfers between devices with their start and end apart: 17 -> 17, of which waited for: 7 -> 8; matrix products, arithmetic and copies ran while one was open for 29% -> 30% of each run, Pallas kernels for 0% -> 0%
where the time goes in v9:
time: 269 us; the launch traced here: 268 us
  blocking collectives  61.7 us (23%)
  starting transfers between devices  57.9 us (22%)
  local copies, waits for them, and re-layouts  56.8 us (21%)
  waiting for transfers between devices  45.2 us (17%)
  other arithmetic  25.7 us (10%)
  matrix products  11.7 us (4%)
  between operations  8.76 us (3%)
    all_to_all x1, blocking collectives, gather_weight(): lax.all_to_all(spread, CHIPS, 0, 0, tiled=True)  61.7 us
    ppermute x14, starting transfers between devices, shifted(): return lax.ppermute(array, axis, pairs)  35.3 us
    all_to_all x1, waiting for transfers between devices, local(): received = lax.all_to_all(sent, CH, 0, 0, tiled=True)  22.5 us
    unnamed x106, local copies, waits for them, and re-layouts  19.8 us
    ppermute x14, waiting for transfers between devices, shifted(): return lax.ppermute(array, axis, pairs)  19.6 us
    reshape x4, local copies, waits for them, and re-layouts, toeplitz_tiles(): repeated.reshape(group_count, row_count, 2 * row_count - 1)  15.2 us
    all_to_all x1, starting transfers between devices, local(): received = lax.all_to_all(sent, CH, 0, 0, tiled=True)  9.91 us
    all_to_all x1, starting transfers between devices, local(): lax.all_to_all(spread, CH, 0, 0, tiled=True)  6.52 us
  transfers between devices with their start and end apart: 17, of which 8 were waited for; matrix products, arithmetic and copies ran while one was open for 30% of the time, Pallas kernels for 0%

profile of v9, /device:TPU:1, one launch (start us, length us, event | category | flops | bytes accessed | tf_op | source)
XLA Modules:
  0.0 267.7 jit_solution(10263042533585407836)
XLA Ops:
  1.8 61.7 %all_to_all.15 = bf16[32,64,512]{2,1,0:T(8,128)(2,1)S(1)} all-to-all(bf16[32,64,512]{2,1,0:T(8,128)(2,1)S(1)} %broadcast_in_dim.199), channel_id=1, replica_groups=mesh['zl'=4,'y'=8,'core'=2,'zh'=2,'x'=4] {'zl','y'}, dimensions={0} | all-to-all | bytes 4194304 | tf_op jit(solution)/shard_map/all_to_all | solution.py:14
  63.4 6.2 %collective-permute-start.8 = (bf16[2048,512]{1,0:T(8,128)(2,1)S(1)}, bf16[2048,512]{1,0:T(8,128)(2,1)S(1)}, u32[]{:S(2)}, u32[]{:S(2)}) collective-permute-start(bf16[2048,512]{1,0:T(8,128)(2,1)S(1)} %bitcast.146), channel_id=1, source_target_pairs={{0,8},{8,0},{1,9},{9,1},{2,10},{10,2},{3,11},{11,3},{4,12},{12,4},... | collective-permute-start | bytes 6291464 | tf_op jit(solution)/shard_map/ppermute | solution.py:15
  70.3 3.0 %collective-permute-done.8 = bf16[2048,512]{1,0:T(8,128)(2,1)S(1)} collective-permute-done((bf16[2048,512]{1,0:T(8,128)(2,1)S(1)}, bf16[2048,512]{1,0:T(8,128)(2,1)S(1)}, u32[]{:S(2)}, u32[]{:S(2)}) %collective-permute-start.8) | collective-permute-done | bytes 2097184 | tf_op jit(solution)/shard_map/ppermute | solution.py:15
  77.5 9.9 %all-to-all-start.1 = ((f32[8,2,4,64,256]{4,3,2,1,0:T(8,128)}), f32[8,2,4,64,256]{4,3,2,1,0:T(8,128)}, u32[]{:S(2)}, u32[]{:S(2)}) async-start(f32[8,2,4,64,256]{4,3,2,1,0:T(8,128)} %copy.50), calls=%async_computation.1 | async-start | bytes 8388608 | tf_op jit(solution)/shard_map/all_to_all | solution.py:175
  88.0 2.6 collective-permute-start.4
  90.6 3.0 %collective-permute-start = (s32[2]{0:T(128)}, s32[2]{0:T(128)}, u32[]{:S(2)}, u32[]{:S(2)}) collective-permute-start(s32[2]{0:T(128)} %get-tuple-element.65), channel_id=1, source_target_pairs={{0,8},{8,16},{16,24},{24,32},{32,40},{40,48},{48,56},{56,64},{64,7... | collective-permute-start | bytes 32 | tf_op jit(solution)/shard_map/ppermute | solution.py:22
  97.3 3.0 %collective-permute-start.3 = (bf16[2,512]{0,1:T(8,128)(2,1)}, bf16[2,512]{0,1:T(8,128)(2,1)S(1)}, u32[]{:S(2)}, u32[]{:S(2)}) collective-permute-start(bf16[2,512]{0,1:T(8,128)(2,1)} %copy.48), channel_id=1, source_target_pairs={{0,8},{8,16},{16,24},{24,32},{32,40},{40,48},{48,56},{56,64},{64,7... | collective-permute-start | bytes 6152 | tf_op jit(solution)/shard_map/ppermute | solution.py:22
  115.0 3.3 %select_select_fusion = (bf16[256,512]{0,1:T(8,128)(2,1)}, bf16[256,512]{0,1:T(8,128)(2,1)}) fusion(pred[256]{0:T(512)(128)(4,1)} %get-tuple-element.53, pred[]{:T(512)S(6)} %eq.75, bf16[256,512]{0,1:T(8,128)(2,1)} %copy.47, bf16[2,512]{0,1:T(8,128)(2,1)S(1)} %collective-permute-done.3, f32[512]{0:T(512)} %bitcast.182, f32[512]{0:T(512)} %bitcast.184, ...), kind=kLoop, calls=%fused_computation.87 | loop fusion | flops 4718592 | bytes 1065729 | tf_op jit(solution)/shard_map/jit(_where)/select_n | solution.py:152
  118.3 2.7 %collective-permute-start.5 = (bf16[256,512]{0,1:T(8,128)(2,1)}, bf16[256,512]{0,1:T(8,128)(2,1)}, u32[]{:S(2)}, u32[]{:S(2)}) collective-permute-start(bf16[256,512]{0,1:T(8,128)(2,1)} %get-tuple-element.24), channel_id=1, source_target_pairs={{0,8},{8,16},{16,24},{24,32},{32,40},{40,48},{48,56},{56,64},{64,7... | collective-permute-start | bytes 786440 | tf_op jit(solution)/shard_map/ppermute | solution.py:22
  127.0 3.0 %reshape.187 = bf16[4,256,511]{2,1,0:T(8,128)(2,1)S(1)} reshape(bf16[4,130816]{1,0:T(4,128)(2,1)} %slice.318) | data formatting | bytes 2093056 | tf_op jit(solution)/shard_map/reshape | solution.py:48
  133.8 4.1 %reshape.185 = bf16[4,256,511]{2,1,0:T(8,128)(2,1)} reshape(bf16[4,130816]{1,0:T(4,128)(2,1)} %slice.316) | data formatting | bytes 2093056 | tf_op jit(solution)/shard_map/reshape | solution.py:48
  141.3 4.0 %reshape.189 = bf16[4,256,511]{2,1,0:T(8,128)(2,1)} reshape(bf16[4,130816]{1,0:T(4,128)(2,1)} %slice.320) | data formatting | bytes 2093056 | tf_op jit(solution)/shard_map/reshape | solution.py:48
  148.7 4.1 %reshape.182 = bf16[4,256,511]{2,1,0:T(8,128)(2,1)} reshape(bf16[4,130816]{1,0:T(4,128)(2,1)} %slice.314) | data formatting | bytes 2093056 | tf_op jit(solution)/shard_map/reshape | solution.py:48
  155.2 2.5 collective-permute-start.6
  161.4 4.3 %collective-permute-start.7 = (bf16[256,512]{0,1:T(8,128)(2,1)S(1)}, bf16[256,512]{0,1:T(8,128)(2,1)S(1)}, u32[]{:S(2)}, u32[]{:S(2)}) collective-permute-start(bf16[256,512]{0,1:T(8,128)(2,1)S(1)} %broadcast_select_fusion.5), channel_id=1, source_target_pairs={{0,8},{8,16},{16,24},{24,32},{32,40},{40,48},{48,56},{56,64},{64,7... | collective-permute-start | bytes 786440 | tf_op jit(solution)/shard_map/ppermute | solution.py:22
  172.4 22.5 %all-to-all-done.1 = f32[8,2,4,64,256]{4,3,2,1,0:T(8,128)} async-done(((f32[8,2,4,64,256]{4,3,2,1,0:T(8,128)}), f32[8,2,4,64,256]{4,3,2,1,0:T(8,128)}, u32[]{:S(2)}, u32[]{:S(2)}) %all-to-all-start.1) | async-done | bytes 4194336 | tf_op jit(solution)/shard_map/all_to_all | solution.py:175
  196.4 6.5 %all-to-all-start.2 = ((bf16[8,256,512]{1,2,0:T(8,128)(2,1)}), bf16[8,256,512]{1,2,0:T(8,128)(2,1)}, u32[]{:S(2)}, u32[]{:S(2)}) async-start(bf16[8,256,512]{1,2,0:T(8,128)(2,1)} %broadcast_in_dim.200), calls=%async_computation.2 | async-start | bytes 4194304 | tf_op jit(solution)/shard_map/all_to_all | solution.py:178
  203.6 2.5 reduce_sum.9
  209.5 3.7 %collective-permute-start.10 = (bf16[257,512]{0,1:T(8,128)(2,1)}, bf16[257,512]{0,1:T(8,128)(2,1)S(1)}, u32[]{:S(2)}, u32[]{:S(2)}) collective-permute-start(bf16[257,512]{0,1:T(8,128)(2,1)} %concatenate.65), channel_id=1, source_target_pairs={{8,0},{16,8},{24,16},{32,24},{40,32},{48,40},{56,48},{64,56},{72,6... | collective-permute-start | bytes 789512 | tf_op jit(solution)/shard_map/ppermute | solution.py:22
  217.0 2.8 %collective-permute-done.10 = bf16[257,512]{0,1:T(8,128)(2,1)S(1)} collective-permute-done((bf16[257,512]{0,1:T(8,128)(2,1)}, bf16[257,512]{0,1:T(8,128)(2,1)S(1)}, u32[]{:S(2)}, u32[]{:S(2)}) %collective-permute-start.10) | collective-permute-done | bytes 263200 | tf_op jit(solution)/shard_map/ppermute | solution.py:22
  222.4 5.0 %collective-permute-done.11 = bf16[257,512]{0,1:T(8,128)(2,1)} collective-permute-done((bf16[257,512]{0,1:T(8,128)(2,1)}, bf16[257,512]{0,1:T(8,128)(2,1)}, u32[]{:S(2)}, u32[]{:S(2)}) %collective-permute-start.11) | collective-permute-done | bytes 263200 | tf_op jit(solution)/shard_map/ppermute | solution.py:22
  229.8 5.4 %collective-permute-done.12 = bf16[257,512]{0,1:T(8,128)(2,1)} collective-permute-done((bf16[257,512]{0,1:T(8,128)(2,1)}, bf16[257,512]{0,1:T(8,128)(2,1)}, u32[]{:S(2)}, u32[]{:S(2)}) %collective-permute-start.12) | collective-permute-done | bytes 263200 | tf_op jit(solution)/shard_map/ppermute | solution.py:22
  245.4 3.1 %collective-permute-start.14 = (bf16[2,512]{0,1:T(8,128)(2,1)S(1)}, bf16[2,512]{0,1:T(8,128)(2,1)S(1)}, u32[]{:S(2)}, u32[]{:S(2)}) collective-permute-start(bf16[2,512]{0,1:T(8,128)(2,1)S(1)} %slice.338), channel_id=1, source_target_pairs={{8,0},{16,8},{24,16},{32,24},{40,32},{48,40},{56,48},{64,56},{72,6... | collective-permute-start | bytes 6152 | tf_op jit(solution)/shard_map/ppermute | solution.py:22
  255.4 3.5 %collective-permute-done.13 = bf16[2,512]{0,1:T(8,128)(2,1)S(1)} collective-permute-done((bf16[2,512]{0,1:T(8,128)(2,1)S(1)}, bf16[2,512]{0,1:T(8,128)(2,1)S(1)}, u32[]{:S(2)}, u32[]{:S(2)}) %collective-permute-start.13) | collective-permute-done | bytes 2080 | tf_op jit(solution)/shard_map/ppermute | solution.py:22
  (190 shorter events, 86.5 us)
Async XLA Ops:
  0.6 69.0 %copy-start = (bf16[256,512]{1,0:T(8,128)(2,1)S(1)}, bf16[256,512]{1,0:T(8,128)(2,1)}, u32[]{:S(2)}) copy-start(bf16[256,512]{1,0:T(8,128)(2,1)} %param.17) | copy-start | bytes 786436
  63.4 9.9 %collective-permute-start.8 = (bf16[2048,512]{1,0:T(8,128)(2,1)S(1)}, bf16[2048,512]{1,0:T(8,128)(2,1)S(1)}, u32[]{:S(2)}, u32[]{:S(2)}) collective-permute-start(bf16[2048,512]{1,0:T(8,128)(2,1)S(1)} %bitcast.146), channel_id=1, source_target_pairs={{0,8},{8,0},{1,9},{9,1},{2,10},{10,2},{3,11},{11,3},{4,12},{12,4},... | collective-permute-start | bytes 6291464 | tf_op jit(solution)/shard_map/ppermute | solution.py:15
  77.5 16.1 %copy-start.18 = (bf16[256,512]{1,0:T(8,128)(2,1)S(1)}, bf16[256,512]{1,0:T(8,128)(2,1)}, u32[]{:S(2)}) copy-start(bf16[256,512]{1,0:T(8,128)(2,1)} %param.10) | copy-start | bytes 786436
  77.5 19.0 %copy-start.19 = (bf16[256,512]{1,0:T(8,128)(2,1)S(1)}, bf16[256,512]{1,0:T(8,128)(2,1)}, u32[]{:S(2)}) copy-start(bf16[256,512]{1,0:T(8,128)(2,1)} %param.11) | copy-start | bytes 786436
  77.5 28.7 %copy-start.28 = (bf16[4,768]{1,0:T(4,128)(2,1)S(1)}, bf16[4,768]{1,0:T(4,128)(2,1)}, u32[]{:S(2)}) copy-start(bf16[4,768]{1,0:T(4,128)(2,1)} %param.13) | copy-start | bytes 18436
  77.5 28.9 %copy-start.38 = (f32[3,3,512]{2,1,0:T(4,128)S(1)}, f32[3,3,512]{2,1,0:T(4,128)}, u32[]{:S(2)}) copy-start(f32[3,3,512]{2,1,0:T(4,128)} %param.12) | copy-start | bytes 55300
  77.5 117.4 %all-to-all-start.1 = ((f32[8,2,4,64,256]{4,3,2,1,0:T(8,128)}), f32[8,2,4,64,256]{4,3,2,1,0:T(8,128)}, u32[]{:S(2)}, u32[]{:S(2)}) async-start(f32[8,2,4,64,256]{4,3,2,1,0:T(8,128)} %copy.50), calls=%async_computation.1 | async-start | bytes 8388608 | tf_op jit(solution)/shard_map/all_to_all | solution.py:175
  88.0 22.3 %collective-permute-start.4 = (s32[2]{0:T(128)}, s32[2]{0:T(128)}, u32[]{:S(2)}, u32[]{:S(2)}) collective-permute-start(s32[2]{0:T(128)} %get-tuple-element.64), channel_id=1, source_target_pairs={{8,0},{16,8},{24,16},{32,24},{40,32},{48,40},{56,48},{64,56},{72,6... | collective-permute-start | bytes 32 | tf_op jit(solution)/shard_map/ppermute | solution.py:22
  90.6 20.5 %collective-permute-start = (s32[2]{0:T(128)}, s32[2]{0:T(128)}, u32[]{:S(2)}, u32[]{:S(2)}) collective-permute-start(s32[2]{0:T(128)} %get-tuple-element.65), channel_id=1, source_target_pairs={{0,8},{8,16},{16,24},{24,32},{32,40},{40,48},{48,56},{56,64},{64,7... | collective-permute-start | bytes 32 | tf_op jit(solution)/shard_map/ppermute | solution.py:22
  94.4 20.6 %collective-permute-start.2 = (bf16[2,512]{0,1:T(8,128)(2,1)}, bf16[2,512]{0,1:T(8,128)(2,1)}, u32[]{:S(2)}, u32[]{:S(2)}) collective-permute-start(bf16[2,512]{0,1:T(8,128)(2,1)} %copy.45), channel_id=1, source_target_pairs={{0,8},{8,16},{16,24},{24,32},{32,40},{40,48},{48,56},{56,64},{64,7... | collective-permute-start | bytes 6152 | tf_op jit(solution)/shard_map/ppermute | solution.py:22
  97.3 17.7 %collective-permute-start.3 = (bf16[2,512]{0,1:T(8,128)(2,1)}, bf16[2,512]{0,1:T(8,128)(2,1)S(1)}, u32[]{:S(2)}, u32[]{:S(2)}) collective-permute-start(bf16[2,512]{0,1:T(8,128)(2,1)} %copy.48), channel_id=1, source_target_pairs={{0,8},{8,16},{16,24},{24,32},{32,40},{40,48},{48,56},{56,64},{64,7... | collective-permute-start | bytes 6152 | tf_op jit(solution)/shard_map/ppermute | solution.py:22
  101.9 68.7 %collective-permute-start.1 = (bf16[2,512]{0,1:T(8,128)(2,1)}, bf16[2,512]{0,1:T(8,128)(2,1)}, u32[]{:S(2)}, u32[]{:S(2)}) collective-permute-start(bf16[2,512]{0,1:T(8,128)(2,1)} %copy.42), channel_id=1, source_target_pairs={{0,8},{8,16},{16,24},{24,32},{32,40},{40,48},{48,56},{56,64},{64,7... | collective-permute-start | bytes 6152 | tf_op jit(solution)/shard_map/ppermute | solution.py:22
  118.3 35.9 %collective-permute-start.5 = (bf16[256,512]{0,1:T(8,128)(2,1)}, bf16[256,512]{0,1:T(8,128)(2,1)}, u32[]{:S(2)}, u32[]{:S(2)}) collective-permute-start(bf16[256,512]{0,1:T(8,128)(2,1)} %get-tuple-element.24), channel_id=1, source_target_pairs={{0,8},{8,16},{16,24},{24,32},{32,40},{40,48},{48,56},{56,64},{64,7... | collective-permute-start | bytes 786440 | tf_op jit(solution)/shard_map/ppermute | solution.py:22
  130.0 36.3 %copy-start.3 = (bf16[4,256,511]{2,1,0:T(8,128)(2,1)}, bf16[4,256,511]{2,1,0:T(8,128)(2,1)S(1)}, u32[]{:S(2)}) copy-start(bf16[4,256,511]{2,1,0:T(8,128)(2,1)S(1)} %reshape.187) | copy-start | bytes 3139588
  155.2 14.5 %copy-start.6 = (bf16[4,256,511]{2,1,0:T(8,128)(2,1)S(1)}, bf16[4,256,511]{2,1,0:T(8,128)(2,1)}, u32[]{:S(2)}) copy-start(bf16[4,256,511]{2,1,0:T(8,128)(2,1)} %reshape.189) | copy-start | bytes 3139588
  155.2 6.1 %collective-permute-start.6 = (bf16[256,512]{0,1:T(8,128)(2,1)S(1)}, bf16[256,512]{0,1:T(8,128)(2,1)S(1)}, u32[]{:S(2)}, u32[]{:S(2)}) collective-permute-start(bf16[256,512]{0,1:T(8,128)(2,1)S(1)} %broadcast_select_fusion.6), channel_id=1, source_target_pairs={{0,8},{8,16},{16,24},{24,32},{32,40},{40,48},{48,56},{56,64},{64,7... | collective-permute-start | bytes 786440 | tf_op jit(solution)/shard_map/ppermute | solution.py:22
  161.4 7.6 %collective-permute-start.7 = (bf16[256,512]{0,1:T(8,128)(2,1)S(1)}, bf16[256,512]{0,1:T(8,128)(2,1)S(1)}, u32[]{:S(2)}, u32[]{:S(2)}) collective-permute-start(bf16[256,512]{0,1:T(8,128)(2,1)S(1)} %broadcast_select_fusion.5), channel_id=1, source_target_pairs={{0,8},{8,16},{16,24},{24,32},{32,40},{40,48},{48,56},{56,64},{64,7... | collective-permute-start | bytes 786440 | tf_op jit(solution)/shard_map/ppermute | solution.py:22
  196.4 66.6 %all-to-all-start.2 = ((bf16[8,256,512]{1,2,0:T(8,128)(2,1)}), bf16[8,256,512]{1,2,0:T(8,128)(2,1)}, u32[]{:S(2)}, u32[]{:S(2)}) async-start(bf16[8,256,512]{1,2,0:T(8,128)(2,1)} %broadcast_in_dim.200), calls=%async_computation.2 | async-start | bytes 4194304 | tf_op jit(solution)/shard_map/all_to_all | solution.py:178
  209.5 10.3 %collective-permute-start.10 = (bf16[257,512]{0,1:T(8,128)(2,1)}, bf16[257,512]{0,1:T(8,128)(2,1)S(1)}, u32[]{:S(2)}, u32[]{:S(2)}) collective-permute-start(bf16[257,512]{0,1:T(8,128)(2,1)} %concatenate.65), channel_id=1, source_target_pairs={{8,0},{16,8},{24,16},{32,24},{40,32},{48,40},{56,48},{64,56},{72,6... | collective-permute-start | bytes 789512 | tf_op jit(solution)/shard_map/ppermute | solution.py:22
  213.2 14.1 %collective-permute-start.11 = (bf16[257,512]{0,1:T(8,128)(2,1)}, bf16[257,512]{0,1:T(8,128)(2,1)}, u32[]{:S(2)}, u32[]{:S(2)}) collective-permute-start(bf16[257,512]{0,1:T(8,128)(2,1)} %concatenate.65), channel_id=1, source_target_pairs={{16,0},{24,8},{32,16},{40,24},{48,32},{56,40},{64,48},{72,56},{80,... | collective-permute-start | bytes 789512 | tf_op jit(solution)/shard_map/ppermute | solution.py:22
  214.5 20.7 %collective-permute-start.12 = (bf16[257,512]{0,1:T(8,128)(2,1)}, bf16[257,512]{0,1:T(8,128)(2,1)}, u32[]{:S(2)}, u32[]{:S(2)}) collective-permute-start(bf16[257,512]{0,1:T(8,128)(2,1)} %concatenate.65), channel_id=1, source_target_pairs={{24,0},{32,8},{40,16},{48,24},{56,32},{64,40},{72,48},{80,56},{88,... | collective-permute-start | bytes 789512 | tf_op jit(solution)/shard_map/ppermute | solution.py:22
  245.4 6.3 %collective-permute-start.14 = (bf16[2,512]{0,1:T(8,128)(2,1)S(1)}, bf16[2,512]{0,1:T(8,128)(2,1)S(1)}, u32[]{:S(2)}, u32[]{:S(2)}) collective-permute-start(bf16[2,512]{0,1:T(8,128)(2,1)S(1)} %slice.338), channel_id=1, source_target_pairs={{8,0},{16,8},{24,16},{32,24},{40,32},{48,40},{56,48},{64,56},{72,6... | collective-permute-start | bytes 6152 | tf_op jit(solution)/shard_map/ppermute | solution.py:22
  248.6 6.8 %collective-permute-start.9 = (bf16[2,512]{0,1:T(8,128)(2,1)S(1)}, bf16[2,512]{0,1:T(8,128)(2,1)S(1)}, u32[]{:S(2)}, u32[]{:S(2)}) collective-permute-start(bf16[2,512]{0,1:T(8,128)(2,1)S(1)} %slice.326), channel_id=1, source_target_pairs={{8,0},{16,8},{24,16},{32,24},{40,32},{48,40},{56,48},{64,56},{72,6... | collective-permute-start | bytes 6152 | tf_op jit(solution)/shard_map/ppermute | solution.py:22
  252.6 6.3 %collective-permute-start.13 = (bf16[2,512]{0,1:T(8,128)(2,1)S(1)}, bf16[2,512]{0,1:T(8,128)(2,1)S(1)}, u32[]{:S(2)}, u32[]{:S(2)}) collective-permute-start(bf16[2,512]{0,1:T(8,128)(2,1)S(1)} %slice.335), channel_id=1, source_target_pairs={{8,0},{16,8},{24,16},{32,24},{40,32},{48,40},{56,48},{64,56},{72,6... | collective-permute-start | bytes 6152 | tf_op jit(solution)/shard_map/ppermute | solution.py:22
  (39 other events, 219.8 us)

commit v10 on v8

--- a/solution.py
+++ b/solution.py
@@ -154,6 +154,8 @@
     weight_rows, weight_rows_other, core_index = gather_weight(out_weight, chip_count)
     ch_count = lax.axis_size(CH)
     on_first = core_index == 0
+    weight_first = jnp.where(on_first, weight_rows, weight_rows_other)
+    weight_second = jnp.where(on_first, weight_rows_other, weight_rows)
     dims = (((1,), (1,)), ((), ()))
     block_chips = chip_count // ch_count
     part_mine = lax.dot_general(
@@ -174,10 +176,8 @@
     )
     pre_first = full_pre[:, :, 0].reshape(row_count, -1)
     pre_second = full_pre[:, :, 1].reshape(row_count, -1)
-    pre_mine = jnp.where(on_first, pre_first, pre_second)
-    pre_other = jnp.where(on_first, pre_second, pre_first)
-    out_sum = jnp.dot(pre_mine, weight_rows, preferred_element_type=jnp.float32) + jnp.dot(
-        pre_other, weight_rows_other, preferred_element_type=jnp.float32
+    out_sum = jnp.dot(pre_first, weight_first, preferred_element_type=jnp.float32) + jnp.dot(
+        pre_second, weight_second, preferred_element_type=jnp.float32
     )
     summed = jnp.sum(received, axis=0)
     cols_mine, cols_other = summed[0][:, None], summed[1][:, None]

time: 280 us -> 263 us (0.939)
  starting transfers between devices: 79.9 us -> 58.5 us
  waiting for transfers between devices: 39.2 us -> 43.1 us
    ppermute x14, starting transfers between devices: 55.6 us -> 35.5 us  [shifted(): return lax.ppermute(array, axis, pairs)]
    ppermute x14, waiting for transfers between devices: 15.5 us -> 18.6 us  [shifted(): return lax.ppermute(array, axis, pairs)]
  transfers between devices with their start and end apart: 17 -> 17, of which waited for: 7 -> 8; matrix products, arithmetic and copies ran while one was open for 29% -> 30% of each run, Pallas kernels for 0% -> 0%
where the time goes in v10:
time: 263 us; the launch traced here: 261 us
  blocking collectives  61.7 us (23%)
  starting transfers between devices  58.5 us (22%)
  local copies, waits for them, and re-layouts  52.5 us (20%)
  waiting for transfers between devices  43.1 us (16%)
  other arithmetic  27 us (10%)
  matrix products  13.1 us (5%)
  between operations  5.42 us (2%)
    all_to_all x1, blocking collectives, gather_weight(): lax.all_to_all(spread, CHIPS, 0, 0, tiled=True)  61.7 us
    ppermute x14, starting transfers between devices, shifted(): return lax.ppermute(array, axis, pairs)  35.5 us
    all_to_all x1, waiting for transfers between devices, local(): received = lax.all_to_all(sent, CH, 0, 0, tiled=True)  21.4 us
    unnamed x98, local copies, waits for them, and re-layouts  19.3 us
    ppermute x14, waiting for transfers between devices, shifted(): return lax.ppermute(array, axis, pairs)  18.6 us
    reshape x4, local copies, waits for them, and re-layouts, toeplitz_tiles(): repeated.reshape(group_count, row_count, 2 * row_count - 1)  15.2 us
    all_to_all x1, starting transfers between devices, local(): received = lax.all_to_all(sent, CH, 0, 0, tiled=True)  9.91 us
    all_to_all x1, starting transfers between devices, local(): lax.all_to_all(spread, CH, 0, 0, tiled=True)  6.92 us
  transfers between devices with their start and end apart: 17, of which 8 were waited for; matrix products, arithmetic and copies ran while one was open for 30% of the time, Pallas kernels for 0%

profile of v10, /device:TPU:1, one launch (start us, length us, event | category | flops | bytes accessed | tf_op | source)
XLA Modules:
  0.0 261.3 jit_solution(2489854056292793177)
XLA Ops:
  1.8 61.7 %all_to_all.15 = bf16[32,64,512]{2,1,0:T(8,128)(2,1)S(1)} all-to-all(bf16[32,64,512]{2,1,0:T(8,128)(2,1)S(1)} %broadcast_in_dim.198), channel_id=1, replica_groups=mesh['zl'=4,'y'=8,'core'=2,'zh'=2,'x'=4] {'zl','y'}, dimensions={0} | all-to-all | bytes 4194304 | tf_op jit(solution)/shard_map/all_to_all | solution.py:14
  63.4 6.2 %collective-permute-start.8 = (bf16[2048,512]{1,0:T(8,128)(2,1)S(1)}, bf16[2048,512]{1,0:T(8,128)(2,1)S(1)}, u32[]{:S(2)}, u32[]{:S(2)}) collective-permute-start(bf16[2048,512]{1,0:T(8,128)(2,1)S(1)} %bitcast.142), channel_id=1, source_target_pairs={{0,8},{8,0},{1,9},{9,1},{2,10},{10,2},{3,11},{11,3},{4,12},{12,4},... | collective-permute-start | bytes 6291464 | tf_op jit(solution)/shard_map/ppermute | solution.py:15
  70.3 3.0 %collective-permute-done.8 = bf16[2048,512]{1,0:T(8,128)(2,1)S(1)} collective-permute-done((bf16[2048,512]{1,0:T(8,128)(2,1)S(1)}, bf16[2048,512]{1,0:T(8,128)(2,1)S(1)}, u32[]{:S(2)}, u32[]{:S(2)}) %collective-permute-start.8) | collective-permute-done | bytes 2097184 | tf_op jit(solution)/shard_map/ppermute | solution.py:15
  77.5 9.9 %all-to-all-start.1 = ((f32[8,2,4,64,256]{4,3,2,1,0:T(8,128)}), f32[8,2,4,64,256]{4,3,2,1,0:T(8,128)}, u32[]{:S(2)}, u32[]{:S(2)}) async-start(f32[8,2,4,64,256]{4,3,2,1,0:T(8,128)} %copy.50), calls=%async_computation.1 | async-start | bytes 8388608 | tf_op jit(solution)/shard_map/all_to_all | solution.py:168
  88.1 2.6 collective-permute-start.4
  90.6 3.0 %collective-permute-start = (s32[2]{0:T(128)}, s32[2]{0:T(128)}, u32[]{:S(2)}, u32[]{:S(2)}) collective-permute-start(s32[2]{0:T(128)} %get-tuple-element.65), channel_id=1, source_target_pairs={{0,8},{8,16},{16,24},{24,32},{32,40},{40,48},{48,56},{56,64},{64,7... | collective-permute-start | bytes 32 | tf_op jit(solution)/shard_map/ppermute | solution.py:22
  98.1 3.0 %collective-permute-start.2 = (bf16[2,512]{0,1:T(8,128)(2,1)}, bf16[2,512]{0,1:T(8,128)(2,1)}, u32[]{:S(2)}, u32[]{:S(2)}) collective-permute-start(bf16[2,512]{0,1:T(8,128)(2,1)} %copy.45), channel_id=1, source_target_pairs={{0,8},{8,16},{16,24},{24,32},{32,40},{40,48},{48,56},{56,64},{64,7... | collective-permute-start | bytes 6152 | tf_op jit(solution)/shard_map/ppermute | solution.py:22
  115.2 3.3 %select_select_fusion.1 = (bf16[256,512]{0,1:T(8,128)(2,1)}, bf16[256,512]{0,1:T(8,128)(2,1)}) fusion(pred[256]{0:T(512)(128)(4,1)} %get-tuple-element.53, pred[]{:T(512)S(6)} %eq.68, bf16[256,512]{0,1:T(8,128)(2,1)} %copy.47, bf16[2,512]{0,1:T(8,128)(2,1)S(1)} %collective-permute-done.3, f32[512]{0:T(512)} %bitcast.179, f32[512]{0:T(512)} %bitcast.181, ...), kind=kLoop, calls=%fused_computation.98 | loop fusion | flops 4718592 | bytes 1065729 | tf_op jit(solution)/shard_map/jit(_where)/select_n | solution.py:143
  118.5 2.7 %collective-permute-start.5 = (bf16[256,512]{0,1:T(8,128)(2,1)}, bf16[256,512]{0,1:T(8,128)(2,1)}, u32[]{:S(2)}, u32[]{:S(2)}) collective-permute-start(bf16[256,512]{0,1:T(8,128)(2,1)} %get-tuple-element.24), channel_id=1, source_target_pairs={{0,8},{8,16},{16,24},{24,32},{32,40},{40,48},{48,56},{56,64},{64,7... | collective-permute-start | bytes 786440 | tf_op jit(solution)/shard_map/ppermute | solution.py:22
  128.4 4.0 %reshape.167 = bf16[4,256,511]{2,1,0:T(8,128)(2,1)} reshape(bf16[4,130816]{1,0:T(4,128)(2,1)} %slice.294) | data formatting | bytes 2093056 | tf_op jit(solution)/shard_map/reshape | solution.py:48
  134.5 3.0 %reshape.172 = bf16[4,256,511]{2,1,0:T(8,128)(2,1)S(1)} reshape(bf16[4,130816]{1,0:T(4,128)(2,1)} %slice.298) | data formatting | bytes 2093056 | tf_op jit(solution)/shard_map/reshape | solution.py:48
  141.4 4.1 %reshape.170 = bf16[4,256,511]{2,1,0:T(8,128)(2,1)} reshape(bf16[4,130816]{1,0:T(4,128)(2,1)} %slice.296) | data formatting | bytes 2093056 | tf_op jit(solution)/shard_map/reshape | solution.py:48
  148.9 4.0 %reshape.174 = bf16[4,256,511]{2,1,0:T(8,128)(2,1)} reshape(bf16[4,130816]{1,0:T(4,128)(2,1)} %slice.300) | data formatting | bytes 2093056 | tf_op jit(solution)/shard_map/reshape | solution.py:48
  155.3 2.5 collective-permute-start.6
  161.5 4.3 %collective-permute-start.7 = (bf16[256,512]{0,1:T(8,128)(2,1)S(1)}, bf16[256,512]{0,1:T(8,128)(2,1)S(1)}, u32[]{:S(2)}, u32[]{:S(2)}) collective-permute-start(bf16[256,512]{0,1:T(8,128)(2,1)S(1)} %broadcast_select_fusion.8), channel_id=1, source_target_pairs={{0,8},{8,16},{16,24},{24,32},{32,40},{40,48},{48,56},{56,64},{64,7... | collective-permute-start | bytes 786440 | tf_op jit(solution)/shard_map/ppermute | solution.py:22
  170.8 2.5 multiply_convert_fusion.2
  173.2 21.4 %all-to-all-done.1 = f32[8,2,4,64,256]{4,3,2,1,0:T(8,128)} async-done(((f32[8,2,4,64,256]{4,3,2,1,0:T(8,128)}), f32[8,2,4,64,256]{4,3,2,1,0:T(8,128)}, u32[]{:S(2)}, u32[]{:S(2)}) %all-to-all-start.1) | async-done | bytes 4194336 | tf_op jit(solution)/shard_map/all_to_all | solution.py:168
  196.1 6.9 %all-to-all-start.2 = ((bf16[8,256,512]{1,2,0:T(8,128)(2,1)}), bf16[8,256,512]{1,2,0:T(8,128)(2,1)}, u32[]{:S(2)}, u32[]{:S(2)}) async-start(bf16[8,256,512]{1,2,0:T(8,128)(2,1)} %broadcast_in_dim.199), calls=%async_computation.2 | async-start | bytes 4194304 | tf_op jit(solution)/shard_map/all_to_all | solution.py:171
  204.9 2.5 reduce_sum.9
  210.6 3.7 %collective-permute-start.10 = (bf16[256,512]{0,1:T(8,128)(2,1)}, bf16[256,512]{0,1:T(8,128)(2,1)S(1)}, u32[]{:S(2)}, u32[]{:S(2)}) collective-permute-start(bf16[256,512]{0,1:T(8,128)(2,1)} %get-tuple-element.20), channel_id=1, source_target_pairs={{8,0},{16,8},{24,16},{32,24},{40,32},{48,40},{56,48},{64,56},{72,6... | collective-permute-start | bytes 786440 | tf_op jit(solution)/shard_map/ppermute | solution.py:22
  215.9 2.6 collective-permute-done.10
  222.4 4.4 %collective-permute-done.11 = bf16[256,512]{0,1:T(8,128)(2,1)S(1)} collective-permute-done((bf16[256,512]{0,1:T(8,128)(2,1)S(1)}, bf16[256,512]{0,1:T(8,128)(2,1)S(1)}, u32[]{:S(2)}, u32[]{:S(2)}) %collective-permute-start.11) | collective-permute-done | bytes 262176 | tf_op jit(solution)/shard_map/ppermute | solution.py:22
  230.4 4.5 %collective-permute-done.12 = bf16[256,512]{0,1:T(8,128)(2,1)S(1)} collective-permute-done((bf16[256,512]{0,1:T(8,128)(2,1)S(1)}, bf16[256,512]{0,1:T(8,128)(2,1)S(1)}, u32[]{:S(2)}, u32[]{:S(2)}) %collective-permute-start.12) | collective-permute-done | bytes 262176 | tf_op jit(solution)/shard_map/ppermute | solution.py:22
  249.8 3.1 %collective-permute-done.13 = bf16[2,512]{0,1:T(8,128)(2,1)S(1)} collective-permute-done((bf16[2,512]{0,1:T(8,128)(2,1)}, bf16[2,512]{0,1:T(8,128)(2,1)S(1)}, u32[]{:S(2)}, u32[]{:S(2)}) %collective-permute-start.13) | collective-permute-done | bytes 2080 | tf_op jit(solution)/shard_map/ppermute | solution.py:22
  (180 shorter events, 86.9 us)
Async XLA Ops:
  0.6 69.0 %copy-start = (bf16[256,512]{1,0:T(8,128)(2,1)S(1)}, bf16[256,512]{1,0:T(8,128)(2,1)}, u32[]{:S(2)}) copy-start(bf16[256,512]{1,0:T(8,128)(2,1)} %param.17) | copy-start | bytes 786436
  63.4 9.9 %collective-permute-start.8 = (bf16[2048,512]{1,0:T(8,128)(2,1)S(1)}, bf16[2048,512]{1,0:T(8,128)(2,1)S(1)}, u32[]{:S(2)}, u32[]{:S(2)}) collective-permute-start(bf16[2048,512]{1,0:T(8,128)(2,1)S(1)} %bitcast.142), channel_id=1, source_target_pairs={{0,8},{8,0},{1,9},{9,1},{2,10},{10,2},{3,11},{11,3},{4,12},{12,4},... | collective-permute-start | bytes 6291464 | tf_op jit(solution)/shard_map/ppermute | solution.py:15
  77.5 19.8 %copy-start.15 = (bf16[256,512]{1,0:T(8,128)(2,1)S(1)}, bf16[256,512]{1,0:T(8,128)(2,1)}, u32[]{:S(2)}) copy-start(bf16[256,512]{1,0:T(8,128)(2,1)} %param.10) | copy-start | bytes 786436
  77.5 23.6 %copy-start.16 = (bf16[256,512]{1,0:T(8,128)(2,1)S(1)}, bf16[256,512]{1,0:T(8,128)(2,1)}, u32[]{:S(2)}) copy-start(bf16[256,512]{1,0:T(8,128)(2,1)} %param.11) | copy-start | bytes 786436
  77.5 28.8 %copy-start.22 = (bf16[4,768]{1,0:T(4,128)(2,1)S(1)}, bf16[4,768]{1,0:T(4,128)(2,1)}, u32[]{:S(2)}) copy-start(bf16[4,768]{1,0:T(4,128)(2,1)} %param.13) | copy-start | bytes 18436
  77.5 29.0 %copy-start.31 = (f32[3,3,512]{2,1,0:T(4,128)S(1)}, f32[3,3,512]{2,1,0:T(4,128)}, u32[]{:S(2)}) copy-start(f32[3,3,512]{2,1,0:T(4,128)} %param.12) | copy-start | bytes 55300
  77.5 117.1 %all-to-all-start.1 = ((f32[8,2,4,64,256]{4,3,2,1,0:T(8,128)}), f32[8,2,4,64,256]{4,3,2,1,0:T(8,128)}, u32[]{:S(2)}, u32[]{:S(2)}) async-start(f32[8,2,4,64,256]{4,3,2,1,0:T(8,128)} %copy.50), calls=%async_computation.1 | async-start | bytes 8388608 | tf_op jit(solution)/shard_map/all_to_all | solution.py:168
  88.1 22.3 %collective-permute-start.4 = (s32[2]{0:T(128)}, s32[2]{0:T(128)}, u32[]{:S(2)}, u32[]{:S(2)}) collective-permute-start(s32[2]{0:T(128)} %get-tuple-element.64), channel_id=1, source_target_pairs={{8,0},{16,8},{24,16},{32,24},{40,32},{48,40},{56,48},{64,56},{72,6... | collective-permute-start | bytes 32 | tf_op jit(solution)/shard_map/ppermute | solution.py:22
  90.6 20.4 %collective-permute-start = (s32[2]{0:T(128)}, s32[2]{0:T(128)}, u32[]{:S(2)}, u32[]{:S(2)}) collective-permute-start(s32[2]{0:T(128)} %get-tuple-element.65), channel_id=1, source_target_pairs={{0,8},{8,16},{16,24},{24,32},{32,40},{40,48},{48,56},{56,64},{64,7... | collective-permute-start | bytes 32 | tf_op jit(solution)/shard_map/ppermute | solution.py:22
  95.2 75.5 %collective-permute-start.1 = (bf16[2,512]{0,1:T(8,128)(2,1)}, bf16[2,512]{0,1:T(8,128)(2,1)}, u32[]{:S(2)}, u32[]{:S(2)}) collective-permute-start(bf16[2,512]{0,1:T(8,128)(2,1)} %copy.42), channel_id=1, source_target_pairs={{0,8},{8,16},{16,24},{24,32},{32,40},{40,48},{48,56},{56,64},{64,7... | collective-permute-start | bytes 6152 | tf_op jit(solution)/shard_map/ppermute | solution.py:22
  98.1 17.1 %collective-permute-start.2 = (bf16[2,512]{0,1:T(8,128)(2,1)}, bf16[2,512]{0,1:T(8,128)(2,1)}, u32[]{:S(2)}, u32[]{:S(2)}) collective-permute-start(bf16[2,512]{0,1:T(8,128)(2,1)} %copy.45), channel_id=1, source_target_pairs={{0,8},{8,16},{16,24},{24,32},{32,40},{40,48},{48,56},{56,64},{64,7... | collective-permute-start | bytes 6152 | tf_op jit(solution)/shard_map/ppermute | solution.py:22
  101.9 13.2 %collective-permute-start.3 = (bf16[2,512]{0,1:T(8,128)(2,1)}, bf16[2,512]{0,1:T(8,128)(2,1)S(1)}, u32[]{:S(2)}, u32[]{:S(2)}) collective-permute-start(bf16[2,512]{0,1:T(8,128)(2,1)} %copy.48), channel_id=1, source_target_pairs={{0,8},{8,16},{16,24},{24,32},{32,40},{40,48},{48,56},{56,64},{64,7... | collective-permute-start | bytes 6152 | tf_op jit(solution)/shard_map/ppermute | solution.py:22
  118.5 35.9 %collective-permute-start.5 = (bf16[256,512]{0,1:T(8,128)(2,1)}, bf16[256,512]{0,1:T(8,128)(2,1)}, u32[]{:S(2)}, u32[]{:S(2)}) collective-permute-start(bf16[256,512]{0,1:T(8,128)(2,1)} %get-tuple-element.24), channel_id=1, source_target_pairs={{0,8},{8,16},{16,24},{24,32},{32,40},{40,48},{48,56},{56,64},{64,7... | collective-permute-start | bytes 786440 | tf_op jit(solution)/shard_map/ppermute | solution.py:22
  137.6 28.9 %copy-start.3 = (bf16[4,256,511]{2,1,0:T(8,128)(2,1)}, bf16[4,256,511]{2,1,0:T(8,128)(2,1)S(1)}, u32[]{:S(2)}) copy-start(bf16[4,256,511]{2,1,0:T(8,128)(2,1)S(1)} %reshape.172) | copy-start | bytes 3139588
  155.3 6.1 %collective-permute-start.6 = (bf16[256,512]{0,1:T(8,128)(2,1)S(1)}, bf16[256,512]{0,1:T(8,128)(2,1)S(1)}, u32[]{:S(2)}, u32[]{:S(2)}) collective-permute-start(bf16[256,512]{0,1:T(8,128)(2,1)S(1)} %broadcast_select_fusion.9), channel_id=1, source_target_pairs={{0,8},{8,16},{16,24},{24,32},{32,40},{40,48},{48,56},{56,64},{64,7... | collective-permute-start | bytes 786440 | tf_op jit(solution)/shard_map/ppermute | solution.py:22
  161.5 7.6 %collective-permute-start.7 = (bf16[256,512]{0,1:T(8,128)(2,1)S(1)}, bf16[256,512]{0,1:T(8,128)(2,1)S(1)}, u32[]{:S(2)}, u32[]{:S(2)}) collective-permute-start(bf16[256,512]{0,1:T(8,128)(2,1)S(1)} %broadcast_select_fusion.8), channel_id=1, source_target_pairs={{0,8},{8,16},{16,24},{24,32},{32,40},{40,48},{48,56},{56,64},{64,7... | collective-permute-start | bytes 786440 | tf_op jit(solution)/shard_map/ppermute | solution.py:22
  196.1 60.6 %all-to-all-start.2 = ((bf16[8,256,512]{1,2,0:T(8,128)(2,1)}), bf16[8,256,512]{1,2,0:T(8,128)(2,1)}, u32[]{:S(2)}, u32[]{:S(2)}) async-start(bf16[8,256,512]{1,2,0:T(8,128)(2,1)} %broadcast_in_dim.199), calls=%async_computation.2 | async-start | bytes 4194304 | tf_op jit(solution)/shard_map/all_to_all | solution.py:171
  210.6 7.9 %collective-permute-start.10 = (bf16[256,512]{0,1:T(8,128)(2,1)}, bf16[256,512]{0,1:T(8,128)(2,1)S(1)}, u32[]{:S(2)}, u32[]{:S(2)}) collective-permute-start(bf16[256,512]{0,1:T(8,128)(2,1)} %get-tuple-element.20), channel_id=1, source_target_pairs={{8,0},{16,8},{24,16},{32,24},{40,32},{48,40},{56,48},{64,56},{72,6... | collective-permute-start | bytes 786440 | tf_op jit(solution)/shard_map/ppermute | solution.py:22
  218.6 17.1 %copy-start.6 = (bf16[4,256,511]{2,1,0:T(8,128)(2,1)S(1)}, bf16[4,256,511]{2,1,0:T(8,128)(2,1)}, u32[]{:S(2)}) copy-start(bf16[4,256,511]{2,1,0:T(8,128)(2,1)} %reshape.174) | copy-start | bytes 3139588
  218.6 8.2 %collective-permute-start.11 = (bf16[256,512]{0,1:T(8,128)(2,1)S(1)}, bf16[256,512]{0,1:T(8,128)(2,1)S(1)}, u32[]{:S(2)}, u32[]{:S(2)}) collective-permute-start(bf16[256,512]{0,1:T(8,128)(2,1)S(1)} %broadcast_select_fusion.7), channel_id=1, source_target_pairs={{8,0},{16,8},{24,16},{32,24},{40,32},{48,40},{56,48},{64,56},{72,6... | collective-permute-start | bytes 786440 | tf_op jit(solution)/shard_map/ppermute | solution.py:22
  226.8 8.1 %collective-permute-start.12 = (bf16[256,512]{0,1:T(8,128)(2,1)S(1)}, bf16[256,512]{0,1:T(8,128)(2,1)S(1)}, u32[]{:S(2)}, u32[]{:S(2)}) collective-permute-start(bf16[256,512]{0,1:T(8,128)(2,1)S(1)} %broadcast_select_fusion.6), channel_id=1, source_target_pairs={{8,0},{16,8},{24,16},{32,24},{40,32},{48,40},{56,48},{64,56},{72,6... | collective-permute-start | bytes 786440 | tf_op jit(solution)/shard_map/ppermute | solution.py:22
  238.5 6.3 %collective-permute-start.14 = (bf16[2,512]{0,1:T(8,128)(2,1)S(1)}, bf16[2,512]{0,1:T(8,128)(2,1)S(1)}, u32[]{:S(2)}, u32[]{:S(2)}) collective-permute-start(bf16[2,512]{0,1:T(8,128)(2,1)S(1)} %slice.312), channel_id=1, source_target_pairs={{8,0},{16,8},{24,16},{32,24},{40,32},{48,40},{56,48},{64,56},{72,6... | collective-permute-start | bytes 6152 | tf_op jit(solution)/shard_map/ppermute | solution.py:22
  240.5 8.6 %collective-permute-start.9 = (bf16[2,512]{0,1:T(8,128)(2,1)S(1)}, bf16[2,512]{0,1:T(8,128)(2,1)S(1)}, u32[]{:S(2)}, u32[]{:S(2)}) collective-permute-start(bf16[2,512]{0,1:T(8,128)(2,1)S(1)} %slice.306), channel_id=1, source_target_pairs={{8,0},{16,8},{24,16},{32,24},{40,32},{48,40},{56,48},{64,56},{72,6... | collective-permute-start | bytes 6152 | tf_op jit(solution)/shard_map/ppermute | solution.py:22
  246.4 6.5 %collective-permute-start.13 = (bf16[2,512]{0,1:T(8,128)(2,1)}, bf16[2,512]{0,1:T(8,128)(2,1)S(1)}, u32[]{:S(2)}, u32[]{:S(2)}) collective-permute-start(bf16[2,512]{0,1:T(8,128)(2,1)} %slice.309), channel_id=1, source_target_pairs={{8,0},{16,8},{24,16},{32,24},{40,32},{48,40},{56,48},{64,56},{72,6... | collective-permute-start | bytes 6152 | tf_op jit(solution)/shard_map/ppermute | solution.py:22
  (35 other events, 294.5 us)
